TPU v7x, 256 devices: a whole 4x4x8 slice. The times are simulated.
256 devices in a mesh: section: 4 (over y), fsdp: 64 (over z, x, core).
Axes of the slice: x: 4, y: 4, z: 8, core: 2. Of those that a mesh axis runs over, the one named last changes fastest.
Arguments:
- acts: bfloat16 [4, 8192, 4096], P('section', 'fsdp'), may hold values from -6 to 6
- out_grad: bfloat16 [4, 8192, 1024], P('section', 'fsdp'), may hold values from -6 to 6
- norm_gain: float32 [4, 4096], P('section'), may hold values from 0.25 to 1.75
- tiles: bfloat16 [4, 512, 4096], P('section', 'fsdp'), may hold values from -0.25 to 0.25
- tile_cols: int32 [4, 64, 8], P('section'), may hold values from 0 to 15, as said below
- tile_count: int32 [4, 64], P('section'), may hold values from 3 to 8, as said below
- tile_store_slot: int32 [4, 512], P('section'), may hold values from 0 to 511, each once within a row
Outputs:
- handed: bfloat16 [4, 8192, 4096], P('section', 'fsdp')
- weight_grad: float32 [4, 512, 4096], P('section', 'fsdp')
Inputs may be any that keep to these rules, and one draw needn't show every extreme that they name: `tile_cols`: within a row panel the listed block columns are all different. `tile_count`: every section has a panel with exactly 8 and a panel with exactly 3 kept tiles. `tile_store_slot`: each section's row is a permutation of the slots.
All inputs are finite; a program needn't handle non-finite values.
Results may differ from a plain program's by a relative error of at most 0.0029.
Values may be sent and summed in bfloat16 or wider, within the bound.
No kernel may reach another device: no remote copies, remote signals or barrier semaphores. Data moves between devices by JAX's collectives and lax.ppermute only.
A program may use at most 128 MiB of HBM per device.

v0:
```python
import jax
import jax.numpy as jnp
from jax import lax
from jax.sharding import PartitionSpec as P

EPS = 1e-05


def shifted(value, axis, steps):
    count = lax.axis_size(axis)
    leading, last = (max(0, -steps), min(count, count - steps))
    return lax.ppermute(value, axis, [(source, source + steps) for source in range(leading, last)])


def local(acts, out_grad, norm_gain, tiles, tile_cols, tile_count, tile_store_slot):
    inputs_f = acts[0].astype(jnp.float32)
    key_grad = out_grad[0]
    gain_row = norm_gain[0]
    column_list = tile_cols[0]
    count_list = tile_count[0]
    slot_lookup = tile_store_slot[0]
    tok_rows, width = inputs_f.shape
    kv_width = key_grad.shape[1]
    panel_list, most_kept = column_list.shape
    blk = width // panel_list
    ncol = kv_width // blk
    store_slots = panel_list * most_kept
    area = blk * blk
    slot_dev = tiles.shape[1]
    grad_scale = (tok_rows * lax.axis_size("fsdp")) ** (-0.5)
    tile_positions = jnp.arange(store_slots, dtype=jnp.int32)
    inverse_order = jnp.zeros((store_slots,), jnp.int32).at[slot_lookup].set(tile_positions)
    kept_grid = jnp.arange(most_kept)[None, :] < count_list[:, None]
    mean_sq = jnp.mean(inputs_f * inputs_f, axis=1, keepdims=True)
    recip = lax.rsqrt(mean_sq + EPS)
    normed = (inputs_f * recip * gain_row[None, :]).astype(jnp.bfloat16)
    gathered = lax.all_gather(tiles[0], "fsdp", axis=0, tiled=True)
    placed = gathered[slot_lookup].reshape(panel_list, most_kept, blk, blk)
    grad_padded = jnp.concatenate(
        [key_grad.reshape(tok_rows, ncol, blk), jnp.zeros((tok_rows, 1, blk), key_grad.dtype)],
        axis=1,
    )
    safe_cols = jnp.where(kept_grid, column_list, ncol)
    selected = grad_padded[:, safe_cols]
    normed_grad = jnp.einsum(
        "tpkb,pkab->tpa", selected, placed, preferred_element_type=jnp.float32
    ).reshape(tok_rows, width)
    normed_blocks = normed.reshape(tok_rows, panel_list, blk)
    terms_pos = jnp.einsum(
        "tpa,tpkb->pkab", normed_blocks, selected, preferred_element_type=jnp.float32
    )
    terms_pos = (terms_pos * grad_scale).reshape(store_slots, area)
    scaled = gain_row[None, :] * normed_grad
    inner = jnp.sum(scaled * inputs_f, axis=1, keepdims=True) / width
    input_grad = (recip * scaled - inputs_f * recip**3 * inner).astype(jnp.bfloat16)
    weight_grad = lax.psum_scatter(
        terms_pos[inverse_order[jnp.arange(lax.axis_size("fsdp") * slot_dev, dtype=jnp.int32)]],
        "fsdp",
        scatter_dimension=0,
        tiled=True,
    )
    handed = shifted(input_grad, "section", -1)
    return (handed[None], weight_grad[None])


def solution(mesh):
    placed = (
        P("section", "fsdp", None),
        P("section", "fsdp", None),
        P("section", None),
        P("section", "fsdp", None),
        P("section", None, None),
        P("section", None),
        P("section", None),
    )
    return jax.shard_map(
        local,
        mesh=mesh,
        in_specs=placed,
        out_specs=(P("section", "fsdp", None), P("section", "fsdp", None)),
        check_vma=False,
    )
```

profile of v0, /device:TPU:8, one launch (start us, length us, event | category | flops | bytes accessed | tf_op | source)
XLA Modules:
  0.0 389.6 jit_solution(2442717008277282318)
XLA Ops:
  7.2 0.0 all-gather.3.cloned.1.call-start
  7.2 0.7 all-gather.3.cloned.1.call-update
  7.9 0.0 all-reduce.4.cloned.1.call-start
  7.9 1.1 copy.17
  9.1 0.7 compare_select_fusion.2
  9.8 0.1 copy.18
  9.9 0.1 reshape.162
  9.9 1.5 copy.20
  11.4 0.5 broadcast.150
  11.9 1.4 reduce.4
  13.4 0.1 mul.81
  13.5 13.3 %gather_fusion.1 = bf16[512,128,64]{1,2,0:T(8,128)(2,1)} fusion(bf16[128,17,64]{0,2,1:T(8,128)(2,1)S(1)} %concatenate.3, s32[1024]{0:T(1024)S(1)} %pad_clamp_fusion.2), kind=kCustom, calls=%fused_computation.1 | custom fusion | bytes 16779264 | tf_op jit(solution)/shard_map/gather | solution.py:44
  26.8 2.6 scatter_custom_fusion
  29.5 3.5 gather_fusion.2
  33.0 0.3 fusion.2
  33.3 59.3 %all-gather.3.cloned.1.call-done = bf16[1,512,4096]{2,1,0:T(8,128)(2,1)} async-done(((bf16[1,8,4096]{2,1,0:T(8,128)(2,1)}), bf16[1,512,4096]{2,1,0:T(8,128)(2,1)}) %all-gather.3.cloned.1.call-update) | async-done | bytes 4194320 | tf_op jit(solution)/shard_map/all_gather | solution.py:37
  92.7 11.3 %gather_fusion = bf16[512,4096]{1,0:T(8,128)(2,1)} fusion(bf16[512,4096]{1,0:T(8,128)(2,1)} %bitcast.57, s32[1024]{0:T(1024)S(1)} %pad_clamp_fusion.3), kind=kCustom, calls=%fused_computation | custom fusion | bytes 8390656 | tf_op jit(solution)/shard_map/gather | solution.py:38
  103.9 12.6 %reshape.147 = bf16[64,8,64,64]{3,2,1,0:T(8,128)(2,1)} reshape(bf16[512,4096]{1,0:T(8,128)(2,1)} %gather_fusion) | data formatting | bytes 8388608 | tf_op jit(solution)/shard_map/reshape | solution.py:38
  116.5 9.3 %fusion.1 = (f32[128]{0:T(128)S(1)}, f32[64,64,128,1]{2,1,3,0:T(8,128)}) fusion(f32[128,64,64]{0,2,1:T(8,128)S(1)} %bitcast.62, f32[64,64]{1,0:T(8,128)S(1)} %mul.81, bf16[64,8,64,64]{3,2,1,0:T(8,128)(2,1)} %reshape.147, bf16[128,64,8,64]{0,3,2,1:T(8,128)(2,1)} %bitcast.58), kind=kOutput, calls=%fused_computation.8 | convolution fusion | flops 538443648 | bytes 16794112 | tf_op jit(solution)/shard_map/tpkb,pkab->tpa/dot_general | solution.py:45
  125.8 7.0 %multiply_bitcast_fusion = f32[64,8,64,64]{2,3,1,0:T(8,128)} fusion(bf16[128,64,8,64]{0,3,2,1:T(8,128)(2,1)S(1)} %bitcast.61, f32[128,64,64]{0,2,1:T(8,128)S(1)} %bitcast.63, f32[128]{0:T(128)S(1)} %get-tuple-element.2, f32[64,64]{1,0:T(8,128)S(1)} %mul.81), kind=kOutput, calls=%fused_computation.5 | convolution fusion | flops 540540928 | bytes 18891264 | tf_op jit(solution)/shard_map/tpa,tpkb->pkab/dot_general | solution.py:49
  132.9 17.4 %copy.21 = f32[64,8,64,64]{3,2,1,0:T(8,128)} copy(f32[64,8,64,64]{2,3,1,0:T(8,128)} %multiply_bitcast_fusion) | data formatting | bytes 16777216 | tf_op jit(solution)/shard_map/mul | solution.py:52
  150.3 14.8 %reshape.149 = f32[512,4096]{1,0:T(8,128)} reshape(f32[64,8,64,64]{3,2,1,0:T(8,128)} %copy.21) | data formatting | bytes 16777216 | tf_op jit(solution)/shard_map/reshape | solution.py:52
  165.1 12.2 %gather_fusion.3 = f32[512,4096]{1,0:T(8,128)} fusion(f32[512,4096]{1,0:T(8,128)} %reshape.149, s32[1024]{0:T(1024)S(1)} %pad_clamp_fusion), kind=kCustom, calls=%fused_computation.3 | custom fusion | bytes 16779264 | tf_op jit(solution)/shard_map/gather | solution.py:57
  177.3 1.6 copy-done
  178.9 1.9 copy.19
  180.8 2.2 fusion.5
  183.0 2.4 collective-permute-start
  185.4 0.6 dynamic-slice
  186.7 23.5 %collective-permute-done = bf16[128,4096]{1,0:T(8,128)(2,1)S(1)} collective-permute-done((bf16[128,4096]{1,0:T(8,128)(2,1)S(1)}, bf16[128,4096]{1,0:T(8,128)(2,1)S(1)}, u32[]{:S(2)}, u32[]{:S(2)}) %collective-permute-start) | collective-permute-done | bytes 1048608 | tf_op jit(solution)/shard_map/ppermute | solution.py:12
  210.2 170.1 %all-reduce.4.cloned.1.call-done = f32[512,4096]{1,0:T(8,128)} async-done(((f32[512,4096]{1,0:T(8,128)}), f32[512,4096]{1,0:T(8,128)}) %all-reduce.4.cloned.1.call-update) | async-done | bytes 8388624
  380.3 1.6 dynamic-slice_bitcast_fusion
  381.8 1.0 copy.26
  (25 shorter events, 0.1 us)
Async XLA Ops:
  7.2 85.5 %all-gather.3.cloned.1.call-start = ((), (), s32[]{:S(2)}) async-start(), calls=%async_computation | async-start | bytes 4259840 | tf_op jit(solution)/shard_map/all_gather | solution.py:37
  7.9 372.4 %all-reduce.4.cloned.1.call-start = ((), (), s32[]{:S(2)}) async-start(), calls=%async_computation.1 | async-start | bytes 16777216
  13.5 13.4 %copy-start.3 = (s32[1,512]{1,0:T(1,128)S(1)}, s32[1,512]{1,0:T(1,128)}, u32[]{:S(2)}) copy-start(s32[1,512]{1,0:T(1,128)} %param.13) | copy-start | bytes 6148
  13.5 19.5 %copy-start.1 = (bf16[1,128,4096]{2,1,0:T(8,128)(2,1)S(1)}, bf16[1,128,4096]{2,1,0:T(8,128)(2,1)}, u32[]{:S(2)}) copy-start(bf16[1,128,4096]{2,1,0:T(8,128)(2,1)} %param.7) | copy-start | bytes 3145732
  116.5 9.3 %slice-start = ((s8[8388608]{0:T(1024)(128)(4,1)}), s8[4194304]{0:T(1024)(128)(4,1)S(1)}, s32[]{:S(2)}) async-start(s8[8388608]{0:T(1024)(128)(4,1)} %bitcast.59), calls=%async_computation.2 | async-start | bytes 8388608
  116.5 9.3 %slice-start.1 = ((s8[8388608]{0:T(1024)(128)(4,1)}), s8[4194304]{0:T(1024)(128)(4,1)S(1)}, s32[]{:S(2)}) async-start(s8[8388608]{0:T(1024)(128)(4,1)} %bitcast.59), calls=%async_computation.3 | async-start | bytes 8388608
  177.3 1.6 copy-start
  177.3 3.4 copy-start.2
  178.9 6.5 %copy-start.4 = (u32[256]{0:T(256)S(1)}, u32[256]{0:T(256)}, u32[]{:S(2)}) copy-start(u32[256]{0:T(256)} %constant.33) | copy-start | bytes 3076
  183.0 27.2 %collective-permute-start = (bf16[128,4096]{1,0:T(8,128)(2,1)S(1)}, bf16[128,4096]{1,0:T(8,128)(2,1)S(1)}, u32[]{:S(2)}, u32[]{:S(2)}) collective-permute-start(bf16[128,4096]{1,0:T(8,128)(2,1)S(1)} %fusion.5), channel_id=1, source_target_pairs={{64,0},{128,64},{192,128},{65,1},{129,65},{193,129},{66,2},{130,66... | collective-permute-start | bytes 3145736 | tf_op jit(solution)/shard_map/ppermute | solution.py:12
Sparse Core Ops, SparseCore 0:
  10.7 81.8 all-gather.2
  177.4 202.7 all-reduce.3
where the time goes:
time: 391 us; the launch traced here: 390 us
  waiting for transfers between devices  254 us (65%)
  local copies, waits for them, and re-layouts  97.7 us (25%)
  matrix products  16.3 us (4%)
  between operations  14.9 us (4%)
  other arithmetic  4.63 us (1%)
    unnamed x3, waiting for transfers between devices  171 us
    all_gather x1, waiting for transfers between devices, local(): gathered = lax.all_gather(tiles[0], 'fsdp', axis=0, tiled=True)  59.3 us
    ppermute x1, waiting for transfers between devices, shifted(): lax.ppermute(value, axis, [(source, source + steps) for source in range(l...  23.5 us
    mul x1, local copies, waits for them, and re-layouts, local(): terms_pos = (terms_pos * grad_scale).reshape(store_slots, area)  17.4 us
    reshape x1, local copies, waits for them, and re-layouts, local(): terms_pos = (terms_pos * grad_scale).reshape(store_slots, area)  14.8 us
    gather x1, local copies, waits for them, and re-layouts, local(): selected = grad_padded[:, safe_cols]  13.3 us
    reshape x1, local copies, waits for them, and re-layouts, local(): placed = gathered[slot_lookup].reshape(panel_list, most_kept, blk, blk)  12.6 us
    gather x1, local copies, waits for them, and re-layouts, local(): terms_pos[inverse_order[jnp.arange(lax.axis_size('fsdp') * slot_dev, dtyp...  12.2 us
  transfers between devices with their start and end apart: 3, of which 3 were waited for; matrix products, arithmetic and copies ran while one was open for 8% of the time, Pallas kernels for 0%

commit v1 on v0

--- a/solution.py
+++ b/solution.py
@@ -27,15 +27,22 @@
     store_slots = panel_list * most_kept
     area = blk * blk
     slot_dev = tiles.shape[1]
-    grad_scale = (tok_rows * lax.axis_size("fsdp")) ** (-0.5)
+    grad_scale = (tok_rows * lax.axis_size("zx") * lax.axis_size("core")) ** (-0.5)
     tile_positions = jnp.arange(store_slots, dtype=jnp.int32)
     inverse_order = jnp.zeros((store_slots,), jnp.int32).at[slot_lookup].set(tile_positions)
     kept_grid = jnp.arange(most_kept)[None, :] < count_list[:, None]
     mean_sq = jnp.mean(inputs_f * inputs_f, axis=1, keepdims=True)
     recip = lax.rsqrt(mean_sq + EPS)
     normed = (inputs_f * recip * gain_row[None, :]).astype(jnp.bfloat16)
-    gathered = lax.all_gather(tiles[0], "fsdp", axis=0, tiled=True)
-    placed = gathered[slot_lookup].reshape(panel_list, most_kept, blk, blk)
+    zx_size = lax.axis_size("zx")
+    core_size = lax.axis_size("core")
+    gathered = lax.all_gather(tiles[0], "zx", axis=0, tiled=True)
+    gathered = lax.all_gather(gathered, "core", axis=0, tiled=True)
+    slot_ids = jnp.arange(store_slots, dtype=jnp.int32)
+    slot_dev_i = slot_ids // (slot_dev * core_size)
+    slot_core = (slot_ids // slot_dev) % core_size
+    row_of_slot = slot_core * (zx_size * slot_dev) + slot_dev_i * slot_dev + slot_ids % slot_dev
+    placed = gathered[row_of_slot[slot_lookup]].reshape(panel_list, most_kept, blk, blk)
     grad_padded = jnp.concatenate(
         [key_grad.reshape(tok_rows, ncol, blk), jnp.zeros((tok_rows, 1, blk), key_grad.dtype)],
         axis=1,
@@ -53,22 +60,25 @@
     scaled = gain_row[None, :] * normed_grad
     inner = jnp.sum(scaled * inputs_f, axis=1, keepdims=True) / width
     input_grad = (recip * scaled - inputs_f * recip**3 * inner).astype(jnp.bfloat16)
-    weight_grad = lax.psum_scatter(
-        terms_pos[inverse_order[jnp.arange(lax.axis_size("fsdp") * slot_dev, dtype=jnp.int32)]],
-        "fsdp",
-        scatter_dimension=0,
-        tiled=True,
-    )
+    order_k = jnp.arange(core_size)[:, None, None]
+    order_i = jnp.arange(zx_size)[None, :, None]
+    order_j = jnp.arange(slot_dev)[None, None, :]
+    rs_order = ((order_i * core_size + order_k) * slot_dev + order_j).reshape(-1)
+    weight_grad = lax.psum_scatter(terms_pos[inverse_order[rs_order]], "core", scatter_dimension=0, tiled=True)
+    weight_grad = lax.psum_scatter(weight_grad, "zx", scatter_dimension=0, tiled=True)
     handed = shifted(input_grad, "section", -1)
     return (handed[None], weight_grad[None])
 
 
 def solution(mesh):
+    sec, fs = mesh.devices.shape
+    mesh = jax.sharding.Mesh(mesh.devices.reshape(sec, fs // 2, 2), ("section", "zx", "core"))
+    F = ("zx", "core")
     placed = (
-        P("section", "fsdp", None),
-        P("section", "fsdp", None),
+        P("section", F, None),
+        P("section", F, None),
         P("section", None),
-        P("section", "fsdp", None),
+        P("section", F, None),
         P("section", None, None),
         P("section", None),
         P("section", None),
@@ -77,6 +87,6 @@
         local,
         mesh=mesh,
         in_specs=placed,
-        out_specs=(P("section", "fsdp", None), P("section", "fsdp", None)),
+        out_specs=(P("section", F, None), P("section", F, None)),
         check_vma=False,
     )

time: 391 us -> 461 us (1.18)
  waiting for transfers between devices: 254 us -> 326 us
    reduce_scatter x0 -> x2, waiting for transfers between devices: none -> 217 us  [the longest x1 198 us: local(): lax.psum_scatter(weight_grad, 'zx', scatter_dimension=0, tiled=True)]
    unnamed x3 -> x4, waiting for transfers between devices: 171 us -> 0.73 us
    all_gather x1 -> x2, waiting for transfers between devices: 59.3 us -> 83.5 us  [the longest x1 83.4 us: local(): gathered = lax.all_gather(tiles[0], 'zx', axis=0, tiled=True)]
    gather x3 -> x4, local copies, waits for them, and re-layouts: 27 us -> 30.5 us  [the longest x1 12.2 us: local(): terms_pos[inverse_order[rs_order]]]
  transfers between devices with their start and end apart: 3 -> 5, of which waited for: 3 -> 4; matrix products, arithmetic and copies ran while one was open for 8% -> 7% of each run, Pallas kernels for 0% -> 0%
where the time goes in v1:
time: 461 us; the launch traced here: 460 us
  waiting for transfers between devices  326 us (71%)
  local copies, waits for them, and re-layouts  97.6 us (21%)
  matrix products  16.4 us (4%)
  between operations  14 us (3%)
    reduce_scatter x1, waiting for transfers between devices, local(): lax.psum_scatter(weight_grad, 'zx', scatter_dimension=0, tiled=True)  198 us
    all_gather x1, waiting for transfers between devices, local(): gathered = lax.all_gather(tiles[0], 'zx', axis=0, tiled=True)  83.4 us
    ppermute x1, waiting for transfers between devices, shifted(): lax.ppermute(value, axis, [(source, source + steps) for source in range(l...  24.4 us
    reduce_scatter x1, waiting for transfers between devices, local(): lax.psum_scatter(terms_pos[inverse_order[rs_order]], 'core', scatter_dime...  19.1 us
    mul x1, local copies, waits for them, and re-layouts, local(): terms_pos = (terms_pos * grad_scale).reshape(store_slots, area)  17.4 us
    reshape x1, local copies, waits for them, and re-layouts, local(): terms_pos = (terms_pos * grad_scale).reshape(store_slots, area)  14.8 us
    gather x1, local copies, waits for them, and re-layouts, local(): selected = grad_padded[:, safe_cols]  13.4 us
    reshape x1, local copies, waits for them, and re-layouts, local(): gathered[row_of_slot[slot_lookup]].reshape(panel_list, most_kept, blk, blk)  12.6 us
  transfers between devices with their start and end apart: 5, of which 4 were waited for; matrix products, arithmetic and copies ran while one was open for 7% of the time, Pallas kernels for 0%

profile of v1, /device:TPU:8, one launch (start us, length us, event | category | flops | bytes accessed | tf_op | source)
XLA Modules:
  0.0 460.4 jit_solution(11396080284697945354)
XLA Ops:
  7.2 0.7 all-gather.5.cloned.1.call-update
  8.0 83.4 %all-gather.5.cloned.1.call-done = bf16[1,256,4096]{2,1,0:T(8,128)(2,1)} async-done(((bf16[1,8,4096]{2,1,0:T(8,128)(2,1)}), bf16[1,256,4096]{2,1,0:T(8,128)(2,1)}) %all-gather.5.cloned.1.call-update) | async-done | bytes 2097168 | tf_op jit(solution)/shard_map/all_gather | solution.py:39
  91.5 1.1 copy.12
  92.6 0.7 compare_select_fusion.4
  93.3 0.1 copy.13
  93.4 0.1 reshape.243
  93.5 1.5 copy.15
  95.0 0.5 broadcast.221
  95.5 0.7 reduce.4
  96.2 0.1 mul.116
  96.2 0.1 iota_add_fusion
  96.3 0.1 add.150
  96.5 3.5 gather_fusion
  100.0 13.4 %gather_fusion.2 = bf16[512,128,64]{1,2,0:T(8,128)(2,1)} fusion(bf16[128,17,64]{0,2,1:T(8,128)(2,1)S(1)} %concatenate.3, s32[1024]{0:T(1024)S(1)} %pad_clamp_fusion.2), kind=kCustom, calls=%fused_computation.2 | custom fusion | bytes 16779264 | tf_op jit(solution)/shard_map/gather | solution.py:51
  113.4 2.6 scatter_custom_fusion
  116.1 3.5 gather_fusion.3
  119.6 0.3 fusion.2
  119.9 11.3 %gather_fusion.1 = bf16[512,4096]{1,0:T(8,128)(2,1)} fusion(bf16[512,4096]{1,0:T(8,128)(2,1)} %bitcast.58, s32[1024]{0:T(1024)S(1)} %pad_clamp_fusion.3), kind=kCustom, calls=%fused_computation.1 | custom fusion | bytes 8390656 | tf_op jit(solution)/shard_map/gather | solution.py:45
  131.2 12.6 %reshape.220 = bf16[64,8,64,64]{3,2,1,0:T(8,128)(2,1)} reshape(bf16[512,4096]{1,0:T(8,128)(2,1)} %gather_fusion.1) | data formatting | bytes 8388608 | tf_op jit(solution)/shard_map/reshape | solution.py:45
  143.8 9.3 %fusion.1 = (f32[128]{0:T(128)S(1)}, f32[64,64,128,1]{2,1,3,0:T(8,128)}) fusion(f32[128,64,64]{0,2,1:T(8,128)S(1)} %bitcast.63, f32[64,64]{1,0:T(8,128)S(1)} %mul.116, bf16[64,8,64,64]{3,2,1,0:T(8,128)(2,1)} %reshape.220, bf16[128,64,8,64]{0,3,2,1:T(8,128)(2,1)} %bitcast.59), kind=kOutput, calls=%fused_computation.9 | convolution fusion | flops 538443648 | bytes 16794112 | tf_op jit(solution)/shard_map/tpkb,pkab->tpa/dot_general | solution.py:52
  153.2 7.1 %multiply_bitcast_fusion = f32[64,8,64,64]{2,3,1,0:T(8,128)} fusion(bf16[128,64,8,64]{0,3,2,1:T(8,128)(2,1)S(1)} %bitcast.62, f32[128,64,64]{0,2,1:T(8,128)S(1)} %bitcast.64, f32[128]{0:T(128)S(1)} %get-tuple-element.2, f32[64,64]{1,0:T(8,128)S(1)} %mul.116), kind=kOutput, calls=%fused_computation.6 | convolution fusion | flops 540540928 | bytes 18891264 | tf_op jit(solution)/shard_map/tpa,tpkb->pkab/dot_general | solution.py:56
  160.2 17.4 %copy.16 = f32[64,8,64,64]{3,2,1,0:T(8,128)} copy(f32[64,8,64,64]{2,3,1,0:T(8,128)} %multiply_bitcast_fusion) | data formatting | bytes 16777216 | tf_op jit(solution)/shard_map/mul | solution.py:59
  177.7 14.8 %reshape.222 = f32[512,4096]{1,0:T(8,128)} reshape(f32[64,8,64,64]{3,2,1,0:T(8,128)} %copy.16) | data formatting | bytes 16777216 | tf_op jit(solution)/shard_map/reshape | solution.py:59
  192.4 12.2 %gather_fusion.4 = f32[512,4096]{1,0:T(8,128)} fusion(f32[512,4096]{1,0:T(8,128)} %reshape.222, s32[1024]{0:T(1024)S(1)} %pad_clamp_fusion), kind=kCustom, calls=%fused_computation.4 | custom fusion | bytes 16779264 | tf_op jit(solution)/shard_map/gather | solution.py:67
  204.7 0.0 reduce-scatter.5.cloned.1.call-start
  204.7 19.1 %reduce-scatter.3.cloned.1.call-done = f32[256,4096]{1,0:T(8,128)} async-done(((f32[512,4096]{1,0:T(8,128)}), f32[256,4096]{1,0:T(8,128)}) %reduce-scatter.3.cloned.1.call-update) | async-done | bytes 4194320 | tf_op jit(solution)/shard_map/reduce_scatter | solution.py:67
  223.9 1.9 copy.14
  225.8 2.2 fusion.5
  228.0 2.7 collective-permute-start
  230.7 24.4 %collective-permute-done = bf16[128,4096]{1,0:T(8,128)(2,1)S(1)} collective-permute-done((bf16[128,4096]{1,0:T(8,128)(2,1)S(1)}, bf16[128,4096]{1,0:T(8,128)(2,1)S(1)}, u32[]{:S(2)}, u32[]{:S(2)}) %collective-permute-start) | collective-permute-done | bytes 1048608 | tf_op jit(solution)/shard_map/ppermute | solution.py:12
  255.1 197.8 %reduce-scatter.5.cloned.1.call-done = f32[8,4096]{1,0:T(8,128)} async-done(((f32[256,4096]{1,0:T(8,128)}), f32[8,4096]{1,0:T(8,128)}) %reduce-scatter.5.cloned.1.call-update) | async-done | bytes 131088 | tf_op jit(solution)/shard_map/reduce_scatter | solution.py:68
  452.9 1.0 copy.20
  (35 shorter events, 0.3 us)
Async XLA Ops:
  7.2 88.3 %copy-start.2 = (f32[1,4096]{1,0:T(1,128)S(1)}, f32[1,4096]{1,0:T(1,128)}, u32[]{:S(2)}) copy-start(f32[1,4096]{1,0:T(1,128)} %param.9) | copy-start | bytes 49156
  7.2 89.3 %copy-start.3 = (s32[1,512]{1,0:T(1,128)S(1)}, s32[1,512]{1,0:T(1,128)}, u32[]{:S(2)}) copy-start(s32[1,512]{1,0:T(1,128)} %param.13) | copy-start | bytes 6148
  7.2 84.2 %all-gather.5.cloned.1.call-start = ((), (), s32[]{:S(2)}) async-start(), calls=%async_computation.4 | async-start | bytes 2162688 | tf_op jit(solution)/shard_map/all_gather | solution.py:39
  7.9 112.0 %all-gather.7.cloned.1.call-start = ((), (), s32[]{:S(2)}) async-start(), calls=%async_computation.5 | async-start | bytes 6291456 | tf_op jit(solution)/shard_map/all_gather | solution.py:40
  91.4 132.4 %reduce-scatter.3.cloned.1.call-start = ((), (), s32[]{:S(2)}) async-start(), calls=%async_computation.2 | async-start | bytes 12582912 | tf_op jit(solution)/shard_map/reduce_scatter | solution.py:67
  100.0 19.6 %copy-start.1 = (bf16[1,128,4096]{2,1,0:T(8,128)(2,1)S(1)}, bf16[1,128,4096]{2,1,0:T(8,128)(2,1)}, u32[]{:S(2)}) copy-start(bf16[1,128,4096]{2,1,0:T(8,128)(2,1)} %param.7) | copy-start | bytes 3145732
  143.8 9.3 %slice-start = ((s8[8388608]{0:T(1024)(128)(4,1)}), s8[4194304]{0:T(1024)(128)(4,1)S(1)}, s32[]{:S(2)}) async-start(s8[8388608]{0:T(1024)(128)(4,1)} %bitcast.60), calls=%async_computation.6 | async-start | bytes 8388608
  143.8 9.3 %slice-start.1 = ((s8[8388608]{0:T(1024)(128)(4,1)}), s8[4194304]{0:T(1024)(128)(4,1)S(1)}, s32[]{:S(2)}) async-start(s8[8388608]{0:T(1024)(128)(4,1)} %bitcast.60), calls=%async_computation.7 | async-start | bytes 8388608
  204.7 19.2 %copy-start = (f32[64,64,128,1]{2,1,3,0:T(8,128)S(1)}, f32[64,64,128,1]{2,1,3,0:T(8,128)}, u32[]{:S(2)}) copy-start(f32[64,64,128,1]{2,1,3,0:T(8,128)} %get-tuple-element.5) | copy-start | bytes 6291460
  204.7 248.2 %reduce-scatter.5.cloned.1.call-start = ((), (), s32[]{:S(2)}) async-start(), calls=%async_computation.3 | async-start | bytes 4325376 | tf_op jit(solution)/shard_map/reduce_scatter | solution.py:68
  228.0 27.1 %collective-permute-start = (bf16[128,4096]{1,0:T(8,128)(2,1)S(1)}, bf16[128,4096]{1,0:T(8,128)(2,1)S(1)}, u32[]{:S(2)}, u32[]{:S(2)}) collective-permute-start(bf16[128,4096]{1,0:T(8,128)(2,1)S(1)} %fusion.5), channel_id=1, source_target_pairs={{64,0},{128,64},{192,128},{65,1},{129,65},{193,129},{66,2},{130,66... | collective-permute-start | bytes 3145736 | tf_op jit(solution)/shard_map/ppermute | solution.py:12
Sparse Core Ops, SparseCore 0:
  10.6 80.7 all-gather.4
  93.2 16.2 all-gather.6
  204.8 18.9 reduce-scatter.2
  228.2 224.7 reduce-scatter.4

commit v2 on v0

v2 whole, which is shorter than its diff:
```python
import jax
import jax.numpy as jnp
from jax import lax
from jax.sharding import PartitionSpec as P

EPS = 1e-05
FS = ("z", "x", "core")


def shifted(value, axis, steps):
    count = lax.axis_size(axis)
    leading, last = (max(0, -steps), min(count, count - steps))
    return lax.ppermute(value, axis, [(source, source + steps) for source in range(leading, last)])


def local(acts, out_grad, norm_gain, tiles, tile_cols, tile_count, tile_store_slot):
    inputs_f = acts[0].astype(jnp.float32)
    key_grad = out_grad[0]
    gain_row = norm_gain[0]
    column_list = tile_cols[0]
    count_list = tile_count[0]
    slot_lookup = tile_store_slot[0]
    tok_rows, width = inputs_f.shape
    kv_width = key_grad.shape[1]
    panel_list, most_kept = column_list.shape
    blk = width // panel_list
    ncol = kv_width // blk
    store_slots = panel_list * most_kept
    slot_dev = tiles.shape[1]
    nz, nx, nc = (lax.axis_size(a) for a in FS)
    half = blk // 2
    lanes = 2 * blk
    grad_scale = (tok_rows * nz * nx * nc) ** (-0.5)

    own_tiles = tiles[0].reshape(slot_dev, half, lanes)
    gathered = lax.all_gather(own_tiles, "x", axis=0, tiled=True)
    gathered = lax.all_gather(gathered, "z", axis=0, tiled=True)
    gathered = lax.all_gather(gathered, "core", axis=0, tiled=True)
    slot_ids = jnp.arange(store_slots, dtype=jnp.int32)
    holder = slot_ids // slot_dev
    row_of_slot = (holder % nc) * (nz * nx * slot_dev) + (holder // nc) * slot_dev + slot_ids % slot_dev

    kept_grid = jnp.arange(most_kept)[None, :] < count_list[:, None]
    col_hit = (column_list[:, :, None] == jnp.arange(ncol)[None, None, :]) & kept_grid[:, :, None]
    has_tile = jnp.any(col_hit, axis=1)
    k_of = jnp.argmax(col_hit, axis=1)
    pos_of = jnp.arange(panel_list)[:, None] * most_kept + k_of
    dense_rows = jnp.where(has_tile, row_of_slot[slot_lookup[pos_of]], store_slots)

    mean_sq = jnp.mean(inputs_f * inputs_f, axis=1, keepdims=True)
    recip = lax.rsqrt(mean_sq + EPS)
    normed = (inputs_f * recip * gain_row[None, :]).astype(jnp.bfloat16)

    og_blocks = key_grad.reshape(tok_rows, ncol, blk).transpose(1, 0, 2)
    diag = (jnp.arange(2)[:, None] == jnp.arange(lanes)[None, :] // blk)
    og_wide = jnp.concatenate([og_blocks, og_blocks], axis=2)
    expand = jnp.where(diag[None, None, :, :], og_wide[:, :, None, :], jnp.zeros((), key_grad.dtype))

    normed_pairs = normed.reshape(tok_rows, panel_list, half, 2).transpose(1, 2, 3, 0)
    normed_pairs = normed_pairs.reshape(panel_list, half, 2 * tok_rows)
    expand_k = expand.transpose(0, 2, 1, 3).reshape(ncol, 2 * tok_rows, lanes)
    dense_terms = jnp.einsum("prk,ckl->pcrl", normed_pairs, expand_k, preferred_element_type=jnp.float32)
    dense_terms = dense_terms.reshape(panel_list * ncol, half, lanes)
    inverse_order = jnp.zeros((store_slots,), jnp.int32).at[slot_lookup].set(slot_ids)
    pos = inverse_order
    term_panel = pos // most_kept
    term_kept = (pos % most_kept) < count_list[term_panel]
    term_index = term_panel * ncol + column_list[term_panel, pos % most_kept]
    oc = jnp.arange(nc)[:, None, None, None]
    oz = jnp.arange(nz)[None, :, None, None]
    ox = jnp.arange(nx)[None, None, :, None]
    oj = jnp.arange(slot_dev)[None, None, None, :]
    rs_order = (((oz * nx + ox) * nc + oc) * slot_dev + oj).reshape(-1)
    terms = jnp.where(
        term_kept[rs_order][:, None, None], dense_terms[term_index[rs_order]], jnp.zeros((), jnp.float32)
    )
    weight_grad = lax.psum_scatter(terms, "core", scatter_dimension=0, tiled=True)
    weight_grad = lax.psum_scatter(weight_grad, "z", scatter_dimension=0, tiled=True)
    weight_grad = lax.psum_scatter(weight_grad, "x", scatter_dimension=0, tiled=True)
    weight_grad = (weight_grad * grad_scale).reshape(slot_dev, blk * blk)

    gathered_ext = jnp.concatenate([gathered, jnp.zeros((1, half, lanes), gathered.dtype)], axis=0)
    dense_w = gathered_ext[dense_rows.reshape(-1)].reshape(panel_list, ncol, half, lanes)
    normed_grad = jnp.einsum("cthl,pcrl->tprh", expand, dense_w, preferred_element_type=jnp.float32)
    normed_grad = normed_grad.reshape(tok_rows, width)

    scaled = gain_row[None, :] * normed_grad
    inner = jnp.sum(scaled * inputs_f, axis=1, keepdims=True) / width
    input_grad = (recip * scaled - inputs_f * recip**3 * inner).astype(jnp.bfloat16)
    handed = shifted(input_grad, "section", -1)
    return (handed[None], weight_grad[None])


def solution(mesh):
    sec, fs = mesh.devices.shape
    mesh = jax.sharding.Mesh(mesh.devices.reshape(sec, fs // 8, 4, 2), ("section",) + FS)
    placed = (
        P("section", FS, None),
        P("section", FS, None),
        P("section", None),
        P("section", FS, None),
        P("section", None, None),
        P("section", None),
        P("section", None),
    )
    return jax.shard_map(
        local,
        mesh=mesh,
        in_specs=placed,
        out_specs=(P("section", FS, None), P("section", FS, None)),
        check_vma=False,
    )
```

time: 391 us -> 305 us (0.78)
  waiting for transfers between devices: 254 us -> 124 us
  other arithmetic: 4.63 us -> 53.4 us
  blocking collectives: 0 us -> 13.3 us
  local copies, waits for them, and re-layouts: 97.7 us -> 88.7 us
  matrix products: 16.3 us -> 7.75 us
    unnamed x3 -> x5, waiting for transfers between devices: 171 us -> 0.08 us
    reduce_scatter x0 -> x3, waiting for transfers between devices: none -> 96.3 us  [the longest x1 52.1 us: local(): lax.psum_scatter(weight_grad, 'z', scatter_dimension=0, tiled=True)]
    lt x0 -> x2, other arithmetic: none -> 40.9 us  [the longest x1 40.2 us: local(): term_kept = pos % most_kept < count_list[term_panel]]
    all_gather x1 -> x2, waiting for transfers between devices: 59.3 us -> 27.2 us  [the longest x1 27.2 us: local(): gathered = lax.all_gather(gathered, 'z', axis=0, tiled=True)]
    reshape x3 -> x0, local copies, waits for them, and re-layouts: 29.2 us -> none  [the longest x1 14.8 us: local(): terms_pos = (terms_pos * grad_scale).reshape(store_slots, area)]
    ppermute x1, waiting for transfers between devices: 23.5 us -> 0.01 us  [shifted(): lax.ppermute(value, axis, [(source, source + steps) for source in range(l...]
    transpose x0 -> x2, local copies, waits for them, and re-layouts: none -> 21.2 us  [the longest x1 19.3 us: local(): jnp.einsum('prk,ckl->pcrl', normed_pairs, expand_k, preferred_element_typ...]
    mul x1 -> x0, local copies, waits for them, and re-layouts: 17.4 us -> none  [local(): terms_pos = (terms_pos * grad_scale).reshape(store_slots, area)]
  transfers between devices with their start and end apart: 3 -> 6, of which waited for: 3 -> 4; matrix products, arithmetic and copies ran while one was open for 8% -> 28% of each run, Pallas kernels for 0% -> 0%
where the time goes in v2:
time: 305 us; the launch traced here: 304 us
  waiting for transfers between devices  124 us (41%)
  local copies, waits for them, and re-layouts  88.7 us (29%)
  other arithmetic  53.4 us (18%)
  between operations  14.2 us (5%)
  blocking collectives  13.3 us (4%)
  matrix products  7.75 us (3%)
    reduce_scatter x1, waiting for transfers between devices, local(): lax.psum_scatter(weight_grad, 'z', scatter_dimension=0, tiled=True)  52.1 us
    lt x1, other arithmetic, local(): term_kept = pos % most_kept < count_list[term_panel]  40.2 us
    all_gather x1, waiting for transfers between devices, local(): gathered = lax.all_gather(gathered, 'z', axis=0, tiled=True)  27.2 us
    reduce_scatter x1, waiting for transfers between devices, local(): lax.psum_scatter(weight_grad, 'x', scatter_dimension=0, tiled=True)  23.9 us
    reduce_scatter x1, waiting for transfers between devices, local(): lax.psum_scatter(terms, 'core', scatter_dimension=0, tiled=True)  20.3 us
    transpose x1, local copies, waits for them, and re-layouts, local(): jnp.einsum('prk,ckl->pcrl', normed_pairs, expand_k, preferred_element_typ...  19.3 us
    all_gather x1, blocking collectives, local(): gathered = lax.all_gather(own_tiles, 'x', axis=0, tiled=True)  13.3 us
    gather x1, local copies, waits for them, and re-layouts, local(): gathered_ext[dense_rows.reshape(-1)].reshape(panel_list, ncol, half, lanes)  12.1 us
  transfers between devices with their start and end apart: 6, of which 4 were waited for; matrix products, arithmetic and copies ran while one was open for 28% of the time, Pallas kernels for 0%

profile of v2, /device:TPU:8, one launch (start us, length us, event | category | flops | bytes accessed | tf_op | source)
XLA Modules:
  0.0 303.9 jit_solution(1027258691933224277)
XLA Ops:
  7.2 0.9 copy.67
  8.1 13.3 %all_gather.9 = bf16[32,32,128]{2,1,0:T(8,128)(2,1)} all-gather(bf16[8,32,128]{2,1,0:T(8,128)(2,1)S(1)} %bitcast.141), channel_id=1, replica_groups=mesh['section'=4,'z'=8,'x'=4,'core'=2] {'x'}, dimensions={0}, use_global_device_ids=true | all-gather | bytes 327680 | tf_op jit(solution)/shard_map/all_gather | solution.py:36
  22.2 1.3 iota_reduce_fusion
  23.7 6.9 %gather_fusion = s32[1024]{0:T(1024)S(1)} fusion(s32[512]{0:T(512)S(1)} %bitcast.130, s32[1024]{0:T(1024)S(1)} %broadcast_clamp_fusion.1), kind=kCustom, calls=%fused_computation | custom fusion | bytes 12288 | tf_op jit(solution)/shard_map/gather | solution.py:48
  30.7 6.9 %gather_fusion.1 = s32[1024]{0:T(1024)S(1)} fusion(s32[512]{0:T(512)S(1)} %fusion.25, s32[1024]{0:T(1024)S(1)} %broadcast_clamp_fusion.2), kind=kCustom, calls=%fused_computation.1 | custom fusion | bytes 12288 | tf_op jit(solution)/shard_map/gather | solution.py:48
  37.8 27.2 %all-gather.3.cloned.1.call-done = bf16[256,32,128]{2,1,0:T(8,128)(2,1)} async-done(((bf16[32,32,128]{2,1,0:T(8,128)(2,1)}), bf16[256,32,128]{2,1,0:T(8,128)(2,1)}) %all-gather.3.cloned.1.call-update) | async-done | bytes 2097168 | tf_op jit(solution)/shard_map/all_gather | solution.py:37
  65.6 1.1 copy.44
  67.3 0.9 convert.8
  69.4 2.0 mul.145
  71.4 1.7 copy.46
  73.1 2.6 scatter_custom_fusion
  75.7 2.6 gather_fusion.4
  78.7 3.5 %gather_fusion.5 = s32[512]{0:T(512)S(1)} fusion(s32[512]{0:T(512)S(1)} %multiply_add_fusion, s32[1024]{0:T(1024)S(1)} %pad_clamp_fusion.1), kind=kCustom, calls=%fused_computation.5 | custom fusion | bytes 6144 | tf_op jit(solution)/shard_map/gather | solution.py:75
  84.3 0.7 fusion.43
  85.0 40.2 %select_compare_fusion = pred[512]{0:T(512)(128)(4,1)S(1)} fusion(s32[]{:T(128)} %bitcast.21, s32[]{:T(128)} %bitcast.22, s32[]{:T(128)} %bitcast.23, s32[]{:T(128)} %bitcast.24, s32[]{:T(128)} %bitcast.25, s32[]{:T(128)} %bitcast.26, s32[]{:T(128)} %bitcast.27, s32[]{:T(128)} %bitcast.28, s32[]{:T(128)} %bitcast.29, s32[]{:T(128)} %bitcast.30, s32[]{:T(128)} %bitcast.31, ...), kind=kLoop, calls=%fused_computation.86 | loop fusion | flops 76288 | bytes 2816 | tf_op jit(solution)/shard_map/lt | solution.py:67
  125.3 3.4 %gather_fusion.3 = pred[512]{0:T(512)(128)(4,1)S(1)} fusion(pred[512]{0:T(512)(128)(4,1)S(1)} %select_compare_fusion, s32[1024]{0:T(1024)S(1)} %pad_clamp_fusion.1), kind=kCustom, calls=%fused_computation.3 | custom fusion | bytes 3072 | tf_op jit(solution)/shard_map/gather | solution.py:75
  129.3 4.9 %concatenate.9 = bf16[513,32,128]{2,1,0:T(8,128)(2,1)} pad(bf16[512,32,128]{2,1,0:T(8,128)(2,1)} %all-gather.5.cloned.1.call-done, bf16[]{:T(256)} %constant.102.clone.1), padding=0_1x0_0x0_0 | pad | bytes 8396802 | tf_op jit(solution)/shard_map/concatenate | solution.py:82
  134.2 12.1 %gather_fusion.2 = bf16[1024,32,128]{2,1,0:T(8,128)(2,1)} fusion(bf16[513,32,128]{2,1,0:T(8,128)(2,1)} %concatenate.9, s32[1024]{0:T(1024)S(1)} %broadcast_clamp_fusion), kind=kCustom, calls=%fused_computation.2 | custom fusion | bytes 16781312 | tf_op jit(solution)/shard_map/gather | solution.py:83
  146.3 5.1 %convolution_bitcast_fusion.1 = f32[128,64,32,2]{0,2,3,1:T(8,128)S(1)} fusion(bf16[64,16,32,128,1]{3,2,1,4,0:T(8,128)(2,1)} %bitcast.136, pred[2,128]{1,0:T(4,128)(4,1)S(1)} %iota_compare_fusion.2, bf16[16,128,128]{2,1,0:T(8,128)(2,1)} %copy.44), kind=kOutput, calls=%fused_computation.18 | convolution fusion | flops 2148007936 | bytes 11010304 | tf_op jit(solution)/shard_map/cthl,pcrl->tprh/dot_general | solution.py:84
  151.4 0.8 fusion.4
  152.8 2.6 convolution_bitcast_fusion
  155.5 19.3 %copy.51 = f32[64,16,32,128]{3,2,1,0:T(8,128)} copy(f32[64,16,32,128]{3,0,2,1:T(8,128)S(1)} %convolution_bitcast_fusion) | data formatting | bytes 33554432 | tf_op jit(solution)/shard_map/prk,ckl->pcrl/transpose | solution.py:62
  174.8 10.1 %gather_fusion.6 = f32[512,32,128]{2,1,0:T(8,128)} fusion(f32[1024,32,128]{2,1,0:T(8,128)} %bitcast.134, s32[1024]{0:T(1024)S(1)} %pad_clamp_fusion), kind=kCustom, calls=%fused_computation.6 | custom fusion | bytes 16779264 | tf_op jit(solution)/shard_map/gather | solution.py:75
  184.9 6.3 %broadcast_select_fusion = f32[512,32,128]{2,1,0:T(8,128)} fusion(f32[512,32,128]{2,1,0:T(8,128)} %gather_fusion.6, pred[512]{0:T(512)(128)(4,1)S(1)} %gather_fusion.3), kind=kLoop, calls=%fused_computation.9 | loop fusion | flops 2097152 | bytes 16777728 | tf_op jit(solution)/shard_map/jit(_where)/select_n | solution.py:74
  191.2 20.3 %reduce-scatter.4.cloned.1.call-done = f32[256,32,128]{2,1,0:T(8,128)} async-done(((f32[512,32,128]{2,1,0:T(8,128)}), f32[256,32,128]{2,1,0:T(8,128)}) %reduce-scatter.4.cloned.1.call-update) | async-done | bytes 4194320 | tf_op jit(solution)/shard_map/reduce_scatter | solution.py:77
  211.6 1.5 copy-done.3
  213.1 1.9 copy.45
  215.7 2.7 collective-permute-start
  218.4 52.1 %reduce-scatter.6.cloned.1.call-done = f32[32,32,128]{2,1,0:T(8,128)} async-done(((f32[256,32,128]{2,1,0:T(8,128)}), f32[32,32,128]{2,1,0:T(8,128)}) %reduce-scatter.6.cloned.1.call-update) | async-done | bytes 524304 | tf_op jit(solution)/shard_map/reduce_scatter | solution.py:78
  270.6 1.3 copy.52
  271.9 23.9 %reduce-scatter.8.cloned.1.call-done = f32[8,32,128]{2,1,0:T(8,128)} async-done(((f32[32,32,128]{2,1,0:T(8,128)}), f32[8,32,128]{2,1,0:T(8,128)}) %reduce-scatter.8.cloned.1.call-update) | async-done | bytes 131088 | tf_op jit(solution)/shard_map/reduce_scatter | solution.py:79
  295.8 0.9 broadcast_multiply_fusion
  (76 shorter events, 8.9 us)
Async XLA Ops:
  7.2 16.5 %copy-start = (s32[1,512]{1,0:T(1,128)S(1)}, s32[1,512]{1,0:T(1,128)}, u32[]{:S(2)}) copy-start(s32[1,512]{1,0:T(1,128)} %param.13) | copy-start | bytes 6148
  7.2 57.8 %all-gather.3.cloned.1.call-start = ((), (), s32[]{:S(2)}) async-start(), calls=%async_computation.3 | async-start | bytes 2359296 | tf_op jit(solution)/shard_map/all_gather | solution.py:37
  21.4 107.8 %all-gather.5.cloned.1.call-start = ((), (), s32[]{:S(2)}) async-start(), calls=%async_computation.4 | async-start | bytes 6291456 | tf_op jit(solution)/shard_map/all_gather | solution.py:38
  30.7 7.0 %copy-start.1 = (s32[1,64,8]{1,2,0:T(8,128)S(1)}, s32[1,64,8]{1,2,0:T(8,128)}, u32[]{:S(2)}) copy-start(s32[1,64,8]{1,2,0:T(8,128)} %param.11) | copy-start | bytes 6148
  37.6 27.7 %copy-start.7 = (bf16[1,128,1024]{2,1,0:T(8,128)(2,1)S(1)}, bf16[1,128,1024]{2,1,0:T(8,128)(2,1)}, u32[]{:S(2)}) copy-start(bf16[1,128,1024]{2,1,0:T(8,128)(2,1)} %param.8) | copy-start | bytes 786436
  65.0 1.6 copy-start.6
  65.0 146.4 %reduce-scatter.4.cloned.1.call-start = ((), (), s32[]{:S(2)}) async-start(), calls=%async_computation.5 | async-start | bytes 12582912 | tf_op jit(solution)/shard_map/reduce_scatter | solution.py:77
  67.3 1.4 copy-start.8
  75.7 6.5 %copy-start.5 = (s32[1,64]{1,0:T(1,128)S(1)}, s32[1,64]{1,0:T(1,128)}, u32[]{:S(2)}) copy-start(s32[1,64]{1,0:T(1,128)} %param.12) | copy-start | bytes 772
  151.4 1.4 copy-start.2
  151.4 1.4 copy-start.4
  191.1 79.4 %reduce-scatter.6.cloned.1.call-start = ((), (), s32[]{:S(2)}) async-start(), calls=%async_computation.6 | async-start | bytes 4718592 | tf_op jit(solution)/shard_map/reduce_scatter | solution.py:78
  211.5 1.6 copy-start.3
  211.5 84.3 %reduce-scatter.8.cloned.1.call-start = ((), (), s32[]{:S(2)}) async-start(), calls=%async_computation.7 | async-start | bytes 655360 | tf_op jit(solution)/shard_map/reduce_scatter | solution.py:79
  215.7 54.8 %collective-permute-start = (bf16[128,4096]{0,1:T(8,128)(2,1)S(1)}, bf16[128,4096]{0,1:T(8,128)(2,1)S(1)}, u32[]{:S(2)}, u32[]{:S(2)}) collective-permute-start(bf16[128,4096]{0,1:T(8,128)(2,1)S(1)} %fusion.3), channel_id=1, source_target_pairs={{64,0},{128,64},{192,128},{65,1},{129,65},{193,129},{66,2},{130,66... | collective-permute-start | bytes 3145736 | tf_op jit(solution)/shard_map/ppermute | solution.py:13
Sparse Core Ops, SparseCore 0:
  21.6 43.3 all-gather.2
  66.8 17.3 all-gather.4
  191.3 20.1 reduce-scatter.3
  213.9 56.6 reduce-scatter.5
  272.9 22.8 reduce-scatter.7

commit v3 on v2

--- a/solution.py
+++ b/solution.py
@@ -37,15 +37,16 @@
     gathered = lax.all_gather(gathered, "z", axis=0, tiled=True)
     gathered = lax.all_gather(gathered, "core", axis=0, tiled=True)
     slot_ids = jnp.arange(store_slots, dtype=jnp.int32)
-    holder = slot_ids // slot_dev
-    row_of_slot = (holder % nc) * (nz * nx * slot_dev) + (holder // nc) * slot_dev + slot_ids % slot_dev
+
+    def row_of(slot):
+        holder = slot // slot_dev
+        return (holder % nc) * (nz * nx * slot_dev) + (holder // nc) * slot_dev + slot % slot_dev
 
     kept_grid = jnp.arange(most_kept)[None, :] < count_list[:, None]
     col_hit = (column_list[:, :, None] == jnp.arange(ncol)[None, None, :]) & kept_grid[:, :, None]
     has_tile = jnp.any(col_hit, axis=1)
-    k_of = jnp.argmax(col_hit, axis=1)
-    pos_of = jnp.arange(panel_list)[:, None] * most_kept + k_of
-    dense_rows = jnp.where(has_tile, row_of_slot[slot_lookup[pos_of]], store_slots)
+    hit_rows = jnp.sum(jnp.where(col_hit, row_of(slot_lookup.reshape(panel_list, most_kept))[:, :, None], 0), axis=1)
+    dense_rows = hit_rows.reshape(-1)
 
     mean_sq = jnp.mean(inputs_f * inputs_f, axis=1, keepdims=True)
     recip = lax.rsqrt(mean_sq + EPS)
@@ -59,28 +60,34 @@
     normed_pairs = normed.reshape(tok_rows, panel_list, half, 2).transpose(1, 2, 3, 0)
     normed_pairs = normed_pairs.reshape(panel_list, half, 2 * tok_rows)
     expand_k = expand.transpose(0, 2, 1, 3).reshape(ncol, 2 * tok_rows, lanes)
-    dense_terms = jnp.einsum("prk,ckl->pcrl", normed_pairs, expand_k, preferred_element_type=jnp.float32)
+    dense_terms = jnp.dot(
+        normed_pairs.reshape(panel_list * half, 2 * tok_rows),
+        expand_k.transpose(1, 0, 2).reshape(2 * tok_rows, ncol * lanes),
+        preferred_element_type=jnp.float32,
+    )
+    dense_terms = dense_terms.reshape(panel_list, half, ncol, lanes).transpose(0, 2, 1, 3)
     dense_terms = dense_terms.reshape(panel_list * ncol, half, lanes)
-    inverse_order = jnp.zeros((store_slots,), jnp.int32).at[slot_lookup].set(slot_ids)
-    pos = inverse_order
-    term_panel = pos // most_kept
-    term_kept = (pos % most_kept) < count_list[term_panel]
-    term_index = term_panel * ncol + column_list[term_panel, pos % most_kept]
     oc = jnp.arange(nc)[:, None, None, None]
     oz = jnp.arange(nz)[None, :, None, None]
     ox = jnp.arange(nx)[None, None, :, None]
     oj = jnp.arange(slot_dev)[None, None, None, :]
     rs_order = (((oz * nx + ox) * nc + oc) * slot_dev + oj).reshape(-1)
-    terms = jnp.where(
-        term_kept[rs_order][:, None, None], dense_terms[term_index[rs_order]], jnp.zeros((), jnp.float32)
-    )
+    slot_match = slot_lookup[None, :] == rs_order[:, None]
+    pos_panel = jnp.arange(store_slots, dtype=jnp.int32) // most_kept
+    pos_index = pos_panel * ncol + column_list.reshape(-1)
+    pos_kept = kept_grid.reshape(-1)
+    term_index = jnp.sum(jnp.where(slot_match, pos_index[None, :], 0), axis=1)
+    term_kept = jnp.any(slot_match & pos_kept[None, :], axis=1)
+    terms = jnp.where(term_kept[:, None, None], dense_terms[term_index], jnp.zeros((), jnp.float32))
+    terms, gathered = lax.optimization_barrier((terms, gathered))
     weight_grad = lax.psum_scatter(terms, "core", scatter_dimension=0, tiled=True)
     weight_grad = lax.psum_scatter(weight_grad, "z", scatter_dimension=0, tiled=True)
     weight_grad = lax.psum_scatter(weight_grad, "x", scatter_dimension=0, tiled=True)
     weight_grad = (weight_grad * grad_scale).reshape(slot_dev, blk * blk)
 
-    gathered_ext = jnp.concatenate([gathered, jnp.zeros((1, half, lanes), gathered.dtype)], axis=0)
-    dense_w = gathered_ext[dense_rows.reshape(-1)].reshape(panel_list, ncol, half, lanes)
+    dense_w = jnp.where(
+        has_tile.reshape(-1)[:, None, None], gathered[dense_rows], jnp.zeros((), gathered.dtype)
+    ).reshape(panel_list, ncol, half, lanes)
     normed_grad = jnp.einsum("cthl,pcrl->tprh", expand, dense_w, preferred_element_type=jnp.float32)
     normed_grad = normed_grad.reshape(tok_rows, width)
 

time: 305 us -> 224 us (0.73)
  local copies, waits for them, and re-layouts: 88.7 us -> 47.1 us
  other arithmetic: 53.4 us -> 12.4 us
  matrix products: 7.75 us -> 15.4 us
  waiting for transfers between devices: 124 us -> 118 us
    lt x1 -> x0, other arithmetic: 40.2 us -> none  [local(): term_kept = pos % most_kept < count_list[term_panel]]
    gather x14 -> x2, local copies, waits for them, and re-layouts: 48.5 us -> 22.2 us  [the longest x1 12.1 us: local(): gathered[dense_rows]]
    reduce_scatter x1, waiting for transfers between devices: 52.1 us -> 31.8 us  [local(): lax.psum_scatter(weight_grad, 'z', scatter_dimension=0, tiled=True)]
    transpose x1, local copies, waits for them, and re-layouts: 19.3 us -> 2.06 us  [local(): normed.reshape(tok_rows, panel_list, half, 2).transpose(1, 2, 3, 0)]
    all_gather x1, waiting for transfers between devices: 27.2 us -> 41.8 us  [local(): gathered = lax.all_gather(gathered, 'z', axis=0, tiled=True)]
    dot_general x1, matrix products: 2.63 us -> 9.63 us  [local(): jnp.dot(normed_pairs.reshape(panel_list * half, 2 * tok_rows), expand_k.t...]
    concatenate x1 -> x0, local copies, waits for them, and re-layouts: 4.88 us -> none  [local(): jnp.concatenate([gathered, jnp.zeros((1, half, lanes), gathered.dtype)],...]
    broadcast_in_dim x1 -> x4, local copies, waits for them, and re-layouts: 0.08 us -> 4.43 us  [local(): jnp.where(diag[None, None, :, :], og_wide[:, :, None, :], jnp.zeros((), k...]
  transfers between devices with their start and end apart: 6 -> 6, of which waited for: 4 -> 4; matrix products, arithmetic and copies ran while one was open for 28% -> 32% of each run, Pallas kernels for 0% -> 0%
where the time goes in v3:
time: 224 us
  waiting for transfers between devices  118 us (53%)
  local copies, waits for them, and re-layouts  47.1 us (21%)
  matrix products  15.4 us (7%)
  between operations  14 us (6%)
  blocking collectives  13.3 us (6%)
  other arithmetic  12.4 us (6%)
  starting transfers between devices  3.06 us (1%)
    all_gather x1, waiting for transfers between devices, local(): gathered = lax.all_gather(gathered, 'z', axis=0, tiled=True)  41.8 us
    reduce_scatter x1, waiting for transfers between devices, local(): lax.psum_scatter(weight_grad, 'z', scatter_dimension=0, tiled=True)  31.8 us
    reduce_scatter x1, waiting for transfers between devices, local(): lax.psum_scatter(weight_grad, 'x', scatter_dimension=0, tiled=True)  23.9 us
    reduce_scatter x1, waiting for transfers between devices, local(): lax.psum_scatter(terms, 'core', scatter_dimension=0, tiled=True)  20.5 us
    all_gather x1, blocking collectives, local(): gathered = lax.all_gather(own_tiles, 'x', axis=0, tiled=True)  13.3 us
    gather x1, local copies, waits for them, and re-layouts, local(): gathered[dense_rows]  12.1 us
    gather x1, local copies, waits for them, and re-layouts, local(): dense_terms[term_index]  10.1 us
    dot_general x1, matrix products, local(): jnp.dot(normed_pairs.reshape(panel_list * half, 2 * tok_rows), expand_k.t...  9.63 us
  transfers between devices with their start and end apart: 6, of which 4 were waited for; matrix products, arithmetic and copies ran while one was open for 32% of the time, Pallas kernels for 0%

profile of v3, /device:TPU:8, one launch (start us, length us, event | category | flops | bytes accessed | tf_op | source)
XLA Modules:
  0.0 223.5 jit_solution(8230067168556819841)
XLA Ops:
  7.2 0.9 copy.81
  8.1 13.3 %all_gather.9 = bf16[32,32,128]{2,1,0:T(8,128)(2,1)} all-gather(bf16[8,32,128]{2,1,0:T(8,128)(2,1)S(1)} %bitcast.78), channel_id=1, replica_groups=mesh['section'=4,'z'=8,'x'=4,'core'=2] {'x'}, dimensions={0}, use_global_device_ids=true | all-gather | bytes 327680 | tf_op jit(solution)/shard_map/all_gather | solution.py:36
  21.5 1.6 copy.54
  23.1 41.8 %all-gather.3.cloned.1.call-done = bf16[256,32,128]{2,1,0:T(8,128)(2,1)} async-done(((bf16[32,32,128]{2,1,0:T(8,128)(2,1)}), bf16[256,32,128]{2,1,0:T(8,128)(2,1)}) %all-gather.3.cloned.1.call-update) | async-done | bytes 2097168 | tf_op jit(solution)/shard_map/all_gather | solution.py:37
  65.0 0.6 fusion.5
  65.6 0.9 convert.4
  67.0 0.7 reduce.7
  67.7 2.0 mul.139
  69.6 1.7 copy.58
  71.3 0.7 fusion.13
  72.1 2.1 copy.59
  74.1 2.5 %reshape.382 = bf16[64,32,256,1]{2,1,0,3:T(8,128)(2,1)} reshape(bf16[64,32,2,128]{3,2,1,0:T(2,128)(2,1)} %copy.59) | data formatting | bytes 2097152 | tf_op jit(solution)/shard_map/dot_general | solution.py:63
  76.7 1.1 copy.61
  77.9 0.8 copy-done
  78.8 1.7 broadcast_in_dim.106
  80.5 2.5 %broadcast_in_dim.107 = bf16[16,256,128]{1,2,0:T(8,128)(2,1)} reshape(bf16[16,2,128,128]{2,1,3,0:T(2,128)(2,1)} %broadcast_in_dim.106) | data formatting | bytes 2097152 | tf_op jit(solution)/shard_map/jit(_where)/broadcast_in_dim | solution.py:58
  84.2 9.6 %fusion.14 = f32[64,32,16,128]{3,1,2,0:T(8,128)} fusion(bf16[64,32,256,1]{2,1,0,3:T(8,128)(2,1)} %reshape.382, bf16[16,256,128]{1,2,0:T(8,128)(2,1)} %broadcast_in_dim.107, pred[256,128]{0,1:T(8,128)(4,1)S(1)} %copy.60), kind=kOutput, calls=%fused_computation.21 | convolution fusion | flops 2148007936 | bytes 18907136 | tf_op jit(solution)/shard_map/dot_general | solution.py:63
  93.8 10.1 %gather_fusion = f32[512,32,128]{2,1,0:T(8,128)} fusion(f32[1024,32,128]{2,1,0:T(8,128)} %bitcast.72, s32[1024]{0:T(1024)S(1)} %pad_clamp_fusion), kind=kCustom, calls=%fused_computation | custom fusion | bytes 16779264 | tf_op jit(solution)/shard_map/gather | solution.py:81
  104.2 6.3 %broadcast_select_fusion = f32[512,32,128]{2,1,0:T(8,128)} fusion(f32[512,32,128]{2,1,0:T(8,128)} %gather_fusion, pred[512]{0:T(512)(128)(4,1)S(1)} %fusion.20), kind=kLoop, calls=%fused_computation.7 | loop fusion | flops 2097152 | bytes 16777728 | tf_op jit(solution)/shard_map/jit(_where)/select_n | solution.py:81
  110.5 20.5 %reduce-scatter.4.cloned.1.call-done = f32[256,32,128]{2,1,0:T(8,128)} async-done(((f32[512,32,128]{2,1,0:T(8,128)}), f32[256,32,128]{2,1,0:T(8,128)}) %reduce-scatter.4.cloned.1.call-update) | async-done | bytes 4194320 | tf_op jit(solution)/shard_map/reduce_scatter | solution.py:83
  131.4 2.1 copy.68
  133.9 0.7 reduce.8
  135.2 12.1 %gather_fusion.1 = bf16[1024,32,128]{2,1,0:T(8,128)(2,1)} fusion(bf16[512,32,128]{2,1,0:T(8,128)(2,1)} %all-gather.5.cloned.1.call-done, s32[1024]{0:T(1024)S(1)} %broadcast_clamp_fusion), kind=kCustom, calls=%fused_computation.1 | custom fusion | bytes 16781312 | tf_op jit(solution)/shard_map/gather | solution.py:89
  147.2 5.8 %multiply_reduce_fusion = (f32[128]{0:T(128)S(1)}, f32[128,64,32,2]{0,2,3,1:T(8,128)S(1)}) fusion(f32[128,64,32,2]{0,3,2,1:T(2,128)S(1)} %convert.4, f32[64,32,2]{1,2,0:T(2,128)S(1)} %copy.58, pred[2,128]{1,0:T(4,128)(4,1)S(1)} %iota_compare_fusion.2, bf16[16,128,128]{2,1,0:T(8,128)(2,1)} %copy.68, bf16[64,16,32,128]{3,2,1,0:T(8,128)(2,1)} %bitcast.74, ...), kind=kOutput, calls=%fused_computation.14 | convolution fusion | flops 2153775104 | bytes 13125376 | tf_op jit(solution)/shard_map/cthl,pcrl->tprh/dot_general | solution.py:91
  153.0 1.9 copy.69
  154.9 0.7 fusion.8
  155.7 2.7 %collective-permute-start = (bf16[128,4096]{0,1:T(8,128)(2,1)S(1)}, bf16[128,4096]{0,1:T(8,128)(2,1)S(1)}, u32[]{:S(2)}, u32[]{:S(2)}) collective-permute-start(bf16[128,4096]{0,1:T(8,128)(2,1)S(1)} %fusion.8), channel_id=1, source_target_pairs={{64,0},{128,64},{192,128},{65,1},{129,65},{193,129},{66,2},{130,66... | collective-permute-start | bytes 3145736 | tf_op jit(solution)/shard_map/ppermute | solution.py:13
  158.3 31.8 %reduce-scatter.6.cloned.1.call-done = f32[32,32,128]{2,1,0:T(8,128)} async-done(((f32[256,32,128]{2,1,0:T(8,128)}), f32[32,32,128]{2,1,0:T(8,128)}) %reduce-scatter.6.cloned.1.call-update) | async-done | bytes 524304 | tf_op jit(solution)/shard_map/reduce_scatter | solution.py:84
  190.2 1.3 copy.71
  191.5 23.9 %reduce-scatter.8.cloned.1.call-done = f32[8,32,128]{2,1,0:T(8,128)} async-done(((f32[32,32,128]{2,1,0:T(8,128)}), f32[8,32,128]{2,1,0:T(8,128)}) %reduce-scatter.8.cloned.1.call-update) | async-done | bytes 131088 | tf_op jit(solution)/shard_map/reduce_scatter | solution.py:85
  215.4 0.9 broadcast_multiply_fusion
  216.3 0.7 broadcast_in_dim_reshape.2
  (55 shorter events, 3.5 us)
Async XLA Ops:
  7.2 57.8 %all-gather.3.cloned.1.call-start = ((), (), s32[]{:S(2)}) async-start(), calls=%async_computation.3 | async-start | bytes 2359296 | tf_op jit(solution)/shard_map/all_gather | solution.py:37
  21.4 89.0 %all-gather.5.cloned.1.call-start = ((), (), s32[]{:S(2)}) async-start(), calls=%async_computation.4 | async-start | bytes 6291456 | tf_op jit(solution)/shard_map/all_gather | solution.py:38
  65.0 2.0 copy-start.1
  65.0 66.1 %reduce-scatter.4.cloned.1.call-start = ((), (), s32[]{:S(2)}) async-start(), calls=%async_computation.5 | async-start | bytes 12582912 | tf_op jit(solution)/shard_map/reduce_scatter | solution.py:83
  77.9 0.8 copy-start
  78.8 4.7 %copy-start.2 = (s32[1,64,8]{1,2,0:T(8,128)S(1)}, s32[1,64,8]{1,2,0:T(8,128)}, u32[]{:S(2)}) copy-start(s32[1,64,8]{1,2,0:T(8,128)} %param.11) | copy-start | bytes 6148
  78.8 4.9 %copy-start.4 = (s32[1,64]{1,0:T(1,128)S(1)}, s32[1,64]{1,0:T(1,128)}, u32[]{:S(2)}) copy-start(s32[1,64]{1,0:T(1,128)} %param.12) | copy-start | bytes 772
  78.8 5.1 %copy-start.3 = (s32[1,512]{1,0:T(1,128)S(1)}, s32[1,512]{1,0:T(1,128)}, u32[]{:S(2)}) copy-start(s32[1,512]{1,0:T(1,128)} %param.13) | copy-start | bytes 6148
  110.5 79.6 %reduce-scatter.6.cloned.1.call-start = ((), (), s32[]{:S(2)}) async-start(), calls=%async_computation.6 | async-start | bytes 4718592 | tf_op jit(solution)/shard_map/reduce_scatter | solution.py:84
  131.1 84.3 %reduce-scatter.8.cloned.1.call-start = ((), (), s32[]{:S(2)}) async-start(), calls=%async_computation.7 | async-start | bytes 655360 | tf_op jit(solution)/shard_map/reduce_scatter | solution.py:85
  155.7 34.5 %collective-permute-start = (bf16[128,4096]{0,1:T(8,128)(2,1)S(1)}, bf16[128,4096]{0,1:T(8,128)(2,1)S(1)}, u32[]{:S(2)}, u32[]{:S(2)}) collective-permute-start(bf16[128,4096]{0,1:T(8,128)(2,1)S(1)} %fusion.8), channel_id=1, source_target_pairs={{64,0},{128,64},{192,128},{65,1},{129,65},{193,129},{66,2},{130,66... | collective-permute-start | bytes 3145736 | tf_op jit(solution)/shard_map/ppermute | solution.py:13
Sparse Core Ops, SparseCore 0:
  21.6 43.3 all-gather.2
  66.8 17.5 all-gather.4
  110.6 20.4 reduce-scatter.3
  133.5 56.6 reduce-scatter.5
  192.5 22.8 reduce-scatter.7

commit v4 on v3

--- a/solution.py
+++ b/solution.py
@@ -35,7 +35,6 @@
     own_tiles = tiles[0].reshape(slot_dev, half, lanes)
     gathered = lax.all_gather(own_tiles, "x", axis=0, tiled=True)
     gathered = lax.all_gather(gathered, "z", axis=0, tiled=True)
-    gathered = lax.all_gather(gathered, "core", axis=0, tiled=True)
     slot_ids = jnp.arange(store_slots, dtype=jnp.int32)
 
     def row_of(slot):
@@ -60,13 +59,14 @@
     normed_pairs = normed.reshape(tok_rows, panel_list, half, 2).transpose(1, 2, 3, 0)
     normed_pairs = normed_pairs.reshape(panel_list, half, 2 * tok_rows)
     expand_k = expand.transpose(0, 2, 1, 3).reshape(ncol, 2 * tok_rows, lanes)
+    normed_pairs = jnp.concatenate([normed_pairs, jnp.zeros((1, half, 2 * tok_rows), normed_pairs.dtype)], axis=0)
     dense_terms = jnp.dot(
-        normed_pairs.reshape(panel_list * half, 2 * tok_rows),
+        normed_pairs.reshape((panel_list + 1) * half, 2 * tok_rows),
         expand_k.transpose(1, 0, 2).reshape(2 * tok_rows, ncol * lanes),
         preferred_element_type=jnp.float32,
     )
-    dense_terms = dense_terms.reshape(panel_list, half, ncol, lanes).transpose(0, 2, 1, 3)
-    dense_terms = dense_terms.reshape(panel_list * ncol, half, lanes)
+    dense_terms = dense_terms.reshape(panel_list + 1, half, ncol, lanes).transpose(0, 2, 1, 3)
+    dense_terms = dense_terms.reshape((panel_list + 1) * ncol, half, lanes)
     oc = jnp.arange(nc)[:, None, None, None]
     oz = jnp.arange(nz)[None, :, None, None]
     ox = jnp.arange(nx)[None, None, :, None]
@@ -78,8 +78,9 @@
     pos_kept = kept_grid.reshape(-1)
     term_index = jnp.sum(jnp.where(slot_match, pos_index[None, :], 0), axis=1)
     term_kept = jnp.any(slot_match & pos_kept[None, :], axis=1)
-    terms = jnp.where(term_kept[:, None, None], dense_terms[term_index], jnp.zeros((), jnp.float32))
+    terms = dense_terms[jnp.where(term_kept, term_index, panel_list * ncol)]
     terms, gathered = lax.optimization_barrier((terms, gathered))
+    gathered = lax.all_gather(gathered, "core", axis=0, tiled=True)
     weight_grad = lax.psum_scatter(terms, "core", scatter_dimension=0, tiled=True)
     weight_grad = lax.psum_scatter(weight_grad, "z", scatter_dimension=0, tiled=True)
     weight_grad = lax.psum_scatter(weight_grad, "x", scatter_dimension=0, tiled=True)

time: 224 us -> 203 us (0.906)
  waiting for transfers between devices: 118 us -> 110 us
  other arithmetic: 12.4 us -> 6.95 us
  local copies, waits for them, and re-layouts: 47.1 us -> 42.7 us
  matrix products: 15.4 us -> 13 us
    all_gather x1, waiting for transfers between devices: 41.8 us -> 9.39 us  [local(): gathered = lax.all_gather(gathered, 'z', axis=0, tiled=True)]
    all_gather x1, waiting for transfers between devices: 0.01 us -> 18.2 us  [local(): gathered = lax.all_gather(gathered, 'core', axis=0, tiled=True)]
    select_n x2, other arithmetic: 6.28 us -> 0.01 us  [local(): terms = dense_terms[jnp.where(term_kept, term_index, panel_list * ncol)]]
    reduce_scatter x1, waiting for transfers between devices: 31.8 us -> 35 us  [local(): lax.psum_scatter(weight_grad, 'z', scatter_dimension=0, tiled=True)]
    dot_general x1 -> x0, local copies, waits for them, and re-layouts: 2.53 us -> none  [local(): jnp.dot(normed_pairs.reshape(panel_list * half, 2 * tok_rows), expand_k.t...]
    dot_general x1, matrix products: 9.63 us -> 7.19 us  [local(): jnp.dot(normed_pairs.reshape((panel_list + 1) * half, 2 * tok_rows), expa...]
    unnamed x17 -> x19, local copies, waits for them, and re-layouts: 6.86 us -> 6.83 us
  transfers between devices with their start and end apart: 6 -> 6, of which waited for: 4 -> 5; matrix products, arithmetic and copies ran while one was open for 32% -> 29% of each run, Pallas kernels for 0% -> 0%
where the time goes in v4:
time: 203 us; the launch traced here: 202 us
  waiting for transfers between devices  110 us (54%)
  local copies, waits for them, and re-layouts  42.7 us (21%)
  between operations  14 us (7%)
  blocking collectives  13.3 us (7%)
  matrix products  13 us (6%)
  other arithmetic  6.95 us (3%)
  starting transfers between devices  2.89 us (1%)
    reduce_scatter x1, waiting for transfers between devices, local(): lax.psum_scatter(weight_grad, 'z', scatter_dimension=0, tiled=True)  35 us
    reduce_scatter x1, waiting for transfers between devices, local(): lax.psum_scatter(weight_grad, 'x', scatter_dimension=0, tiled=True)  23.9 us
    reduce_scatter x1, waiting for transfers between devices, local(): lax.psum_scatter(terms, 'core', scatter_dimension=0, tiled=True)  22.3 us
    all_gather x1, waiting for transfers between devices, local(): gathered = lax.all_gather(gathered, 'core', axis=0, tiled=True)  18.2 us
    all_gather x1, blocking collectives, local(): gathered = lax.all_gather(own_tiles, 'x', axis=0, tiled=True)  13.3 us
    gather x1, local copies, waits for them, and re-layouts, local(): gathered[dense_rows]  12.1 us
    gather x1, local copies, waits for them, and re-layouts, local(): terms = dense_terms[jnp.where(term_kept, term_index, panel_list * ncol)]  10.3 us
    all_gather x1, waiting for transfers between devices, local(): gathered = lax.all_gather(gathered, 'z', axis=0, tiled=True)  9.39 us
  transfers between devices with their start and end apart: 6, of which 5 were waited for; matrix products, arithmetic and copies ran while one was open for 29% of the time, Pallas kernels for 0%

profile of v4, /device:TPU:8, one launch (start us, length us, event | category | flops | bytes accessed | tf_op | source)
XLA Modules:
  0.0 202.5 jit_solution(1272518827935144545)
XLA Ops:
  7.2 0.9 copy.85
  8.1 13.3 %all_gather.9 = bf16[32,32,128]{2,1,0:T(8,128)(2,1)} all-gather(bf16[8,32,128]{2,1,0:T(8,128)(2,1)S(1)} %bitcast.84), channel_id=1, replica_groups=mesh['section'=4,'z'=8,'x'=4,'core'=2] {'x'}, dimensions={0}, use_global_device_ids=true | all-gather | bytes 327680 | tf_op jit(solution)/shard_map/all_gather | solution.py:36
  21.5 1.6 copy.55
  23.1 0.9 convert.4
  24.0 0.5 broadcast.370
  24.5 0.7 reduce.7
  25.2 2.0 mul.134
  27.2 1.7 copy.59
  28.9 1.1 copy.62
  30.1 0.8 copy-done
  30.9 1.7 broadcast_in_dim.97
  32.7 2.5 %broadcast_in_dim.98 = bf16[16,256,128]{1,2,0:T(8,128)(2,1)} reshape(bf16[16,2,128,128]{2,1,3,0:T(2,128)(2,1)} %broadcast_in_dim.97) | data formatting | bytes 2097152 | tf_op jit(solution)/shard_map/jit(_where)/broadcast_in_dim | solution.py:57
  36.6 0.6 fusion.5
  37.2 0.7 copy_bitcast_fusion
  37.9 7.2 %fusion.12 = f32[65,32,16,128]{3,1,2,0:T(8,128)} fusion(bf16[64,32,256]{2,1,0:T(8,128)(2,1)S(1)} %copy_bitcast_fusion, bf16[16,256,128]{1,2,0:T(8,128)(2,1)S(1)} %copy-done.1, pred[256,128]{0,1:T(8,128)(4,1)S(1)} %copy.61), kind=kOutput, calls=%fused_computation.18 | convolution fusion | flops 2181562368 | bytes 19169280 | tf_op jit(solution)/shard_map/dot_general | solution.py:63
  45.1 10.3 %gather_fusion = f32[512,32,128]{2,1,0:T(8,128)} fusion(f32[1040,32,128]{2,1,0:T(8,128)} %bitcast.78, s32[1024]{0:T(1024)S(1)} %pad_clamp_fusion), kind=kCustom, calls=%fused_computation | custom fusion | bytes 16779264 | tf_op jit(solution)/shard_map/gather | solution.py:81
  55.4 9.4 %all-gather.3.cloned.1.call-done = bf16[256,32,128]{2,1,0:T(8,128)(2,1)} async-done(((bf16[32,32,128]{2,1,0:T(8,128)(2,1)}), bf16[256,32,128]{2,1,0:T(8,128)(2,1)}) %all-gather.3.cloned.1.call-update) | async-done | bytes 2097168 | tf_op jit(solution)/shard_map/all_gather | solution.py:37
  64.9 0.7 all-gather.5.cloned.1.call-update
  65.6 22.3 %reduce-scatter.4.cloned.1.call-done = f32[256,32,128]{2,1,0:T(8,128)} async-done(((f32[512,32,128]{2,1,0:T(8,128)}), f32[256,32,128]{2,1,0:T(8,128)}) %reduce-scatter.4.cloned.1.call-update) | async-done | bytes 4194320 | tf_op jit(solution)/shard_map/reduce_scatter | solution.py:84
  88.1 2.1 %copy.69 = bf16[16,128,128]{2,1,0:T(8,128)(2,1)} copy(bf16[16,128,128]{1,2,0:T(8,128)(2,1)} %copy-done) | data formatting | bytes 1048576 | tf_op jit(solution)/shard_map/concatenate | solution.py:56
  90.6 0.7 reduce.8
  91.8 18.2 %all-gather.5.cloned.1.call-done = bf16[512,32,128]{2,1,0:T(8,128)(2,1)} async-done(((bf16[256,32,128]{2,1,0:T(8,128)(2,1)}), bf16[512,32,128]{2,1,0:T(8,128)(2,1)}) %all-gather.5.cloned.1.call-update) | async-done | bytes 4194320 | tf_op jit(solution)/shard_map/all_gather | solution.py:83
  110.1 12.1 %gather_fusion.1 = bf16[1024,32,128]{2,1,0:T(8,128)(2,1)} fusion(bf16[512,32,128]{2,1,0:T(8,128)(2,1)} %all-gather.5.cloned.1.call-done, s32[1024]{0:T(1024)S(1)} %broadcast_clamp_fusion), kind=kCustom, calls=%fused_computation.1 | custom fusion | bytes 16781312 | tf_op jit(solution)/shard_map/gather | solution.py:90
  122.1 5.8 %multiply_reduce_fusion = (f32[128]{0:T(128)S(1)}, f32[128,64,32,2]{0,2,3,1:T(8,128)S(1)}) fusion(f32[128,64,32,2]{0,3,2,1:T(2,128)S(1)} %convert.4, f32[64,32,2]{1,2,0:T(2,128)S(1)} %copy.59, pred[2,128]{1,0:T(4,128)(4,1)S(1)} %iota_compare_fusion.2, bf16[16,128,128]{2,1,0:T(8,128)(2,1)} %copy.69, bf16[64,16,32,128]{3,2,1,0:T(8,128)(2,1)} %bitcast.80, ...), kind=kOutput, calls=%fused_computation.13 | convolution fusion | flops 2153775104 | bytes 13125376 | tf_op jit(solution)/shard_map/cthl,pcrl->tprh/dot_general | solution.py:92
  128.0 1.9 copy.70
  129.9 1.5 fusion.8
  131.4 2.7 %collective-permute-start = (bf16[128,4096]{0,1:T(8,128)(2,1)}, bf16[128,4096]{0,1:T(8,128)(2,1)S(1)}, u32[]{:S(2)}, u32[]{:S(2)}) collective-permute-start(bf16[128,4096]{0,1:T(8,128)(2,1)} %fusion.8), channel_id=1, source_target_pairs={{64,0},{128,64},{192,128},{65,1},{129,65},{193,129},{66,2},{130,66... | collective-permute-start | bytes 3145736 | tf_op jit(solution)/shard_map/ppermute | solution.py:13
  134.1 35.0 %reduce-scatter.6.cloned.1.call-done = f32[32,32,128]{2,1,0:T(8,128)} async-done(((f32[256,32,128]{2,1,0:T(8,128)}), f32[32,32,128]{2,1,0:T(8,128)}) %reduce-scatter.6.cloned.1.call-update) | async-done | bytes 524304 | tf_op jit(solution)/shard_map/reduce_scatter | solution.py:85
  169.1 1.3 copy.72
  170.5 23.9 %reduce-scatter.8.cloned.1.call-done = f32[8,32,128]{2,1,0:T(8,128)} async-done(((f32[32,32,128]{2,1,0:T(8,128)}), f32[8,32,128]{2,1,0:T(8,128)}) %reduce-scatter.8.cloned.1.call-update) | async-done | bytes 131088 | tf_op jit(solution)/shard_map/reduce_scatter | solution.py:86
  194.3 0.9 broadcast_multiply_fusion
  195.2 0.7 broadcast_in_dim_reshape.2
  (55 shorter events, 2.8 us)
Async XLA Ops:
  7.2 57.6 %all-gather.3.cloned.1.call-start = ((), (), s32[]{:S(2)}) async-start(), calls=%async_computation.3 | async-start | bytes 2359296 | tf_op jit(solution)/shard_map/all_gather | solution.py:37
  21.4 66.5 %reduce-scatter.4.cloned.1.call-start = ((), (), s32[]{:S(2)}) async-start(), calls=%async_computation.5 | async-start | bytes 12582912 | tf_op jit(solution)/shard_map/reduce_scatter | solution.py:84
  23.1 1.4 copy-start.2
  30.1 0.8 copy-start
  30.9 4.7 %copy-start.5 = (s32[1,64]{1,0:T(1,128)S(1)}, s32[1,64]{1,0:T(1,128)}, u32[]{:S(2)}) copy-start(s32[1,64]{1,0:T(1,128)} %param.12) | copy-start | bytes 772
  30.9 4.9 %copy-start.3 = (s32[1,64,8]{1,2,0:T(8,128)S(1)}, s32[1,64,8]{1,2,0:T(8,128)}, u32[]{:S(2)}) copy-start(s32[1,64,8]{1,2,0:T(8,128)} %param.11) | copy-start | bytes 6148
  30.9 5.1 %copy-start.4 = (s32[1,512]{1,0:T(1,128)S(1)}, s32[1,512]{1,0:T(1,128)}, u32[]{:S(2)}) copy-start(s32[1,512]{1,0:T(1,128)} %param.13) | copy-start | bytes 6148
  36.6 1.3 copy-start.1
  64.8 45.2 %all-gather.5.cloned.1.call-start = ((), (), s32[]{:S(2)}) async-start(), calls=%async_computation.4 | async-start | bytes 6291456 | tf_op jit(solution)/shard_map/all_gather | solution.py:83
  65.6 103.5 %reduce-scatter.6.cloned.1.call-start = ((), (), s32[]{:S(2)}) async-start(), calls=%async_computation.6 | async-start | bytes 4718592 | tf_op jit(solution)/shard_map/reduce_scatter | solution.py:85
  87.9 106.4 %reduce-scatter.8.cloned.1.call-start = ((), (), s32[]{:S(2)}) async-start(), calls=%async_computation.7 | async-start | bytes 655360 | tf_op jit(solution)/shard_map/reduce_scatter | solution.py:86
  131.4 37.7 %collective-permute-start = (bf16[128,4096]{0,1:T(8,128)(2,1)}, bf16[128,4096]{0,1:T(8,128)(2,1)S(1)}, u32[]{:S(2)}, u32[]{:S(2)}) collective-permute-start(bf16[128,4096]{0,1:T(8,128)(2,1)} %fusion.8), channel_id=1, source_target_pairs={{64,0},{128,64},{192,128},{65,1},{129,65},{193,129},{66,2},{130,66... | collective-permute-start | bytes 3145736 | tf_op jit(solution)/shard_map/ppermute | solution.py:13
Sparse Core Ops, SparseCore 0:
  21.6 43.1 all-gather.2
  67.3 20.5 reduce-scatter.3
  89.7 20.2 all-gather.4
  112.5 56.6 reduce-scatter.5
  171.5 22.7 reduce-scatter.7

commit v5 on v4

--- a/solution.py
+++ b/solution.py
@@ -11,6 +11,11 @@
     count = lax.axis_size(axis)
     leading, last = (max(0, -steps), min(count, count - steps))
     return lax.ppermute(value, axis, [(source, source + steps) for source in range(leading, last)])
+
+
+def sibling(value):
+    count = lax.axis_size("core")
+    return lax.ppermute(value, "core", [(source, (source + 1) % count) for source in range(count)])
 
 
 def local(acts, out_grad, norm_gain, tiles, tile_cols, tile_count, tile_store_slot):
@@ -37,9 +42,12 @@
     gathered = lax.all_gather(gathered, "z", axis=0, tiled=True)
     slot_ids = jnp.arange(store_slots, dtype=jnp.int32)
 
+    my_core = lax.axis_index("core")
+
     def row_of(slot):
         holder = slot // slot_dev
-        return (holder % nc) * (nz * nx * slot_dev) + (holder // nc) * slot_dev + slot % slot_dev
+        half_of = (holder % nc - my_core) % nc
+        return half_of * (nz * nx * slot_dev) + (holder // nc) * slot_dev + slot % slot_dev
 
     kept_grid = jnp.arange(most_kept)[None, :] < count_list[:, None]
     col_hit = (column_list[:, :, None] == jnp.arange(ncol)[None, None, :]) & kept_grid[:, :, None]
@@ -50,28 +58,33 @@
     mean_sq = jnp.mean(inputs_f * inputs_f, axis=1, keepdims=True)
     recip = lax.rsqrt(mean_sq + EPS)
     normed = (inputs_f * recip * gain_row[None, :]).astype(jnp.bfloat16)
+    pair_tokens = nc * tok_rows
+    normed_pair = jnp.concatenate([normed, sibling(normed)], axis=0)
+    og_pair = jnp.concatenate([key_grad, sibling(key_grad)], axis=0)
 
     og_blocks = key_grad.reshape(tok_rows, ncol, blk).transpose(1, 0, 2)
     diag = (jnp.arange(2)[:, None] == jnp.arange(lanes)[None, :] // blk)
     og_wide = jnp.concatenate([og_blocks, og_blocks], axis=2)
     expand = jnp.where(diag[None, None, :, :], og_wide[:, :, None, :], jnp.zeros((), key_grad.dtype))
 
-    normed_pairs = normed.reshape(tok_rows, panel_list, half, 2).transpose(1, 2, 3, 0)
-    normed_pairs = normed_pairs.reshape(panel_list, half, 2 * tok_rows)
-    expand_k = expand.transpose(0, 2, 1, 3).reshape(ncol, 2 * tok_rows, lanes)
-    normed_pairs = jnp.concatenate([normed_pairs, jnp.zeros((1, half, 2 * tok_rows), normed_pairs.dtype)], axis=0)
+    pair_blocks = og_pair.reshape(pair_tokens, ncol, blk).transpose(1, 0, 2)
+    pair_wide = jnp.concatenate([pair_blocks, pair_blocks], axis=2)
+    expand_pair = jnp.where(diag[None, None, :, :], pair_wide[:, :, None, :], jnp.zeros((), key_grad.dtype))
+    normed_pairs = normed_pair.reshape(pair_tokens, panel_list, half, 2).transpose(1, 2, 3, 0)
+    normed_pairs = normed_pairs.reshape(panel_list, half, 2 * pair_tokens)
+    expand_k = expand_pair.transpose(0, 2, 1, 3).reshape(ncol, 2 * pair_tokens, lanes)
+    normed_pairs = jnp.concatenate([normed_pairs, jnp.zeros((1, half, 2 * pair_tokens), normed_pairs.dtype)], axis=0)
     dense_terms = jnp.dot(
-        normed_pairs.reshape((panel_list + 1) * half, 2 * tok_rows),
-        expand_k.transpose(1, 0, 2).reshape(2 * tok_rows, ncol * lanes),
+        normed_pairs.reshape((panel_list + 1) * half, 2 * pair_tokens),
+        expand_k.transpose(1, 0, 2).reshape(2 * pair_tokens, ncol * lanes),
         preferred_element_type=jnp.float32,
     )
     dense_terms = dense_terms.reshape(panel_list + 1, half, ncol, lanes).transpose(0, 2, 1, 3)
     dense_terms = dense_terms.reshape((panel_list + 1) * ncol, half, lanes)
-    oc = jnp.arange(nc)[:, None, None, None]
-    oz = jnp.arange(nz)[None, :, None, None]
-    ox = jnp.arange(nx)[None, None, :, None]
-    oj = jnp.arange(slot_dev)[None, None, None, :]
-    rs_order = (((oz * nx + ox) * nc + oc) * slot_dev + oj).reshape(-1)
+    oz = jnp.arange(nz)[:, None, None]
+    ox = jnp.arange(nx)[None, :, None]
+    oj = jnp.arange(slot_dev)[None, None, :]
+    rs_order = (((oz * nx + ox) * nc + my_core) * slot_dev + oj).reshape(-1)
     slot_match = slot_lookup[None, :] == rs_order[:, None]
     pos_panel = jnp.arange(store_slots, dtype=jnp.int32) // most_kept
     pos_index = pos_panel * ncol + column_list.reshape(-1)
@@ -80,9 +93,8 @@
     term_kept = jnp.any(slot_match & pos_kept[None, :], axis=1)
     terms = dense_terms[jnp.where(term_kept, term_index, panel_list * ncol)]
     terms, gathered = lax.optimization_barrier((terms, gathered))
-    gathered = lax.all_gather(gathered, "core", axis=0, tiled=True)
-    weight_grad = lax.psum_scatter(terms, "core", scatter_dimension=0, tiled=True)
-    weight_grad = lax.psum_scatter(weight_grad, "z", scatter_dimension=0, tiled=True)
+    gathered = jnp.concatenate([gathered, sibling(gathered)], axis=0)
+    weight_grad = lax.psum_scatter(terms, "z", scatter_dimension=0, tiled=True)
     weight_grad = lax.psum_scatter(weight_grad, "x", scatter_dimension=0, tiled=True)
     weight_grad = (weight_grad * grad_scale).reshape(slot_dev, blk * blk)
 

time: 203 us -> 159 us (0.78)
  waiting for transfers between devices: 110 us -> 55.2 us
  other arithmetic: 6.95 us -> 14.7 us
  matrix products: 13 us -> 15.5 us
    reduce_scatter x2 -> x1, waiting for transfers between devices: 57.3 us -> 20.5 us  [local(): weight_grad = lax.psum_scatter(terms, 'z', scatter_dimension=0, tiled=True)]
    all_gather x1 -> x0, waiting for transfers between devices: 18.2 us -> none  [local(): gathered = lax.all_gather(gathered, 'core', axis=0, tiled=True)]
    reshape x0 -> x2, local copies, waits for them, and re-layouts: none -> 6.8 us  [the longest x1 4.54 us: local(): normed_pairs = normed_pairs.reshape(panel_list, half, 2 * pair_tokens)]
    concatenate x0 -> x3, other arithmetic: none -> 6.47 us  [the longest x1 4.58 us: local(): gathered = jnp.concatenate([gathered, sibling(gathered)], axis=0)]
    ppermute x1, waiting for transfers between devices: 0.01 us -> 4.45 us  [shifted(): lax.ppermute(value, axis, [(source, source + steps) for source in range(l...]
    reduce_scatter x1, waiting for transfers between devices: 23.9 us -> 19.6 us  [local(): lax.psum_scatter(weight_grad, 'x', scatter_dimension=0, tiled=True)]
    unnamed x19 -> x23, local copies, waits for them, and re-layouts: 6.83 us -> 4.26 us
    dot_general x1, matrix products: 7.19 us -> 9.64 us  [local(): jnp.dot(normed_pairs.reshape((panel_list + 1) * half, 2 * pair_tokens), e...]
  transfers between devices with their start and end apart: 6 -> 7, of which waited for: 5 -> 4; matrix products, arithmetic and copies ran while one was open for 29% -> 42% of each run, Pallas kernels for 0% -> 0%
where the time goes in v5:
time: 159 us
  waiting for transfers between devices  55.2 us (35%)
  local copies, waits for them, and re-layouts  42.4 us (27%)
  matrix products  15.5 us (10%)
  other arithmetic  14.7 us (9%)
  between operations  14.1 us (9%)
  blocking collectives  13.3 us (8%)
  starting transfers between devices  3.45 us (2%)
    reduce_scatter x1, waiting for transfers between devices, local(): weight_grad = lax.psum_scatter(terms, 'z', scatter_dimension=0, tiled=True)  20.5 us
    reduce_scatter x1, waiting for transfers between devices, local(): lax.psum_scatter(weight_grad, 'x', scatter_dimension=0, tiled=True)  19.6 us
    all_gather x1, blocking collectives, local(): gathered = lax.all_gather(own_tiles, 'x', axis=0, tiled=True)  13.3 us
    gather x1, local copies, waits for them, and re-layouts, local(): gathered[dense_rows]  12.1 us
    all_gather x1, waiting for transfers between devices, local(): gathered = lax.all_gather(gathered, 'z', axis=0, tiled=True)  10.6 us
    dot_general x1, matrix products, local(): jnp.dot(normed_pairs.reshape((panel_list + 1) * half, 2 * pair_tokens), e...  9.64 us
    gather x1, local copies, waits for them, and re-layouts, local(): terms = dense_terms[jnp.where(term_kept, term_index, panel_list * ncol)]  8.83 us
    dot_general x1, matrix products, local(): jnp.einsum('cthl,pcrl->tprh', expand, dense_w, preferred_element_type=jnp...  5.83 us
  transfers between devices with their start and end apart: 7, of which 4 were waited for; matrix products, arithmetic and copies ran while one was open for 42% of the time, Pallas kernels for 0%

profile of v5, /device:TPU:8, one launch (start us, length us, event | category | flops | bytes accessed | tf_op | source)
XLA Modules:
  0.0 158.7 jit_solution(8936962513074828035)
XLA Ops:
  7.2 1.6 %copy.52 = bf16[1,128,4096]{1,2,0:T(8,128)(2,1)S(1)} copy(bf16[1,128,4096]{2,1,0:T(8,128)(2,1)} %param.7) | data formatting | bytes 2097152 | tf_op args[0]
  8.9 0.6 fusion.9
  9.5 1.5 fusion.11
  11.2 0.6 collective-permute-start.1
  11.8 13.3 %all_gather.6 = bf16[32,32,128]{2,1,0:T(8,128)(2,1)} all-gather(bf16[8,32,128]{2,1,0:T(8,128)(2,1)S(1)} %bitcast.93), channel_id=1, replica_groups=mesh['section'=4,'z'=8,'x'=4,'core'=2] {'x'}, dimensions={0}, use_global_device_ids=true | all-gather | bytes 327680 | tf_op jit(solution)/shard_map/all_gather | solution.py:41
  26.7 1.7 %broadcast_in_dim.112 = bf16[16,2,256,128]{2,1,3,0:T(2,128)(2,1)S(1)} broadcast(bf16[16,256,128]{1,2,0:T(8,128)(2,1)S(1)} %pad_maximum_fusion.2), dimensions={0,2,3} | broadcast | bytes 3145728 | tf_op jit(solution)/shard_map/jit(_where)/broadcast_in_dim | solution.py:72
  28.5 2.7 %broadcast_in_dim.113 = bf16[16,512,128]{1,2,0:T(8,128)(2,1)} reshape(bf16[16,2,256,128]{2,1,3,0:T(2,128)(2,1)S(1)} %broadcast_in_dim.112) | data formatting | bytes 4194304 | tf_op jit(solution)/shard_map/jit(_where)/broadcast_in_dim | solution.py:72
  31.1 1.8 %pad_maximum_fusion.1 = bf16[256,4096]{0,1:T(8,128)(2,1)S(1)} fusion(bf16[128,4096]{0,1:T(8,128)(2,1)} %collective-permute-done, bf16[128,4096]{0,1:T(8,128)(2,1)} %fusion.11), kind=kLoop, calls=%fused_computation.11 | loop fusion | flops 4194304 | bytes 4194304 | tf_op jit(solution)/shard_map/concatenate | solution.py:62
  32.9 2.3 %reshape.373 = bf16[256,64,32,2]{0,3,2,1:T(2,128)(2,1)} reshape(bf16[256,4096]{0,1:T(8,128)(2,1)S(1)} %pad_maximum_fusion.1) | data formatting | bytes 4194304 | tf_op jit(solution)/shard_map/reshape | solution.py:73
  35.2 4.5 %reshape.374 = bf16[64,32,512]{2,1,0:T(8,128)(2,1)} reshape(bf16[64,32,2,256]{3,2,1,0:T(2,128)(2,1)} %bitcast.87) | data formatting | bytes 4194304 | tf_op jit(solution)/shard_map/reshape | solution.py:74
  39.7 9.6 %fusion.5 = f32[65,32,16,128]{3,1,2,0:T(8,128)} fusion(bf16[64,32,512]{2,1,0:T(8,128)(2,1)} %reshape.374, bf16[16,512,128]{1,2,0:T(8,128)(2,1)S(1)} %copy-done.1, pred[512,128]{0,1:T(8,128)(4,1)S(1)} %copy.55), kind=kOutput, calls=%fused_computation.8 | convolution fusion | flops 4363124736 | bytes 21299200 | tf_op jit(solution)/shard_map/dot_general | solution.py:77
  49.4 8.8 %gather_fusion = f32[256,32,128]{2,1,0:T(8,128)} fusion(f32[1040,32,128]{2,1,0:T(8,128)} %bitcast.92, s32[1024]{0:T(1024)S(1)} %pad_clamp_fusion), kind=kCustom, calls=%fused_computation | custom fusion | bytes 8389632 | tf_op jit(solution)/shard_map/gather | solution.py:94
  58.2 10.6 %all-gather.2.cloned.1.call-done = bf16[256,32,128]{2,1,0:T(8,128)(2,1)} async-done(((bf16[32,32,128]{2,1,0:T(8,128)(2,1)}), bf16[256,32,128]{2,1,0:T(8,128)(2,1)}) %all-gather.2.cloned.1.call-update) | async-done | bytes 2097168 | tf_op jit(solution)/shard_map/all_gather | solution.py:42
  69.2 0.5 broadcast.386
  69.7 0.7 reduce.7
  70.8 2.3 %convert.4 = f32[128,64,32,2]{0,3,2,1:T(2,128)} convert(bf16[128,64,32,2]{0,3,2,1:T(2,128)(2,1)S(1)} %bitcast.84) | non-fusion elementwise | flops 524288 | bytes 3145728 | tf_op jit(solution)/shard_map/convert_element_type | solution.py:22
  73.3 1.0 copy.64
  74.3 0.5 broadcast.387
  74.8 0.7 reduce.8
  75.5 1.0 mul.144
  77.0 4.6 %pad_maximum_fusion = bf16[512,32,128]{2,1,0:T(8,128)(2,1)} fusion(bf16[256,32,128]{2,1,0:T(8,128)(2,1)} %collective-permute-done.2, bf16[256,32,128]{2,1,0:T(8,128)(2,1)} %all-gather.2.cloned.1.call-done), kind=kLoop, calls=%fused_computation.6 | loop fusion | flops 2097152 | bytes 8388608 | tf_op jit(solution)/shard_map/concatenate | solution.py:96
  81.6 12.1 %gather_fusion.1 = bf16[1024,32,128]{2,1,0:T(8,128)(2,1)} fusion(bf16[512,32,128]{2,1,0:T(8,128)(2,1)} %pad_maximum_fusion, s32[1024]{0:T(1024)S(1)} %broadcast_clamp_fusion), kind=kCustom, calls=%fused_computation.1 | custom fusion | bytes 16781312 | tf_op jit(solution)/shard_map/gather | solution.py:102
  93.7 5.8 %fusion.15 = (f32[128]{0:T(128)S(1)}, f32[128,64,32,2]{0,2,3,1:T(8,128)S(1)}) fusion(f32[128,64,32,2]{0,3,2,1:T(2,128)S(1)} %copy-done, f32[64,32,2]{1,2,0:T(2,128)S(1)} %copy.66, pred[2,128]{1,0:T(4,128)(4,1)S(1)} %iota_compare_fusion.2, bf16[16,128,128]{2,1,0:T(8,128)(2,1)} %copy.64, bf16[64,16,32,128]{3,2,1,0:T(8,128)(2,1)} %bitcast.85, ...), kind=kOutput, calls=%fused_computation.23 | convolution fusion | flops 2153775104 | bytes 13125376 | tf_op jit(solution)/shard_map/cthl,pcrl->tprh/dot_general | solution.py:104
  99.6 1.9 %copy.65 = f32[128,64,32,2]{0,3,2,1:T(2,128)S(1)} copy(f32[128,64,32,2]{0,2,3,1:T(8,128)S(1)} %get-tuple-element.17) | data formatting | bytes 4194304 | tf_op jit(solution)/shard_map/cthl,pcrl->tprh/transpose | solution.py:104
  101.5 0.7 fusion.14
  102.2 2.5 %collective-permute-start.3 = (bf16[128,4096]{0,1:T(8,128)(2,1)S(1)}, bf16[128,4096]{0,1:T(8,128)(2,1)S(1)}, u32[]{:S(2)}, u32[]{:S(2)}) collective-permute-start(bf16[128,4096]{0,1:T(8,128)(2,1)S(1)} %fusion.14), channel_id=1, source_target_pairs={{64,0},{128,64},{192,128},{65,1},{129,65},{193,129},{66,2},{130,66... | collective-permute-start | bytes 3145736 | tf_op jit(solution)/shard_map/ppermute | solution.py:13
  104.7 20.5 %reduce-scatter.3.cloned.1.call-done = f32[32,32,128]{2,1,0:T(8,128)} async-done(((f32[256,32,128]{2,1,0:T(8,128)}), f32[32,32,128]{2,1,0:T(8,128)}) %reduce-scatter.3.cloned.1.call-update) | async-done | bytes 524304 | tf_op jit(solution)/shard_map/reduce_scatter | solution.py:97
  125.2 4.5 %collective-permute-done.3 = bf16[128,4096]{0,1:T(8,128)(2,1)S(1)} collective-permute-done((bf16[128,4096]{0,1:T(8,128)(2,1)S(1)}, bf16[128,4096]{0,1:T(8,128)(2,1)S(1)}, u32[]{:S(2)}, u32[]{:S(2)}) %collective-permute-start.3) | collective-permute-done | bytes 1048608 | tf_op jit(solution)/shard_map/ppermute | solution.py:13
  129.6 1.3 copy.68
  130.9 19.6 %reduce-scatter.5.cloned.1.call-done = f32[8,32,128]{2,1,0:T(8,128)} async-done(((f32[32,32,128]{2,1,0:T(8,128)}), f32[8,32,128]{2,1,0:T(8,128)}) %reduce-scatter.5.cloned.1.call-update) | async-done | bytes 131088 | tf_op jit(solution)/shard_map/reduce_scatter | solution.py:98
  150.6 0.9 broadcast_multiply_fusion
  151.5 0.7 broadcast_in_dim_reshape.2
  (64 shorter events, 3.3 us)
Async XLA Ops:
  7.2 2.3 %copy-start.3 = (f32[1,4096]{1,0:T(1,128)S(1)}, f32[1,4096]{1,0:T(1,128)}, u32[]{:S(2)}) copy-start(f32[1,4096]{1,0:T(1,128)} %param.9) | copy-start | bytes 49156
  7.2 61.6 %all-gather.2.cloned.1.call-start = ((), (), s32[]{:S(2)}) async-start(), calls=%async_computation.2 | async-start | bytes 2359296 | tf_op jit(solution)/shard_map/all_gather | solution.py:42
  8.8 2.1 %copy-start.2 = (bf16[1,128,1024]{2,1,0:T(8,128)(2,1)S(1)}, bf16[1,128,1024]{2,1,0:T(8,128)(2,1)}, u32[]{:S(2)}) copy-start(bf16[1,128,1024]{2,1,0:T(8,128)(2,1)} %param.8) | copy-start | bytes 786436
  8.9 2.9 %copy-start.4 = (bf16[1,8,4096]{2,1,0:T(8,128)(2,1)S(1)}, bf16[1,8,4096]{2,1,0:T(8,128)(2,1)}, u32[]{:S(2)}) copy-start(bf16[1,8,4096]{2,1,0:T(8,128)(2,1)} %param.10) | copy-start | bytes 196612
  8.9 16.8 %copy-start.7 = (s32[1,64]{1,0:T(1,128)S(1)}, s32[1,64]{1,0:T(1,128)}, u32[]{:S(2)}) copy-start(s32[1,64]{1,0:T(1,128)} %param.12) | copy-start | bytes 772
  8.9 17.0 %copy-start.5 = (s32[1,64,8]{1,2,0:T(8,128)S(1)}, s32[1,64,8]{1,2,0:T(8,128)}, u32[]{:S(2)}) copy-start(s32[1,64,8]{1,2,0:T(8,128)} %param.11) | copy-start | bytes 6148
  9.4 16.6 %copy-start.6 = (s32[1,512]{1,0:T(1,128)S(1)}, s32[1,512]{1,0:T(1,128)}, u32[]{:S(2)}) copy-start(s32[1,512]{1,0:T(1,128)} %param.13) | copy-start | bytes 6148
  11.0 20.2 %collective-permute-start = (bf16[128,4096]{0,1:T(8,128)(2,1)}, bf16[128,4096]{0,1:T(8,128)(2,1)}, u32[]{:S(2)}, u32[]{:S(2)}) collective-permute-start(bf16[128,4096]{0,1:T(8,128)(2,1)} %fusion.11), channel_id=1, source_target_pairs={{0,1},{1,0},{2,3},{3,2},{4,5},{5,4},{6,7},{7,6},{8,9},{9,8},{10,11... | collective-permute-start | bytes 3145736 | tf_op jit(solution)/shard_map/ppermute | solution.py:18
  11.2 15.4 %collective-permute-start.1 = (bf16[128,1024]{0,1:T(8,128)(2,1)S(1)}, bf16[128,1024]{0,1:T(8,128)(2,1)S(1)}, u32[]{:S(2)}, u32[]{:S(2)}) collective-permute-start(bf16[128,1024]{0,1:T(8,128)(2,1)S(1)} %bitcast.88), channel_id=1, source_target_pairs={{0,1},{1,0},{2,3},{3,2},{4,5},{5,4},{6,7},{7,6},{8,9},{9,8},{10,11... | collective-permute-start | bytes 786440 | tf_op jit(solution)/shard_map/ppermute | solution.py:18
  25.1 100.0 %reduce-scatter.3.cloned.1.call-start = ((), (), s32[]{:S(2)}) async-start(), calls=%async_computation.3 | async-start | bytes 4718592 | tf_op jit(solution)/shard_map/reduce_scatter | solution.py:97
  35.2 4.5 %copy-start.1 = (bf16[16,512,128]{1,2,0:T(8,128)(2,1)S(1)}, bf16[16,512,128]{1,2,0:T(8,128)(2,1)}, u32[]{:S(2)}) copy-start(bf16[16,512,128]{1,2,0:T(8,128)(2,1)} %broadcast_in_dim.113) | copy-start | bytes 6291460
  68.8 81.8 %reduce-scatter.5.cloned.1.call-start = ((), (), s32[]{:S(2)}) async-start(), calls=%async_computation.4 | async-start | bytes 655360 | tf_op jit(solution)/shard_map/reduce_scatter | solution.py:98
  68.8 8.2 %collective-permute-start.2 = (bf16[256,32,128]{2,1,0:T(8,128)(2,1)}, bf16[256,32,128]{2,1,0:T(8,128)(2,1)}, u32[]{:S(2)}, u32[]{:S(2)}) collective-permute-start(bf16[256,32,128]{2,1,0:T(8,128)(2,1)} %all-gather.2.cloned.1.call-done), channel_id=1, source_target_pairs={{0,1},{1,0},{2,3},{3,2},{4,5},{5,4},{6,7},{7,6},{8,9},{9,8},{10,11... | collective-permute-start | bytes 6291464 | tf_op jit(solution)/shard_map/ppermute | solution.py:18
  81.6 12.1 %copy-start = (f32[128,64,32,2]{0,3,2,1:T(2,128)S(1)}, f32[128,64,32,2]{0,3,2,1:T(2,128)}, u32[]{:S(2)}) copy-start(f32[128,64,32,2]{0,3,2,1:T(2,128)} %convert.4) | copy-start | bytes 6291460
  102.2 27.4 %collective-permute-start.3 = (bf16[128,4096]{0,1:T(8,128)(2,1)S(1)}, bf16[128,4096]{0,1:T(8,128)(2,1)S(1)}, u32[]{:S(2)}, u32[]{:S(2)}) collective-permute-start(bf16[128,4096]{0,1:T(8,128)(2,1)S(1)} %fusion.14), channel_id=1, source_target_pairs={{64,0},{128,64},{192,128},{65,1},{129,65},{193,129},{66,2},{130,66... | collective-permute-start | bytes 3145736 | tf_op jit(solution)/shard_map/ppermute | solution.py:13
Sparse Core Ops, SparseCore 0:
  25.3 43.4 all-gather.1
  71.3 53.8 reduce-scatter.2
  127.7 22.8 reduce-scatter.4

commit v6 on v5

--- a/solution.py
+++ b/solution.py
@@ -38,16 +38,23 @@
     grad_scale = (tok_rows * nz * nx * nc) ** (-0.5)
 
     own_tiles = tiles[0].reshape(slot_dev, half, lanes)
-    gathered = lax.all_gather(own_tiles, "x", axis=0, tiled=True)
+    gathered = jnp.concatenate(
+        [own_tiles]
+        + [lax.ppermute(own_tiles, "x", [(src, (src + s) % nx) for src in range(nx)]) for s in range(1, nx)],
+        axis=0,
+    )
     gathered = lax.all_gather(gathered, "z", axis=0, tiled=True)
     slot_ids = jnp.arange(store_slots, dtype=jnp.int32)
 
     my_core = lax.axis_index("core")
+    my_x = lax.axis_index("x")
 
     def row_of(slot):
         holder = slot // slot_dev
         half_of = (holder % nc - my_core) % nc
-        return half_of * (nz * nx * slot_dev) + (holder // nc) * slot_dev + slot % slot_dev
+        chip = holder // nc
+        shift = (my_x - chip % nx) % nx
+        return half_of * (nz * nx * slot_dev) + ((chip // nx) * nx + shift) * slot_dev + slot % slot_dev
 
     kept_grid = jnp.arange(most_kept)[None, :] < count_list[:, None]
     col_hit = (column_list[:, :, None] == jnp.arange(ncol)[None, None, :]) & kept_grid[:, :, None]

time: 159 us -> 151 us (0.950)
  blocking collectives: 13.3 us -> 0 us
  starting transfers between devices: 3.45 us -> 9.21 us
  waiting for transfers between devices: 55.2 us -> 53.4 us
    all_gather x1 -> x0, blocking collectives: 13.3 us -> none  [local(): gathered = lax.all_gather(own_tiles, 'x', axis=0, tiled=True)]
    ppermute x0 -> x3, starting transfers between devices: none -> 5.73 us  [local(): lax.ppermute(own_tiles, 'x', [(src, (src + s) % nx) for src in range(nx)])]
    all_gather x1, waiting for transfers between devices: 10.6 us -> 8.51 us  [local(): gathered = lax.all_gather(gathered, 'z', axis=0, tiled=True)]
    unnamed x23 -> x21, local copies, waits for them, and re-layouts: 4.26 us -> 5.09 us
  transfers between devices with their start and end apart: 7 -> 10, of which waited for: 4 -> 5; matrix products, arithmetic and copies ran while one was open for 42% -> 48% of each run, Pallas kernels for 0% -> 0%
where the time goes in v6:
time: 151 us
  waiting for transfers between devices  53.4 us (35%)
  local copies, waits for them, and re-layouts  43.3 us (29%)
  other arithmetic  15.5 us (10%)
  matrix products  15.5 us (10%)
  between operations  14.1 us (9%)
  starting transfers between devices  9.21 us (6%)
    reduce_scatter x1, waiting for transfers between devices, local(): weight_grad = lax.psum_scatter(terms, 'z', scatter_dimension=0, tiled=True)  20.5 us
    reduce_scatter x1, waiting for transfers between devices, local(): lax.psum_scatter(weight_grad, 'x', scatter_dimension=0, tiled=True)  19.7 us
    gather x1, local copies, waits for them, and re-layouts, local(): gathered[dense_rows]  12.1 us
    dot_general x1, matrix products, local(): jnp.dot(normed_pairs.reshape((panel_list + 1) * half, 2 * pair_tokens), e...  9.68 us
    gather x1, local copies, waits for them, and re-layouts, local(): terms = dense_terms[jnp.where(term_kept, term_index, panel_list * ncol)]  8.81 us
    all_gather x1, waiting for transfers between devices, local(): gathered = lax.all_gather(gathered, 'z', axis=0, tiled=True)  8.51 us
    dot_general x1, matrix products, local(): jnp.einsum('cthl,pcrl->tprh', expand, dense_w, preferred_element_type=jnp...  5.83 us
    ppermute x3, starting transfers between devices, local(): lax.ppermute(own_tiles, 'x', [(src, (src + s) % nx) for src in range(nx)])  5.73 us
  transfers between devices with their start and end apart: 10, of which 5 were waited for; matrix products, arithmetic and copies ran while one was open for 48% of the time, Pallas kernels for 0%

profile of v6, /device:TPU:8, one launch (start us, length us, event | category | flops | bytes accessed | tf_op | source)
XLA Modules:
  0.0 151.0 jit_solution(6210568388679695421)
XLA Ops:
  7.2 0.9 copy.77
  8.1 1.6 %collective-permute-start.2 = (bf16[8,32,128]{2,1,0:T(8,128)(2,1)S(1)}, bf16[8,32,128]{2,1,0:T(8,128)(2,1)S(1)}, u32[]{:S(2)}, u32[]{:S(2)}) collective-permute-start(bf16[8,32,128]{2,1,0:T(8,128)(2,1)S(1)} %bitcast.95), channel_id=1, source_target_pairs={{0,2},{2,4},{4,6},{6,0},{1,3},{3,5},{5,7},{7,1},{8,10},{10,12},{12... | collective-permute-start | bytes 196616 | tf_op jit(solution)/shard_map/ppermute | solution.py:43
  9.6 2.7 %collective-permute-start.3 = (bf16[8,32,128]{2,1,0:T(8,128)(2,1)S(1)}, bf16[8,32,128]{2,1,0:T(8,128)(2,1)S(1)}, u32[]{:S(2)}, u32[]{:S(2)}) collective-permute-start(bf16[8,32,128]{2,1,0:T(8,128)(2,1)S(1)} %bitcast.96), channel_id=1, source_target_pairs={{0,4},{2,6},{4,0},{6,2},{1,5},{3,7},{5,1},{7,3},{8,12},{10,14},{12... | collective-permute-start | bytes 196616 | tf_op jit(solution)/shard_map/ppermute | solution.py:43
  12.4 1.4 collective-permute-start.4
  13.8 1.6 %copy.52 = bf16[1,128,4096]{1,2,0:T(8,128)(2,1)S(1)} copy(bf16[1,128,4096]{2,1,0:T(8,128)(2,1)} %param.7) | data formatting | bytes 2097152 | tf_op args[0]
  16.0 1.5 fusion.11
  18.3 0.7 pad_maximum_fusion.4
  21.0 1.7 %broadcast_in_dim.112 = bf16[16,2,256,128]{2,1,3,0:T(2,128)(2,1)S(1)} broadcast(bf16[16,256,128]{1,2,0:T(8,128)(2,1)S(1)} %pad_maximum_fusion.2), dimensions={0,2,3} | broadcast | bytes 3145728 | tf_op jit(solution)/shard_map/jit(_where)/broadcast_in_dim | solution.py:79
  22.7 2.7 %broadcast_in_dim.113 = bf16[16,512,128]{1,2,0:T(8,128)(2,1)} reshape(bf16[16,2,256,128]{2,1,3,0:T(2,128)(2,1)S(1)} %broadcast_in_dim.112) | data formatting | bytes 4194304 | tf_op jit(solution)/shard_map/jit(_where)/broadcast_in_dim | solution.py:79
  25.4 1.8 %pad_maximum_fusion.1 = bf16[256,4096]{0,1:T(8,128)(2,1)S(1)} fusion(bf16[128,4096]{0,1:T(8,128)(2,1)} %collective-permute-done, bf16[128,4096]{0,1:T(8,128)(2,1)} %fusion.11), kind=kLoop, calls=%fused_computation.11 | loop fusion | flops 4194304 | bytes 4194304 | tf_op jit(solution)/shard_map/concatenate | solution.py:69
  27.2 2.3 %reshape.413 = bf16[256,64,32,2]{0,3,2,1:T(2,128)(2,1)} reshape(bf16[256,4096]{0,1:T(8,128)(2,1)S(1)} %pad_maximum_fusion.1) | data formatting | bytes 4194304 | tf_op jit(solution)/shard_map/reshape | solution.py:80
  29.4 4.5 %reshape.414 = bf16[64,32,512]{2,1,0:T(8,128)(2,1)} reshape(bf16[64,32,2,256]{3,2,1,0:T(2,128)(2,1)} %bitcast.87) | data formatting | bytes 4194304 | tf_op jit(solution)/shard_map/reshape | solution.py:81
  34.0 9.7 %fusion.5 = f32[65,32,16,128]{3,1,2,0:T(8,128)} fusion(bf16[64,32,512]{2,1,0:T(8,128)(2,1)} %reshape.414, bf16[16,512,128]{1,2,0:T(8,128)(2,1)S(1)} %copy-done.1, pred[512,128]{0,1:T(8,128)(4,1)S(1)} %copy.55), kind=kOutput, calls=%fused_computation.8 | convolution fusion | flops 4363124736 | bytes 21299200 | tf_op jit(solution)/shard_map/dot_general | solution.py:84
  43.6 8.8 %gather_fusion = f32[256,32,128]{2,1,0:T(8,128)} fusion(f32[1040,32,128]{2,1,0:T(8,128)} %bitcast.92, s32[1024]{0:T(1024)S(1)} %pad_clamp_fusion), kind=kCustom, calls=%fused_computation | custom fusion | bytes 8389632 | tf_op jit(solution)/shard_map/gather | solution.py:101
  52.5 8.5 %all-gather.2.cloned.1.call-done = bf16[256,32,128]{2,1,0:T(8,128)(2,1)} async-done(((bf16[32,32,128]{2,1,0:T(8,128)(2,1)}), bf16[256,32,128]{2,1,0:T(8,128)(2,1)}) %all-gather.2.cloned.1.call-update) | async-done | bytes 2097168 | tf_op jit(solution)/shard_map/all_gather | solution.py:46
  61.9 0.7 reduce.7
  63.0 2.3 %convert.4 = f32[128,64,32,2]{0,3,2,1:T(2,128)} convert(bf16[128,64,32,2]{0,3,2,1:T(2,128)(2,1)S(1)} %bitcast.84) | non-fusion elementwise | flops 524288 | bytes 3145728 | tf_op jit(solution)/shard_map/convert_element_type | solution.py:22
  65.5 1.0 copy.64
  67.0 0.7 reduce.8
  67.7 1.0 mul.153
  69.2 4.6 %pad_maximum_fusion = bf16[512,32,128]{2,1,0:T(8,128)(2,1)} fusion(bf16[256,32,128]{2,1,0:T(8,128)(2,1)} %collective-permute-done.5, bf16[256,32,128]{2,1,0:T(8,128)(2,1)} %all-gather.2.cloned.1.call-done), kind=kLoop, calls=%fused_computation.6 | loop fusion | flops 2097152 | bytes 8388608 | tf_op jit(solution)/shard_map/concatenate | solution.py:103
  73.8 12.1 %gather_fusion.1 = bf16[1024,32,128]{2,1,0:T(8,128)(2,1)} fusion(bf16[512,32,128]{2,1,0:T(8,128)(2,1)} %pad_maximum_fusion, s32[1024]{0:T(1024)S(1)} %broadcast_clamp_fusion), kind=kCustom, calls=%fused_computation.1 | custom fusion | bytes 16781312 | tf_op jit(solution)/shard_map/gather | solution.py:109
  85.9 5.8 %fusion.15 = (f32[128]{0:T(128)S(1)}, f32[128,64,32,2]{0,2,3,1:T(8,128)S(1)}) fusion(f32[128,64,32,2]{0,3,2,1:T(2,128)S(1)} %copy-done, f32[64,32,2]{1,2,0:T(2,128)S(1)} %copy.66, pred[2,128]{1,0:T(4,128)(4,1)S(1)} %iota_compare_fusion.2, bf16[16,128,128]{2,1,0:T(8,128)(2,1)} %copy.64, bf16[64,16,32,128]{3,2,1,0:T(8,128)(2,1)} %bitcast.85, ...), kind=kOutput, calls=%fused_computation.23 | convolution fusion | flops 2153775104 | bytes 13125376 | tf_op jit(solution)/shard_map/cthl,pcrl->tprh/dot_general | solution.py:111
  91.8 1.9 %copy.65 = f32[128,64,32,2]{0,3,2,1:T(2,128)S(1)} copy(f32[128,64,32,2]{0,2,3,1:T(8,128)S(1)} %get-tuple-element.17) | data formatting | bytes 4194304 | tf_op jit(solution)/shard_map/cthl,pcrl->tprh/transpose | solution.py:111
  93.7 0.7 fusion.14
  94.4 2.5 %collective-permute-start.6 = (bf16[128,4096]{0,1:T(8,128)(2,1)S(1)}, bf16[128,4096]{0,1:T(8,128)(2,1)S(1)}, u32[]{:S(2)}, u32[]{:S(2)}) collective-permute-start(bf16[128,4096]{0,1:T(8,128)(2,1)S(1)} %fusion.14), channel_id=1, source_target_pairs={{64,0},{128,64},{192,128},{65,1},{129,65},{193,129},{66,2},{130,66... | collective-permute-start | bytes 3145736 | tf_op jit(solution)/shard_map/ppermute | solution.py:13
  96.9 20.5 %reduce-scatter.3.cloned.1.call-done = f32[32,32,128]{2,1,0:T(8,128)} async-done(((f32[256,32,128]{2,1,0:T(8,128)}), f32[32,32,128]{2,1,0:T(8,128)}) %reduce-scatter.3.cloned.1.call-update) | async-done | bytes 524304 | tf_op jit(solution)/shard_map/reduce_scatter | solution.py:104
  117.5 4.4 %collective-permute-done.6 = bf16[128,4096]{0,1:T(8,128)(2,1)S(1)} collective-permute-done((bf16[128,4096]{0,1:T(8,128)(2,1)S(1)}, bf16[128,4096]{0,1:T(8,128)(2,1)S(1)}, u32[]{:S(2)}, u32[]{:S(2)}) %collective-permute-start.6) | collective-permute-done | bytes 1048608 | tf_op jit(solution)/shard_map/ppermute | solution.py:13
  121.9 1.3 copy.68
  123.2 19.7 %reduce-scatter.5.cloned.1.call-done = f32[8,32,128]{2,1,0:T(8,128)} async-done(((f32[32,32,128]{2,1,0:T(8,128)}), f32[8,32,128]{2,1,0:T(8,128)}) %reduce-scatter.5.cloned.1.call-update) | async-done | bytes 131088 | tf_op jit(solution)/shard_map/reduce_scatter | solution.py:105
  142.8 0.9 broadcast_multiply_fusion
  143.7 0.7 broadcast_in_dim_reshape.2
  (68 shorter events, 5.8 us)
Async XLA Ops:
  7.2 8.9 %copy-start.3 = (f32[1,4096]{1,0:T(1,128)S(1)}, f32[1,4096]{1,0:T(1,128)}, u32[]{:S(2)}) copy-start(f32[1,4096]{1,0:T(1,128)} %param.9) | copy-start | bytes 49156
  7.2 53.8 %all-gather.2.cloned.1.call-start = ((), (), s32[]{:S(2)}) async-start(), calls=%async_computation.2 | async-start | bytes 2359296 | tf_op jit(solution)/shard_map/all_gather | solution.py:46
  8.1 10.2 %collective-permute-start.2 = (bf16[8,32,128]{2,1,0:T(8,128)(2,1)S(1)}, bf16[8,32,128]{2,1,0:T(8,128)(2,1)S(1)}, u32[]{:S(2)}, u32[]{:S(2)}) collective-permute-start(bf16[8,32,128]{2,1,0:T(8,128)(2,1)S(1)} %bitcast.95), channel_id=1, source_target_pairs={{0,2},{2,4},{4,6},{6,0},{1,3},{3,5},{5,7},{7,1},{8,10},{10,12},{12... | collective-permute-start | bytes 196616 | tf_op jit(solution)/shard_map/ppermute | solution.py:43
  9.6 8.7 %collective-permute-start.3 = (bf16[8,32,128]{2,1,0:T(8,128)(2,1)S(1)}, bf16[8,32,128]{2,1,0:T(8,128)(2,1)S(1)}, u32[]{:S(2)}, u32[]{:S(2)}) collective-permute-start(bf16[8,32,128]{2,1,0:T(8,128)(2,1)S(1)} %bitcast.96), channel_id=1, source_target_pairs={{0,4},{2,6},{4,0},{6,2},{1,5},{3,7},{5,1},{7,3},{8,12},{10,14},{12... | collective-permute-start | bytes 196616 | tf_op jit(solution)/shard_map/ppermute | solution.py:43
  12.4 6.0 %collective-permute-start.4 = (bf16[8,32,128]{2,1,0:T(8,128)(2,1)S(1)}, bf16[8,32,128]{2,1,0:T(8,128)(2,1)S(1)}, u32[]{:S(2)}, u32[]{:S(2)}) collective-permute-start(bf16[8,32,128]{2,1,0:T(8,128)(2,1)S(1)} %bitcast.97), channel_id=1, source_target_pairs={{0,6},{2,0},{4,2},{6,4},{1,7},{3,1},{5,3},{7,5},{8,14},{10,8},{12,... | collective-permute-start | bytes 196616 | tf_op jit(solution)/shard_map/ppermute | solution.py:43
  15.4 2.1 %copy-start.2 = (bf16[1,128,1024]{2,1,0:T(8,128)(2,1)S(1)}, bf16[1,128,1024]{2,1,0:T(8,128)(2,1)}, u32[]{:S(2)}) copy-start(bf16[1,128,1024]{2,1,0:T(8,128)(2,1)} %param.8) | copy-start | bytes 786436
  16.0 3.6 %copy-start.6 = (s32[1,64]{1,0:T(1,128)S(1)}, s32[1,64]{1,0:T(1,128)}, u32[]{:S(2)}) copy-start(s32[1,64]{1,0:T(1,128)} %param.12) | copy-start | bytes 772
  16.0 3.8 %copy-start.4 = (s32[1,64,8]{1,2,0:T(8,128)S(1)}, s32[1,64,8]{1,2,0:T(8,128)}, u32[]{:S(2)}) copy-start(s32[1,64,8]{1,2,0:T(8,128)} %param.11) | copy-start | bytes 6148
  16.0 4.0 %copy-start.5 = (s32[1,512]{1,0:T(1,128)S(1)}, s32[1,512]{1,0:T(1,128)}, u32[]{:S(2)}) copy-start(s32[1,512]{1,0:T(1,128)} %param.13) | copy-start | bytes 6148
  17.5 7.9 %collective-permute-start = (bf16[128,4096]{0,1:T(8,128)(2,1)}, bf16[128,4096]{0,1:T(8,128)(2,1)}, u32[]{:S(2)}, u32[]{:S(2)}) collective-permute-start(bf16[128,4096]{0,1:T(8,128)(2,1)} %fusion.11), channel_id=1, source_target_pairs={{0,1},{1,0},{2,3},{3,2},{4,5},{5,4},{6,7},{7,6},{8,9},{9,8},{10,11... | collective-permute-start | bytes 3145736 | tf_op jit(solution)/shard_map/ppermute | solution.py:18
  17.7 3.1 %collective-permute-start.1 = (bf16[128,1024]{0,1:T(8,128)(2,1)S(1)}, bf16[128,1024]{0,1:T(8,128)(2,1)S(1)}, u32[]{:S(2)}, u32[]{:S(2)}) collective-permute-start(bf16[128,1024]{0,1:T(8,128)(2,1)S(1)} %bitcast.88), channel_id=1, source_target_pairs={{0,1},{1,0},{2,3},{3,2},{4,5},{5,4},{6,7},{7,6},{8,9},{9,8},{10,11... | collective-permute-start | bytes 786440 | tf_op jit(solution)/shard_map/ppermute | solution.py:18
  19.1 98.4 %reduce-scatter.3.cloned.1.call-start = ((), (), s32[]{:S(2)}) async-start(), calls=%async_computation.3 | async-start | bytes 4718592 | tf_op jit(solution)/shard_map/reduce_scatter | solution.py:104
  29.4 4.5 %copy-start.1 = (bf16[16,512,128]{1,2,0:T(8,128)(2,1)S(1)}, bf16[16,512,128]{1,2,0:T(8,128)(2,1)}, u32[]{:S(2)}) copy-start(bf16[16,512,128]{1,2,0:T(8,128)(2,1)} %broadcast_in_dim.113) | copy-start | bytes 6291460
  61.0 81.8 %reduce-scatter.5.cloned.1.call-start = ((), (), s32[]{:S(2)}) async-start(), calls=%async_computation.4 | async-start | bytes 655360 | tf_op jit(solution)/shard_map/reduce_scatter | solution.py:105
  61.0 8.2 %collective-permute-start.5 = (bf16[256,32,128]{2,1,0:T(8,128)(2,1)}, bf16[256,32,128]{2,1,0:T(8,128)(2,1)}, u32[]{:S(2)}, u32[]{:S(2)}) collective-permute-start(bf16[256,32,128]{2,1,0:T(8,128)(2,1)} %all-gather.2.cloned.1.call-done), channel_id=1, source_target_pairs={{0,1},{1,0},{2,3},{3,2},{4,5},{5,4},{6,7},{7,6},{8,9},{9,8},{10,11... | collective-permute-start | bytes 6291464 | tf_op jit(solution)/shard_map/ppermute | solution.py:18
  73.8 12.1 %copy-start = (f32[128,64,32,2]{0,3,2,1:T(2,128)S(1)}, f32[128,64,32,2]{0,3,2,1:T(2,128)}, u32[]{:S(2)}) copy-start(f32[128,64,32,2]{0,3,2,1:T(2,128)} %convert.4) | copy-start | bytes 6291460
  94.4 27.4 %collective-permute-start.6 = (bf16[128,4096]{0,1:T(8,128)(2,1)S(1)}, bf16[128,4096]{0,1:T(8,128)(2,1)S(1)}, u32[]{:S(2)}, u32[]{:S(2)}) collective-permute-start(bf16[128,4096]{0,1:T(8,128)(2,1)S(1)} %fusion.14), channel_id=1, source_target_pairs={{64,0},{128,64},{192,128},{65,1},{129,65},{193,129},{66,2},{130,66... | collective-permute-start | bytes 3145736 | tf_op jit(solution)/shard_map/ppermute | solution.py:13
Sparse Core Ops, SparseCore 0:
  19.2 41.7 all-gather.1
  63.5 53.8 reduce-scatter.2
  120.0 22.7 reduce-scatter.4

commit v7 on v6

--- a/solution.py
+++ b/solution.py
@@ -102,7 +102,12 @@
     terms, gathered = lax.optimization_barrier((terms, gathered))
     gathered = jnp.concatenate([gathered, sibling(gathered)], axis=0)
     weight_grad = lax.psum_scatter(terms, "z", scatter_dimension=0, tiled=True)
-    weight_grad = lax.psum_scatter(weight_grad, "x", scatter_dimension=0, tiled=True)
+    x_blocks = weight_grad.reshape(nx, slot_dev, half, lanes)
+    own_sum = lax.dynamic_index_in_dim(x_blocks, my_x, axis=0, keepdims=False)
+    for s in range(1, nx):
+        outgoing = lax.dynamic_index_in_dim(x_blocks, (my_x + s) % nx, axis=0, keepdims=False)
+        own_sum = own_sum + lax.ppermute(outgoing, "x", [(src, (src + s) % nx) for src in range(nx)])
+    weight_grad = own_sum
     weight_grad = (weight_grad * grad_scale).reshape(slot_dev, blk * blk)
 
     dense_w = jnp.where(

time: 151 us -> 137 us (0.907)
  waiting for transfers between devices: 53.4 us -> 32.3 us
  starting transfers between devices: 9.21 us -> 15 us
    reduce_scatter x1 -> x0, waiting for transfers between devices: 19.7 us -> none  [local(): lax.psum_scatter(weight_grad, 'x', scatter_dimension=0, tiled=True)]
    ppermute x0 -> x3, starting transfers between devices: none -> 5.86 us  [local(): lax.ppermute(outgoing, 'x', [(src, (src + s) % nx) for src in range(nx)])]
    ppermute x1, waiting for transfers between devices: 4.37 us -> 0.01 us  [shifted(): lax.ppermute(value, axis, [(source, source + steps) for source in range(l...]
    ppermute x0 -> x3, waiting for transfers between devices: none -> 2.87 us  [local(): lax.ppermute(outgoing, 'x', [(src, (src + s) % nx) for src in range(nx)])]
  transfers between devices with their start and end apart: 10 -> 12, of which waited for: 5 -> 4; matrix products, arithmetic and copies ran while one was open for 48% -> 54% of each run, Pallas kernels for 0% -> 0%
where the time goes in v7:
time: 137 us; the launch traced here: 136 us
  local copies, waits for them, and re-layouts  43.9 us (32%)
  waiting for transfers between devices  32.3 us (24%)
  matrix products  15.5 us (11%)
  other arithmetic  15.3 us (11%)
  starting transfers between devices  15 us (11%)
  between operations  14.4 us (11%)
    reduce_scatter x1, waiting for transfers between devices, local(): weight_grad = lax.psum_scatter(terms, 'z', scatter_dimension=0, tiled=True)  20.5 us
    gather x1, local copies, waits for them, and re-layouts, local(): gathered[dense_rows]  12.1 us
    dot_general x1, matrix products, local(): jnp.dot(normed_pairs.reshape((panel_list + 1) * half, 2 * pair_tokens), e...  9.68 us
    gather x1, local copies, waits for them, and re-layouts, local(): terms = dense_terms[jnp.where(term_kept, term_index, panel_list * ncol)]  8.81 us
    all_gather x1, waiting for transfers between devices, local(): gathered = lax.all_gather(gathered, 'z', axis=0, tiled=True)  8.53 us
    ppermute x3, starting transfers between devices, local(): lax.ppermute(outgoing, 'x', [(src, (src + s) % nx) for src in range(nx)])  5.86 us
    dot_general x1, matrix products, local(): jnp.einsum('cthl,pcrl->tprh', expand, dense_w, preferred_element_type=jnp...  5.83 us
    ppermute x3, starting transfers between devices, local(): lax.ppermute(own_tiles, 'x', [(src, (src + s) % nx) for src in range(nx)])  5.73 us
  transfers between devices with their start and end apart: 12, of which 4 were waited for; matrix products, arithmetic and copies ran while one was open for 54% of the time, Pallas kernels for 0%

profile of v7, /device:TPU:8, one launch (start us, length us, event | category | flops | bytes accessed | tf_op | source)
XLA Modules:
  0.0 136.5 jit_solution(10066175029485640520)
XLA Ops:
  7.2 0.9 copy.104
  8.1 1.6 %collective-permute-start.2 = (bf16[8,32,128]{2,1,0:T(8,128)(2,1)S(1)}, bf16[8,32,128]{2,1,0:T(8,128)(2,1)S(1)}, u32[]{:S(2)}, u32[]{:S(2)}) collective-permute-start(bf16[8,32,128]{2,1,0:T(8,128)(2,1)S(1)} %bitcast.118), channel_id=1, source_target_pairs={{0,2},{2,4},{4,6},{6,0},{1,3},{3,5},{5,7},{7,1},{8,10},{10,12},{12... | collective-permute-start | bytes 196616 | tf_op jit(solution)/shard_map/ppermute | solution.py:43
  9.6 2.7 %collective-permute-start.3 = (bf16[8,32,128]{2,1,0:T(8,128)(2,1)S(1)}, bf16[8,32,128]{2,1,0:T(8,128)(2,1)S(1)}, u32[]{:S(2)}, u32[]{:S(2)}) collective-permute-start(bf16[8,32,128]{2,1,0:T(8,128)(2,1)S(1)} %bitcast.119), channel_id=1, source_target_pairs={{0,4},{2,6},{4,0},{6,2},{1,5},{3,7},{5,1},{7,3},{8,12},{10,14},{12... | collective-permute-start | bytes 196616 | tf_op jit(solution)/shard_map/ppermute | solution.py:43
  12.4 1.4 %collective-permute-start.4 = (bf16[8,32,128]{2,1,0:T(8,128)(2,1)S(1)}, bf16[8,32,128]{2,1,0:T(8,128)(2,1)S(1)}, u32[]{:S(2)}, u32[]{:S(2)}) collective-permute-start(bf16[8,32,128]{2,1,0:T(8,128)(2,1)S(1)} %bitcast.120), channel_id=1, source_target_pairs={{0,6},{2,0},{4,2},{6,4},{1,7},{3,1},{5,3},{7,5},{8,14},{10,8},{12,... | collective-permute-start | bytes 196616 | tf_op jit(solution)/shard_map/ppermute | solution.py:43
  13.8 1.6 %copy.68 = bf16[1,128,4096]{1,2,0:T(8,128)(2,1)S(1)} copy(bf16[1,128,4096]{2,1,0:T(8,128)(2,1)} %param.7) | data formatting | bytes 2097152 | tf_op args[0]
  16.0 1.5 %fusion.11 = bf16[128,4096]{0,1:T(8,128)(2,1)} fusion(bf16[1,128,4096]{1,2,0:T(8,128)(2,1)S(1)} %copy.68, f32[4096]{0:T(1024)S(1)} %bitcast.122, f32[128]{0:T(128)S(1)} %get-tuple-element.19), kind=kLoop, calls=%fused_computation.18 | loop fusion | flops 2097152 | bytes 2114048 | tf_op jit(solution)/shard_map/convert_element_type | solution.py:67
  18.3 0.7 pad_maximum_fusion.4
  21.0 1.7 %broadcast_in_dim.112 = bf16[16,2,256,128]{2,1,3,0:T(2,128)(2,1)S(1)} broadcast(bf16[16,256,128]{1,2,0:T(8,128)(2,1)S(1)} %pad_maximum_fusion.2), dimensions={0,2,3} | broadcast | bytes 3145728 | tf_op jit(solution)/shard_map/jit(_where)/broadcast_in_dim | solution.py:79
  22.7 2.7 %broadcast_in_dim.113 = bf16[16,512,128]{1,2,0:T(8,128)(2,1)} reshape(bf16[16,2,256,128]{2,1,3,0:T(2,128)(2,1)S(1)} %broadcast_in_dim.112) | data formatting | bytes 4194304 | tf_op jit(solution)/shard_map/jit(_where)/broadcast_in_dim | solution.py:79
  25.4 1.8 %pad_maximum_fusion.1 = bf16[256,4096]{0,1:T(8,128)(2,1)S(1)} fusion(bf16[128,4096]{0,1:T(8,128)(2,1)} %collective-permute-done, bf16[128,4096]{0,1:T(8,128)(2,1)} %fusion.11), kind=kLoop, calls=%fused_computation.11 | loop fusion | flops 4194304 | bytes 4194304 | tf_op jit(solution)/shard_map/concatenate | solution.py:69
  27.2 2.3 %reshape.416 = bf16[256,64,32,2]{0,3,2,1:T(2,128)(2,1)} reshape(bf16[256,4096]{0,1:T(8,128)(2,1)S(1)} %pad_maximum_fusion.1) | data formatting | bytes 4194304 | tf_op jit(solution)/shard_map/reshape | solution.py:80
  29.4 4.5 %reshape.417 = bf16[64,32,512]{2,1,0:T(8,128)(2,1)} reshape(bf16[64,32,2,256]{3,2,1,0:T(2,128)(2,1)} %bitcast.109) | data formatting | bytes 4194304 | tf_op jit(solution)/shard_map/reshape | solution.py:81
  34.0 9.7 %fusion.5 = f32[65,32,16,128]{3,1,2,0:T(8,128)} fusion(bf16[64,32,512]{2,1,0:T(8,128)(2,1)} %reshape.417, bf16[16,512,128]{1,2,0:T(8,128)(2,1)S(1)} %copy-done.1, pred[512,128]{0,1:T(8,128)(4,1)S(1)} %copy.71), kind=kOutput, calls=%fused_computation.8 | convolution fusion | flops 4363124736 | bytes 21299200 | tf_op jit(solution)/shard_map/dot_general | solution.py:84
  43.6 8.8 %gather_fusion = f32[256,32,128]{2,1,0:T(8,128)} fusion(f32[1040,32,128]{2,1,0:T(8,128)} %bitcast.114, s32[1024]{0:T(1024)S(1)} %pad_clamp_fusion), kind=kCustom, calls=%fused_computation | custom fusion | bytes 8389632 | tf_op jit(solution)/shard_map/gather | solution.py:101
  52.5 8.5 %all-gather.2.cloned.1.call-done = bf16[256,32,128]{2,1,0:T(8,128)(2,1)} async-done(((bf16[32,32,128]{2,1,0:T(8,128)(2,1)}), bf16[256,32,128]{2,1,0:T(8,128)(2,1)}) %all-gather.2.cloned.1.call-update) | async-done | bytes 2097168 | tf_op jit(solution)/shard_map/all_gather | solution.py:46
  63.0 2.3 %convert.4 = f32[128,64,32,2]{0,3,2,1:T(2,128)} convert(bf16[128,64,32,2]{0,3,2,1:T(2,128)(2,1)S(1)} %bitcast.106) | non-fusion elementwise | flops 524288 | bytes 3145728 | tf_op jit(solution)/shard_map/convert_element_type | solution.py:22
  65.5 1.0 copy.80
  67.7 1.0 mul.153
  69.2 4.6 %pad_maximum_fusion = bf16[512,32,128]{2,1,0:T(8,128)(2,1)} fusion(bf16[256,32,128]{2,1,0:T(8,128)(2,1)} %collective-permute-done.5, bf16[256,32,128]{2,1,0:T(8,128)(2,1)} %all-gather.2.cloned.1.call-done), kind=kLoop, calls=%fused_computation.6 | loop fusion | flops 2097152 | bytes 8388608 | tf_op jit(solution)/shard_map/concatenate | solution.py:103
  73.8 12.1 %gather_fusion.1 = bf16[1024,32,128]{2,1,0:T(8,128)(2,1)} fusion(bf16[512,32,128]{2,1,0:T(8,128)(2,1)} %pad_maximum_fusion, s32[1024]{0:T(1024)S(1)} %broadcast_clamp_fusion), kind=kCustom, calls=%fused_computation.1 | custom fusion | bytes 16781312 | tf_op jit(solution)/shard_map/gather | solution.py:114
  85.9 5.8 %fusion.15 = (f32[128]{0:T(128)S(1)}, f32[128,64,32,2]{0,2,3,1:T(8,128)S(1)}) fusion(f32[128,64,32,2]{0,3,2,1:T(2,128)S(1)} %copy-done, f32[64,32,2]{1,2,0:T(2,128)S(1)} %copy.82, pred[2,128]{1,0:T(4,128)(4,1)S(1)} %iota_compare_fusion.2, bf16[16,128,128]{2,1,0:T(8,128)(2,1)} %copy.80, bf16[64,16,32,128]{3,2,1,0:T(8,128)(2,1)} %bitcast.107, ...), kind=kOutput, calls=%fused_computation.23 | convolution fusion | flops 2153775104 | bytes 13125376 | tf_op jit(solution)/shard_map/cthl,pcrl->tprh/dot_general | solution.py:116
  91.8 1.9 %copy.81 = f32[128,64,32,2]{0,3,2,1:T(2,128)S(1)} copy(f32[128,64,32,2]{0,2,3,1:T(8,128)S(1)} %get-tuple-element.21) | data formatting | bytes 4194304 | tf_op jit(solution)/shard_map/cthl,pcrl->tprh/transpose | solution.py:116
  93.7 0.7 fusion.14
  94.4 2.4 %collective-permute-start.6 = (bf16[128,4096]{0,1:T(8,128)(2,1)S(1)}, bf16[128,4096]{0,1:T(8,128)(2,1)S(1)}, u32[]{:S(2)}, u32[]{:S(2)}) collective-permute-start(bf16[128,4096]{0,1:T(8,128)(2,1)S(1)} %fusion.14), channel_id=1, source_target_pairs={{64,0},{128,64},{192,128},{65,1},{129,65},{193,129},{66,2},{130,66... | collective-permute-start | bytes 3145736 | tf_op jit(solution)/shard_map/ppermute | solution.py:13
  96.9 20.5 %reduce-scatter.2.cloned.1.call-done = f32[32,32,128]{2,1,0:T(8,128)} async-done(((f32[256,32,128]{2,1,0:T(8,128)}), f32[32,32,128]{2,1,0:T(8,128)}) %reduce-scatter.2.cloned.1.call-update) | async-done | bytes 524304 | tf_op jit(solution)/shard_map/reduce_scatter | solution.py:104
  117.4 1.1 constant_dynamic-slice_fusion.2
  118.7 1.6 %collective-permute-start.7 = (f32[8,32,128]{2,0,1:T(8,128)S(1)}, f32[8,32,128]{2,0,1:T(8,128)S(1)}, u32[]{:S(2)}, u32[]{:S(2)}) collective-permute-start(f32[8,32,128]{2,0,1:T(8,128)S(1)} %bitcast.124), channel_id=1, source_target_pairs={{0,2},{2,4},{4,6},{6,0},{1,3},{3,5},{5,7},{7,1},{8,10},{10,12},{12... | collective-permute-start | bytes 393224 | tf_op jit(solution)/shard_map/ppermute | solution.py:109
  120.3 2.8 %collective-permute-start.8 = (f32[8,32,128]{2,0,1:T(8,128)S(1)}, f32[8,32,128]{2,0,1:T(8,128)S(1)}, u32[]{:S(2)}, u32[]{:S(2)}) collective-permute-start(f32[8,32,128]{2,0,1:T(8,128)S(1)} %bitcast.125), channel_id=1, source_target_pairs={{0,4},{2,6},{4,0},{6,2},{1,5},{3,7},{5,1},{7,3},{8,12},{10,14},{12... | collective-permute-start | bytes 393224 | tf_op jit(solution)/shard_map/ppermute | solution.py:109
  123.2 1.5 %collective-permute-start.9 = (f32[8,32,128]{2,0,1:T(8,128)S(1)}, f32[8,32,128]{2,0,1:T(8,128)S(1)}, u32[]{:S(2)}, u32[]{:S(2)}) collective-permute-start(f32[8,32,128]{2,0,1:T(8,128)S(1)} %bitcast.126), channel_id=1, source_target_pairs={{0,6},{2,0},{4,2},{6,4},{1,7},{3,1},{5,3},{7,5},{8,14},{10,8},{12,... | collective-permute-start | bytes 393224 | tf_op jit(solution)/shard_map/ppermute | solution.py:109
  124.7 1.3 copy.88
  126.0 2.9 %collective-permute-done.8 = f32[8,32,128]{2,0,1:T(8,128)S(1)} collective-permute-done((f32[8,32,128]{2,0,1:T(8,128)S(1)}, f32[8,32,128]{2,0,1:T(8,128)S(1)}, u32[]{:S(2)}, u32[]{:S(2)}) %collective-permute-start.8) | collective-permute-done | bytes 131104 | tf_op jit(solution)/shard_map/ppermute | solution.py:109
  128.9 0.8 fusion.32
  (74 shorter events, 7.3 us)
Async XLA Ops:
  7.2 8.9 %copy-start.3 = (f32[1,4096]{1,0:T(1,128)S(1)}, f32[1,4096]{1,0:T(1,128)}, u32[]{:S(2)}) copy-start(f32[1,4096]{1,0:T(1,128)} %param.9) | copy-start | bytes 49156
  7.2 53.8 %all-gather.2.cloned.1.call-start = ((), (), s32[]{:S(2)}) async-start(), calls=%async_computation.1 | async-start | bytes 2359296 | tf_op jit(solution)/shard_map/all_gather | solution.py:46
  8.1 10.2 %collective-permute-start.2 = (bf16[8,32,128]{2,1,0:T(8,128)(2,1)S(1)}, bf16[8,32,128]{2,1,0:T(8,128)(2,1)S(1)}, u32[]{:S(2)}, u32[]{:S(2)}) collective-permute-start(bf16[8,32,128]{2,1,0:T(8,128)(2,1)S(1)} %bitcast.118), channel_id=1, source_target_pairs={{0,2},{2,4},{4,6},{6,0},{1,3},{3,5},{5,7},{7,1},{8,10},{10,12},{12... | collective-permute-start | bytes 196616 | tf_op jit(solution)/shard_map/ppermute | solution.py:43
  9.6 8.7 %collective-permute-start.3 = (bf16[8,32,128]{2,1,0:T(8,128)(2,1)S(1)}, bf16[8,32,128]{2,1,0:T(8,128)(2,1)S(1)}, u32[]{:S(2)}, u32[]{:S(2)}) collective-permute-start(bf16[8,32,128]{2,1,0:T(8,128)(2,1)S(1)} %bitcast.119), channel_id=1, source_target_pairs={{0,4},{2,6},{4,0},{6,2},{1,5},{3,7},{5,1},{7,3},{8,12},{10,14},{12... | collective-permute-start | bytes 196616 | tf_op jit(solution)/shard_map/ppermute | solution.py:43
  12.4 6.0 %collective-permute-start.4 = (bf16[8,32,128]{2,1,0:T(8,128)(2,1)S(1)}, bf16[8,32,128]{2,1,0:T(8,128)(2,1)S(1)}, u32[]{:S(2)}, u32[]{:S(2)}) collective-permute-start(bf16[8,32,128]{2,1,0:T(8,128)(2,1)S(1)} %bitcast.120), channel_id=1, source_target_pairs={{0,6},{2,0},{4,2},{6,4},{1,7},{3,1},{5,3},{7,5},{8,14},{10,8},{12,... | collective-permute-start | bytes 196616 | tf_op jit(solution)/shard_map/ppermute | solution.py:43
  15.4 2.1 %copy-start.2 = (bf16[1,128,1024]{2,1,0:T(8,128)(2,1)S(1)}, bf16[1,128,1024]{2,1,0:T(8,128)(2,1)}, u32[]{:S(2)}) copy-start(bf16[1,128,1024]{2,1,0:T(8,128)(2,1)} %param.8) | copy-start | bytes 786436
  16.0 3.6 %copy-start.6 = (s32[1,64]{1,0:T(1,128)S(1)}, s32[1,64]{1,0:T(1,128)}, u32[]{:S(2)}) copy-start(s32[1,64]{1,0:T(1,128)} %param.12) | copy-start | bytes 772
  16.0 3.8 %copy-start.4 = (s32[1,64,8]{1,2,0:T(8,128)S(1)}, s32[1,64,8]{1,2,0:T(8,128)}, u32[]{:S(2)}) copy-start(s32[1,64,8]{1,2,0:T(8,128)} %param.11) | copy-start | bytes 6148
  16.0 4.0 %copy-start.5 = (s32[1,512]{1,0:T(1,128)S(1)}, s32[1,512]{1,0:T(1,128)}, u32[]{:S(2)}) copy-start(s32[1,512]{1,0:T(1,128)} %param.13) | copy-start | bytes 6148
  17.5 7.8 %collective-permute-start = (bf16[128,4096]{0,1:T(8,128)(2,1)}, bf16[128,4096]{0,1:T(8,128)(2,1)}, u32[]{:S(2)}, u32[]{:S(2)}) collective-permute-start(bf16[128,4096]{0,1:T(8,128)(2,1)} %fusion.11), channel_id=1, source_target_pairs={{0,1},{1,0},{2,3},{3,2},{4,5},{5,4},{6,7},{7,6},{8,9},{9,8},{10,11... | collective-permute-start | bytes 3145736 | tf_op jit(solution)/shard_map/ppermute | solution.py:18
  17.7 3.1 %collective-permute-start.1 = (bf16[128,1024]{0,1:T(8,128)(2,1)S(1)}, bf16[128,1024]{0,1:T(8,128)(2,1)S(1)}, u32[]{:S(2)}, u32[]{:S(2)}) collective-permute-start(bf16[128,1024]{0,1:T(8,128)(2,1)S(1)} %bitcast.110), channel_id=1, source_target_pairs={{0,1},{1,0},{2,3},{3,2},{4,5},{5,4},{6,7},{7,6},{8,9},{9,8},{10,11... | collective-permute-start | bytes 786440 | tf_op jit(solution)/shard_map/ppermute | solution.py:18
  19.1 98.3 %reduce-scatter.2.cloned.1.call-start = ((), (), s32[]{:S(2)}) async-start(), calls=%async_computation.2 | async-start | bytes 4718592 | tf_op jit(solution)/shard_map/reduce_scatter | solution.py:104
  29.4 4.5 %copy-start.1 = (bf16[16,512,128]{1,2,0:T(8,128)(2,1)S(1)}, bf16[16,512,128]{1,2,0:T(8,128)(2,1)}, u32[]{:S(2)}) copy-start(bf16[16,512,128]{1,2,0:T(8,128)(2,1)} %broadcast_in_dim.113) | copy-start | bytes 6291460
  61.0 8.2 %collective-permute-start.5 = (bf16[256,32,128]{2,1,0:T(8,128)(2,1)}, bf16[256,32,128]{2,1,0:T(8,128)(2,1)}, u32[]{:S(2)}, u32[]{:S(2)}) collective-permute-start(bf16[256,32,128]{2,1,0:T(8,128)(2,1)} %all-gather.2.cloned.1.call-done), channel_id=1, source_target_pairs={{0,1},{1,0},{2,3},{3,2},{4,5},{5,4},{6,7},{7,6},{8,9},{9,8},{10,11... | collective-permute-start | bytes 6291464 | tf_op jit(solution)/shard_map/ppermute | solution.py:18
  73.8 12.1 %copy-start = (f32[128,64,32,2]{0,3,2,1:T(2,128)S(1)}, f32[128,64,32,2]{0,3,2,1:T(2,128)}, u32[]{:S(2)}) copy-start(f32[128,64,32,2]{0,3,2,1:T(2,128)} %convert.4) | copy-start | bytes 6291460
  94.4 30.3 %collective-permute-start.6 = (bf16[128,4096]{0,1:T(8,128)(2,1)S(1)}, bf16[128,4096]{0,1:T(8,128)(2,1)S(1)}, u32[]{:S(2)}, u32[]{:S(2)}) collective-permute-start(bf16[128,4096]{0,1:T(8,128)(2,1)S(1)} %fusion.14), channel_id=1, source_target_pairs={{64,0},{128,64},{192,128},{65,1},{129,65},{193,129},{66,2},{130,66... | collective-permute-start | bytes 3145736 | tf_op jit(solution)/shard_map/ppermute | solution.py:13
  118.7 7.3 %collective-permute-start.7 = (f32[8,32,128]{2,0,1:T(8,128)S(1)}, f32[8,32,128]{2,0,1:T(8,128)S(1)}, u32[]{:S(2)}, u32[]{:S(2)}) collective-permute-start(f32[8,32,128]{2,0,1:T(8,128)S(1)} %bitcast.124), channel_id=1, source_target_pairs={{0,2},{2,4},{4,6},{6,0},{1,3},{3,5},{5,7},{7,1},{8,10},{10,12},{12... | collective-permute-start | bytes 393224 | tf_op jit(solution)/shard_map/ppermute | solution.py:109
  120.3 8.6 %collective-permute-start.8 = (f32[8,32,128]{2,0,1:T(8,128)S(1)}, f32[8,32,128]{2,0,1:T(8,128)S(1)}, u32[]{:S(2)}, u32[]{:S(2)}) collective-permute-start(f32[8,32,128]{2,0,1:T(8,128)S(1)} %bitcast.125), channel_id=1, source_target_pairs={{0,4},{2,6},{4,0},{6,2},{1,5},{3,7},{5,1},{7,3},{8,12},{10,14},{12... | collective-permute-start | bytes 393224 | tf_op jit(solution)/shard_map/ppermute | solution.py:109
  123.2 5.7 %collective-permute-start.9 = (f32[8,32,128]{2,0,1:T(8,128)S(1)}, f32[8,32,128]{2,0,1:T(8,128)S(1)}, u32[]{:S(2)}, u32[]{:S(2)}) collective-permute-start(f32[8,32,128]{2,0,1:T(8,128)S(1)} %bitcast.126), channel_id=1, source_target_pairs={{0,6},{2,0},{4,2},{6,4},{1,7},{3,1},{5,3},{7,5},{8,14},{10,8},{12,... | collective-permute-start | bytes 393224 | tf_op jit(solution)/shard_map/ppermute | solution.py:109
Sparse Core Ops, SparseCore 0:
  19.2 41.7 all-gather.1
  63.5 53.8 reduce-scatter.1

commit v8 on v7

--- a/solution.py
+++ b/solution.py
@@ -88,8 +88,8 @@
     )
     dense_terms = dense_terms.reshape(panel_list + 1, half, ncol, lanes).transpose(0, 2, 1, 3)
     dense_terms = dense_terms.reshape((panel_list + 1) * ncol, half, lanes)
-    oz = jnp.arange(nz)[:, None, None]
-    ox = jnp.arange(nx)[None, :, None]
+    ox = jnp.arange(nx)[:, None, None]
+    oz = jnp.arange(nz)[None, :, None]
     oj = jnp.arange(slot_dev)[None, None, :]
     rs_order = (((oz * nx + ox) * nc + my_core) * slot_dev + oj).reshape(-1)
     slot_match = slot_lookup[None, :] == rs_order[:, None]
@@ -101,13 +101,12 @@
     terms = dense_terms[jnp.where(term_kept, term_index, panel_list * ncol)]
     terms, gathered = lax.optimization_barrier((terms, gathered))
     gathered = jnp.concatenate([gathered, sibling(gathered)], axis=0)
-    weight_grad = lax.psum_scatter(terms, "z", scatter_dimension=0, tiled=True)
-    x_blocks = weight_grad.reshape(nx, slot_dev, half, lanes)
+    x_blocks = terms.reshape(nx, nz * slot_dev, half, lanes)
     own_sum = lax.dynamic_index_in_dim(x_blocks, my_x, axis=0, keepdims=False)
     for s in range(1, nx):
         outgoing = lax.dynamic_index_in_dim(x_blocks, (my_x + s) % nx, axis=0, keepdims=False)
         own_sum = own_sum + lax.ppermute(outgoing, "x", [(src, (src + s) % nx) for src in range(nx)])
-    weight_grad = own_sum
+    weight_grad = lax.psum_scatter(own_sum, "z", scatter_dimension=0, tiled=True)
     weight_grad = (weight_grad * grad_scale).reshape(slot_dev, blk * blk)
 
     dense_w = jnp.where(

time: 137 us -> 184 us (1.34)
  waiting for transfers between devices: 32.3 us -> 68 us
  local copies, waits for them, and re-layouts: 43.9 us -> 49.9 us
  other arithmetic: 15.3 us -> 19.6 us
    ppermute x3, waiting for transfers between devices: 2.87 us -> 35.2 us  [local(): lax.ppermute(outgoing, 'x', [(src, (src + s) % nx) for src in range(nx)])]
    ppermute x1, waiting for transfers between devices: 0.01 us -> 23.9 us  [shifted(): lax.ppermute(value, axis, [(source, source + steps) for source in range(l...]
    reduce_scatter x1, waiting for transfers between devices: 20.5 us -> 0.01 us  [local(): lax.psum_scatter(own_sum, 'z', scatter_dimension=0, tiled=True)]
    dynamic_slice x3, local copies, waits for them, and re-layouts: 0.24 us -> 4.78 us  [local(): lax.dynamic_index_in_dim(x_blocks, (my_x + s) % nx, axis=0, keepdims=False)]
    add x0 -> x1, other arithmetic: none -> 3.62 us  [local(): own_sum + lax.ppermute(outgoing, 'x', [(src, (src + s) % nx) for src in r...]
  transfers between devices with their start and end apart: 12 -> 12, of which waited for: 4 -> 6; matrix products, arithmetic and copies ran while one was open for 54% -> 45% of each run, Pallas kernels for 0% -> 0%
where the time goes in v8:
time: 184 us; the launch traced here: 182 us
  waiting for transfers between devices  68 us (37%)
  local copies, waits for them, and re-layouts  49.9 us (27%)
  other arithmetic  19.6 us (11%)
  matrix products  15.5 us (8%)
  starting transfers between devices  14.5 us (8%)
  between operations  14.4 us (8%)
    ppermute x3, waiting for transfers between devices, local(): lax.ppermute(outgoing, 'x', [(src, (src + s) % nx) for src in range(nx)])  35.2 us
    ppermute x1, waiting for transfers between devices, shifted(): lax.ppermute(value, axis, [(source, source + steps) for source in range(l...  23.9 us
    gather x1, local copies, waits for them, and re-layouts, local(): gathered[dense_rows]  12.2 us
    dot_general x1, matrix products, local(): jnp.dot(normed_pairs.reshape((panel_list + 1) * half, 2 * pair_tokens), e...  9.73 us
    gather x1, local copies, waits for them, and re-layouts, local(): terms = dense_terms[jnp.where(term_kept, term_index, panel_list * ncol)]  8.72 us
    all_gather x1, waiting for transfers between devices, local(): gathered = lax.all_gather(gathered, 'z', axis=0, tiled=True)  8.54 us
    dot_general x1, matrix products, local(): jnp.einsum('cthl,pcrl->tprh', expand, dense_w, preferred_element_type=jnp...  5.75 us
    ppermute x3, starting transfers between devices, local(): lax.ppermute(own_tiles, 'x', [(src, (src + s) % nx) for src in range(nx)])  5.73 us
  transfers between devices with their start and end apart: 12, of which 6 were waited for; matrix products, arithmetic and copies ran while one was open for 45% of the time, Pallas kernels for 0%

profile of v8, /device:TPU:8, one launch (start us, length us, event | category | flops | bytes accessed | tf_op | source)
XLA Modules:
  0.0 181.9 jit_solution(2455355354036071851)
XLA Ops:
  8.1 1.6 collective-permute-start.2
  9.6 2.7 %collective-permute-start.3 = (bf16[8,32,128]{2,1,0:T(8,128)(2,1)S(1)}, bf16[8,32,128]{2,1,0:T(8,128)(2,1)S(1)}, u32[]{:S(2)}, u32[]{:S(2)}) collective-permute-start(bf16[8,32,128]{2,1,0:T(8,128)(2,1)S(1)} %bitcast.115), channel_id=1, source_target_pairs={{0,4},{2,6},{4,0},{6,2},{1,5},{3,7},{5,1},{7,3},{8,12},{10,14},{12... | collective-permute-start | bytes 196616 | tf_op jit(solution)/shard_map/ppermute | solution.py:43
  12.4 1.4 collective-permute-start.4
  13.8 1.6 copy.68
  16.0 1.5 fusion.11
  21.0 1.7 broadcast_in_dim.112
  22.7 2.6 %broadcast_in_dim.113 = bf16[16,512,128]{1,2,0:T(8,128)(2,1)} reshape(bf16[16,2,256,128]{2,1,3,0:T(2,128)(2,1)S(1)} %broadcast_in_dim.112) | data formatting | bytes 4194304 | tf_op jit(solution)/shard_map/jit(_where)/broadcast_in_dim | solution.py:79
  25.4 1.8 pad_maximum_fusion.1
  27.2 2.2 %reshape.415 = bf16[256,64,32,2]{0,3,2,1:T(2,128)(2,1)} reshape(bf16[256,4096]{0,1:T(8,128)(2,1)S(1)} %pad_maximum_fusion.1) | data formatting | bytes 4194304 | tf_op jit(solution)/shard_map/reshape | solution.py:80
  29.4 4.5 %reshape.416 = bf16[64,32,512]{2,1,0:T(8,128)(2,1)} reshape(bf16[64,32,2,256]{3,2,1,0:T(2,128)(2,1)} %bitcast.106) | data formatting | bytes 4194304 | tf_op jit(solution)/shard_map/reshape | solution.py:81
  33.9 9.7 %fusion.5 = f32[65,32,16,128]{3,1,2,0:T(8,128)} fusion(bf16[64,32,512]{2,1,0:T(8,128)(2,1)} %reshape.416, bf16[16,512,128]{1,2,0:T(8,128)(2,1)S(1)} %copy-done.1, pred[512,128]{0,1:T(8,128)(4,1)S(1)} %copy.71), kind=kOutput, calls=%fused_computation.8 | convolution fusion | flops 4363124736 | bytes 21299200 | tf_op jit(solution)/shard_map/dot_general | solution.py:84
  43.6 8.7 %gather_fusion = f32[256,32,128]{2,1,0:T(8,128)} fusion(f32[1040,32,128]{2,1,0:T(8,128)} %bitcast.111, s32[1024]{0:T(1024)S(1)} %pad_clamp_fusion), kind=kCustom, calls=%fused_computation | custom fusion | bytes 8389632 | tf_op jit(solution)/shard_map/gather | solution.py:101
  52.4 8.5 %all-gather.2.cloned.1.call-done = bf16[256,32,128]{2,1,0:T(8,128)(2,1)} async-done(((bf16[32,32,128]{2,1,0:T(8,128)(2,1)}), bf16[256,32,128]{2,1,0:T(8,128)(2,1)}) %all-gather.2.cloned.1.call-update) | async-done | bytes 2097168 | tf_op jit(solution)/shard_map/all_gather | solution.py:46
  60.9 2.6 %constant_dynamic-slice_fusion.2 = (f32[1,64,32,128]{3,2,1,0:T(8,128)S(1)}, f32[1,64,32,128]{3,2,1,0:T(8,128)S(1)}, f32[1,64,32,128]{3,2,1,0:T(8,128)S(1)}, f32[1,64,32,128]{3,2,1,0:T(8,128)S(1)}) fusion(f32[4,64,32,128]{3,2,1,0:T(8,128)} %bitcast.103, s32[]{:T(128)S(6)} %select_n.190, s32[]{:T(128)S(6)} %select_n.196, s32[]{:T(128)S(6)} %select_n.194, ...), kind=kLoop, calls=%fused_computation.111 | loop fusion | bytes 8388624 | tf_op jit(solution)/shard_map/jit(dynamic_index_in_dim)/dynamic_slice | solution.py:105
  63.5 1.6 copy.103
  65.1 1.5 collective-permute-start.7
  66.6 1.6 copy.102
  68.2 2.7 %collective-permute-start.8 = (f32[64,32,128]{2,0,1:T(8,128)}, f32[64,32,128]{2,0,1:T(8,128)}, u32[]{:S(2)}, u32[]{:S(2)}) collective-permute-start(f32[64,32,128]{2,0,1:T(8,128)} %bitcast.99), channel_id=1, source_target_pairs={{0,4},{2,6},{4,0},{6,2},{1,5},{3,7},{5,1},{7,3},{8,12},{10,14},{12... | collective-permute-start | bytes 3145736 | tf_op jit(solution)/shard_map/ppermute | solution.py:108
  70.9 1.6 copy.101
  72.5 1.4 collective-permute-start.9
  75.6 2.2 %convert.4 = f32[128,64,32,2]{0,3,2,1:T(2,128)} convert(bf16[128,64,32,2]{0,3,2,1:T(2,128)(2,1)S(1)} %bitcast.102) | non-fusion elementwise | flops 524288 | bytes 3145728 | tf_op jit(solution)/shard_map/convert_element_type | solution.py:22
  81.8 10.5 %collective-permute-done.7 = f32[64,32,128]{2,0,1:T(8,128)} collective-permute-done((f32[64,32,128]{2,0,1:T(8,128)}, f32[64,32,128]{2,0,1:T(8,128)}, u32[]{:S(2)}, u32[]{:S(2)}) %collective-permute-start.7) | collective-permute-done | bytes 1048608 | tf_op jit(solution)/shard_map/ppermute | solution.py:108
  92.2 23.4 %collective-permute-done.8 = f32[64,32,128]{2,0,1:T(8,128)} collective-permute-done((f32[64,32,128]{2,0,1:T(8,128)}, f32[64,32,128]{2,0,1:T(8,128)}, u32[]{:S(2)}, u32[]{:S(2)}) %collective-permute-start.8) | collective-permute-done | bytes 1048608 | tf_op jit(solution)/shard_map/ppermute | solution.py:108
  115.6 1.3 collective-permute-done.9
  116.9 3.6 %fusion.22 = f32[64,32,128]{2,0,1:T(8,128)} fusion(f32[64,32,128]{2,0,1:T(8,128)} %collective-permute-done.9, f32[64,32,128]{2,0,1:T(8,128)} %collective-permute-done.8, f32[64,32,128]{2,0,1:T(8,128)} %collective-permute-done.7, f32[1,64,32,128]{3,2,1,0:T(8,128)S(1)} %get-tuple-element.14), kind=kLoop, calls=%fused_computation.30 | loop fusion | flops 786432 | bytes 5242880 | tf_op jit(solution)/shard_map/add | solution.py:108
  120.6 4.6 %pad_maximum_fusion = bf16[512,32,128]{2,1,0:T(8,128)(2,1)} fusion(bf16[256,32,128]{2,1,0:T(8,128)(2,1)} %collective-permute-done.5, bf16[256,32,128]{2,1,0:T(8,128)(2,1)} %all-gather.2.cloned.1.call-done), kind=kLoop, calls=%fused_computation.6 | loop fusion | flops 2097152 | bytes 8388608 | tf_op jit(solution)/shard_map/concatenate | solution.py:103
  125.1 12.2 %gather_fusion.1 = bf16[1024,32,128]{2,1,0:T(8,128)(2,1)} fusion(bf16[512,32,128]{2,1,0:T(8,128)(2,1)} %pad_maximum_fusion, s32[1024]{0:T(1024)S(1)} %broadcast_clamp_fusion), kind=kCustom, calls=%fused_computation.1 | custom fusion | bytes 16781312 | tf_op jit(solution)/shard_map/gather | solution.py:113
  137.4 5.8 %fusion.15 = (f32[128]{0:T(128)S(1)}, f32[128,64,32,2]{0,2,3,1:T(8,128)S(1)}) fusion(f32[128,64,32,2]{0,3,2,1:T(2,128)S(1)} %copy-done, f32[64,32,2]{1,2,0:T(2,128)S(1)} %copy.82, pred[2,128]{1,0:T(4,128)(4,1)S(1)} %iota_compare_fusion.2, bf16[16,128,128]{2,1,0:T(8,128)(2,1)} %copy.80, bf16[64,16,32,128]{3,2,1,0:T(8,128)(2,1)} %bitcast.104, ...), kind=kOutput, calls=%fused_computation.23 | convolution fusion | flops 2153775104 | bytes 13125376 | tf_op jit(solution)/shard_map/cthl,pcrl->tprh/dot_general | solution.py:115
  143.1 1.9 %copy.81 = f32[128,64,32,2]{0,3,2,1:T(2,128)S(1)} copy(f32[128,64,32,2]{0,2,3,1:T(8,128)S(1)} %get-tuple-element.21) | data formatting | bytes 4194304 | tf_op jit(solution)/shard_map/cthl,pcrl->tprh/transpose | solution.py:115
  145.8 2.5 %collective-permute-start.6 = (bf16[128,4096]{0,1:T(8,128)(2,1)S(1)}, bf16[128,4096]{0,1:T(8,128)(2,1)S(1)}, u32[]{:S(2)}, u32[]{:S(2)}) collective-permute-start(bf16[128,4096]{0,1:T(8,128)(2,1)S(1)} %fusion.14), channel_id=1, source_target_pairs={{64,0},{128,64},{192,128},{65,1},{129,65},{193,129},{66,2},{130,66... | collective-permute-start | bytes 3145736 | tf_op jit(solution)/shard_map/ppermute | solution.py:13
  148.3 23.9 %collective-permute-done.6 = bf16[128,4096]{0,1:T(8,128)(2,1)S(1)} collective-permute-done((bf16[128,4096]{0,1:T(8,128)(2,1)S(1)}, bf16[128,4096]{0,1:T(8,128)(2,1)S(1)}, u32[]{:S(2)}, u32[]{:S(2)}) %collective-permute-start.6) | collective-permute-done | bytes 1048608 | tf_op jit(solution)/shard_map/ppermute | solution.py:13
  173.5 1.6 multiply_bitcast_fusion
  (75 shorter events, 12.4 us)
Async XLA Ops:
  7.2 8.9 %copy-start.3 = (f32[1,4096]{1,0:T(1,128)S(1)}, f32[1,4096]{1,0:T(1,128)}, u32[]{:S(2)}) copy-start(f32[1,4096]{1,0:T(1,128)} %param.9) | copy-start | bytes 49156
  7.2 53.7 %all-gather.2.cloned.1.call-start = ((), (), s32[]{:S(2)}) async-start(), calls=%async_computation.1 | async-start | bytes 2359296 | tf_op jit(solution)/shard_map/all_gather | solution.py:46
  8.1 10.2 %collective-permute-start.2 = (bf16[8,32,128]{2,1,0:T(8,128)(2,1)S(1)}, bf16[8,32,128]{2,1,0:T(8,128)(2,1)S(1)}, u32[]{:S(2)}, u32[]{:S(2)}) collective-permute-start(bf16[8,32,128]{2,1,0:T(8,128)(2,1)S(1)} %bitcast.114), channel_id=1, source_target_pairs={{0,2},{2,4},{4,6},{6,0},{1,3},{3,5},{5,7},{7,1},{8,10},{10,12},{12... | collective-permute-start | bytes 196616 | tf_op jit(solution)/shard_map/ppermute | solution.py:43
  9.6 8.7 %collective-permute-start.3 = (bf16[8,32,128]{2,1,0:T(8,128)(2,1)S(1)}, bf16[8,32,128]{2,1,0:T(8,128)(2,1)S(1)}, u32[]{:S(2)}, u32[]{:S(2)}) collective-permute-start(bf16[8,32,128]{2,1,0:T(8,128)(2,1)S(1)} %bitcast.115), channel_id=1, source_target_pairs={{0,4},{2,6},{4,0},{6,2},{1,5},{3,7},{5,1},{7,3},{8,12},{10,14},{12... | collective-permute-start | bytes 196616 | tf_op jit(solution)/shard_map/ppermute | solution.py:43
  12.4 6.0 %collective-permute-start.4 = (bf16[8,32,128]{2,1,0:T(8,128)(2,1)S(1)}, bf16[8,32,128]{2,1,0:T(8,128)(2,1)S(1)}, u32[]{:S(2)}, u32[]{:S(2)}) collective-permute-start(bf16[8,32,128]{2,1,0:T(8,128)(2,1)S(1)} %bitcast.116), channel_id=1, source_target_pairs={{0,6},{2,0},{4,2},{6,4},{1,7},{3,1},{5,3},{7,5},{8,14},{10,8},{12,... | collective-permute-start | bytes 196616 | tf_op jit(solution)/shard_map/ppermute | solution.py:43
  15.4 2.1 %copy-start.2 = (bf16[1,128,1024]{2,1,0:T(8,128)(2,1)S(1)}, bf16[1,128,1024]{2,1,0:T(8,128)(2,1)}, u32[]{:S(2)}) copy-start(bf16[1,128,1024]{2,1,0:T(8,128)(2,1)} %param.8) | copy-start | bytes 786436
  16.0 3.5 %copy-start.6 = (s32[1,64]{1,0:T(1,128)S(1)}, s32[1,64]{1,0:T(1,128)}, u32[]{:S(2)}) copy-start(s32[1,64]{1,0:T(1,128)} %param.12) | copy-start | bytes 772
  16.0 3.7 %copy-start.4 = (s32[1,64,8]{1,2,0:T(8,128)S(1)}, s32[1,64,8]{1,2,0:T(8,128)}, u32[]{:S(2)}) copy-start(s32[1,64,8]{1,2,0:T(8,128)} %param.11) | copy-start | bytes 6148
  16.0 3.9 %copy-start.5 = (s32[1,512]{1,0:T(1,128)S(1)}, s32[1,512]{1,0:T(1,128)}, u32[]{:S(2)}) copy-start(s32[1,512]{1,0:T(1,128)} %param.13) | copy-start | bytes 6148
  17.5 7.8 %collective-permute-start = (bf16[128,4096]{0,1:T(8,128)(2,1)}, bf16[128,4096]{0,1:T(8,128)(2,1)}, u32[]{:S(2)}, u32[]{:S(2)}) collective-permute-start(bf16[128,4096]{0,1:T(8,128)(2,1)} %fusion.11), channel_id=1, source_target_pairs={{0,1},{1,0},{2,3},{3,2},{4,5},{5,4},{6,7},{7,6},{8,9},{9,8},{10,11... | collective-permute-start | bytes 3145736 | tf_op jit(solution)/shard_map/ppermute | solution.py:18
  17.7 3.1 %collective-permute-start.1 = (bf16[128,1024]{0,1:T(8,128)(2,1)S(1)}, bf16[128,1024]{0,1:T(8,128)(2,1)S(1)}, u32[]{:S(2)}, u32[]{:S(2)}) collective-permute-start(bf16[128,1024]{0,1:T(8,128)(2,1)S(1)} %bitcast.107), channel_id=1, source_target_pairs={{0,1},{1,0},{2,3},{3,2},{4,5},{5,4},{6,7},{7,6},{8,9},{9,8},{10,11... | collective-permute-start | bytes 786440 | tf_op jit(solution)/shard_map/ppermute | solution.py:18
  19.1 154.4 %reduce-scatter.2.cloned.1.call-start = ((), (), s32[]{:S(2)}) async-start(), calls=%async_computation.2 | async-start | bytes 1179648 | tf_op jit(solution)/shard_map/reduce_scatter | solution.py:109
  29.4 4.5 %copy-start.1 = (bf16[16,512,128]{1,2,0:T(8,128)(2,1)S(1)}, bf16[16,512,128]{1,2,0:T(8,128)(2,1)}, u32[]{:S(2)}) copy-start(bf16[16,512,128]{1,2,0:T(8,128)(2,1)} %broadcast_in_dim.113) | copy-start | bytes 6291460
  60.9 59.7 %collective-permute-start.5 = (bf16[256,32,128]{2,1,0:T(8,128)(2,1)}, bf16[256,32,128]{2,1,0:T(8,128)(2,1)}, u32[]{:S(2)}, u32[]{:S(2)}) collective-permute-start(bf16[256,32,128]{2,1,0:T(8,128)(2,1)} %all-gather.2.cloned.1.call-done), channel_id=1, source_target_pairs={{0,1},{1,0},{2,3},{3,2},{4,5},{5,4},{6,7},{7,6},{8,9},{9,8},{10,11... | collective-permute-start | bytes 6291464 | tf_op jit(solution)/shard_map/ppermute | solution.py:18
  65.1 27.1 %collective-permute-start.7 = (f32[64,32,128]{2,0,1:T(8,128)}, f32[64,32,128]{2,0,1:T(8,128)}, u32[]{:S(2)}, u32[]{:S(2)}) collective-permute-start(f32[64,32,128]{2,0,1:T(8,128)} %bitcast.100), channel_id=1, source_target_pairs={{0,2},{2,4},{4,6},{6,0},{1,3},{3,5},{5,7},{7,1},{8,10},{10,12},{12... | collective-permute-start | bytes 3145736 | tf_op jit(solution)/shard_map/ppermute | solution.py:108
  68.2 47.4 %collective-permute-start.8 = (f32[64,32,128]{2,0,1:T(8,128)}, f32[64,32,128]{2,0,1:T(8,128)}, u32[]{:S(2)}, u32[]{:S(2)}) collective-permute-start(f32[64,32,128]{2,0,1:T(8,128)} %bitcast.99), channel_id=1, source_target_pairs={{0,4},{2,6},{4,0},{6,2},{1,5},{3,7},{5,1},{7,3},{8,12},{10,14},{12... | collective-permute-start | bytes 3145736 | tf_op jit(solution)/shard_map/ppermute | solution.py:108
  72.5 44.5 %collective-permute-start.9 = (f32[64,32,128]{2,0,1:T(8,128)}, f32[64,32,128]{2,0,1:T(8,128)}, u32[]{:S(2)}, u32[]{:S(2)}) collective-permute-start(f32[64,32,128]{2,0,1:T(8,128)} %bitcast.98), channel_id=1, source_target_pairs={{0,6},{2,0},{4,2},{6,4},{1,7},{3,1},{5,3},{7,5},{8,14},{10,8},{12,... | collective-permute-start | bytes 3145736 | tf_op jit(solution)/shard_map/ppermute | solution.py:108
  125.1 12.2 %copy-start = (f32[128,64,32,2]{0,3,2,1:T(2,128)S(1)}, f32[128,64,32,2]{0,3,2,1:T(2,128)}, u32[]{:S(2)}) copy-start(f32[128,64,32,2]{0,3,2,1:T(2,128)} %convert.4) | copy-start | bytes 6291460
  145.8 26.4 %collective-permute-start.6 = (bf16[128,4096]{0,1:T(8,128)(2,1)S(1)}, bf16[128,4096]{0,1:T(8,128)(2,1)S(1)}, u32[]{:S(2)}, u32[]{:S(2)}) collective-permute-start(bf16[128,4096]{0,1:T(8,128)(2,1)S(1)} %fusion.14), channel_id=1, source_target_pairs={{64,0},{128,64},{192,128},{65,1},{129,65},{193,129},{66,2},{130,66... | collective-permute-start | bytes 3145736 | tf_op jit(solution)/shard_map/ppermute | solution.py:13
Sparse Core Ops, SparseCore 0:
  19.2 41.6 all-gather.1
  120.7 37.4 reduce-scatter.1

commit v9 on v5

--- a/solution.py
+++ b/solution.py
@@ -38,7 +38,17 @@
     grad_scale = (tok_rows * nz * nx * nc) ** (-0.5)
 
     own_tiles = tiles[0].reshape(slot_dev, half, lanes)
-    gathered = lax.all_gather(own_tiles, "x", axis=0, tiled=True)
+    my_x = lax.axis_index("x")
+    ring4 = nx == 4
+    if ring4:
+        first = jnp.concatenate([own_tiles, lax.ppermute(own_tiles, "x", [(i, i ^ 1) for i in range(nx)])], axis=0)
+        gathered = jnp.concatenate([first, lax.ppermute(first, "x", [(i, nx - 1 - i) for i in range(nx)])], axis=0)
+    else:
+        gathered = jnp.concatenate(
+            [own_tiles]
+            + [lax.ppermute(own_tiles, "x", [(src, (src + s) % nx) for src in range(nx)]) for s in range(1, nx)],
+            axis=0,
+        )
     gathered = lax.all_gather(gathered, "z", axis=0, tiled=True)
     slot_ids = jnp.arange(store_slots, dtype=jnp.int32)
 
@@ -47,7 +57,13 @@
     def row_of(slot):
         holder = slot // slot_dev
         half_of = (holder % nc - my_core) % nc
-        return half_of * (nz * nx * slot_dev) + (holder // nc) * slot_dev + slot % slot_dev
+        chip = holder // nc
+        src_x = chip % nx
+        if ring4:
+            shift = jnp.where(src_x == my_x, 0, jnp.where(src_x == my_x ^ 1, 1, jnp.where(src_x == nx - 1 - my_x, 2, 3)))
+        else:
+            shift = (my_x - src_x) % nx
+        return half_of * (nz * nx * slot_dev) + ((chip // nx) * nx + shift) * slot_dev + slot % slot_dev
 
     kept_grid = jnp.arange(most_kept)[None, :] < count_list[:, None]
     col_hit = (column_list[:, :, None] == jnp.arange(ncol)[None, None, :]) & kept_grid[:, :, None]
@@ -95,7 +111,23 @@
     terms, gathered = lax.optimization_barrier((terms, gathered))
     gathered = jnp.concatenate([gathered, sibling(gathered)], axis=0)
     weight_grad = lax.psum_scatter(terms, "z", scatter_dimension=0, tiled=True)
-    weight_grad = lax.psum_scatter(weight_grad, "x", scatter_dimension=0, tiled=True)
+    x_blocks = weight_grad.reshape(nx, slot_dev, half, lanes)
+
+    def block(index):
+        return lax.dynamic_index_in_dim(x_blocks, index, axis=0, keepdims=False)
+
+    if ring4:
+        pair_x = my_x ^ 1
+        sent = jnp.stack([block(pair_x), block(nx - 1 - pair_x)])
+        got = lax.ppermute(sent, "x", [(i, i ^ 1) for i in range(nx)])
+        keep_own = block(my_x) + got[0]
+        keep_far = block(nx - 1 - my_x) + got[1]
+        weight_grad = keep_own + lax.ppermute(keep_far, "x", [(i, nx - 1 - i) for i in range(nx)])
+    else:
+        own_sum = block(my_x)
+        for s in range(1, nx):
+            own_sum = own_sum + lax.ppermute(block((my_x + s) % nx), "x", [(src, (src + s) % nx) for src in range(nx)])
+        weight_grad = own_sum
     weight_grad = (weight_grad * grad_scale).reshape(slot_dev, blk * blk)
 
     dense_w = jnp.where(

time: 159 us -> 143 us (0.90)
  waiting for transfers between devices: 55.2 us -> 41.6 us
  blocking collectives: 13.3 us -> 0 us
  starting transfers between devices: 3.45 us -> 12.2 us
    reduce_scatter x1 -> x0, waiting for transfers between devices: 19.6 us -> none  [local(): lax.psum_scatter(weight_grad, 'x', scatter_dimension=0, tiled=True)]
    all_gather x1 -> x0, blocking collectives: 13.3 us -> none  [local(): gathered = lax.all_gather(own_tiles, 'x', axis=0, tiled=True)]
    ppermute x0 -> x4, waiting for transfers between devices: none -> 10.4 us  [the longest x1 6.5 us: local(): got = lax.ppermute(sent, 'x', [(i, i ^ 1) for i in range(nx)])]
    ppermute x0 -> x4, starting transfers between devices: none -> 8.76 us  [the longest x1 2.85 us: local(): lax.ppermute(first, 'x', [(i, nx - 1 - i) for i in range(nx)])]
    ppermute x1, waiting for transfers between devices: 4.45 us -> 0.01 us  [shifted(): lax.ppermute(value, axis, [(source, source + steps) for source in range(l...]
  transfers between devices with their start and end apart: 7 -> 10, of which waited for: 4 -> 6; matrix products, arithmetic and copies ran while one was open for 42% -> 51% of each run, Pallas kernels for 0% -> 0%
where the time goes in v9:
time: 143 us
  local copies, waits for them, and re-layouts  43.9 us (31%)
  waiting for transfers between devices  41.6 us (29%)
  matrix products  15.5 us (11%)
  other arithmetic  15.4 us (11%)
  between operations  14.4 us (10%)
  starting transfers between devices  12.2 us (9%)
    reduce_scatter x1, waiting for transfers between devices, local(): weight_grad = lax.psum_scatter(terms, 'z', scatter_dimension=0, tiled=True)  20.5 us
    gather x1, local copies, waits for them, and re-layouts, local(): gathered[dense_rows]  12.1 us
    all_gather x1, waiting for transfers between devices, local(): gathered = lax.all_gather(gathered, 'z', axis=0, tiled=True)  10.6 us
    dot_general x1, matrix products, local(): jnp.dot(normed_pairs.reshape((panel_list + 1) * half, 2 * pair_tokens), e...  9.64 us
    gather x1, local copies, waits for them, and re-layouts, local(): terms = dense_terms[jnp.where(term_kept, term_index, panel_list * ncol)]  8.82 us
    ppermute x1, waiting for transfers between devices, local(): got = lax.ppermute(sent, 'x', [(i, i ^ 1) for i in range(nx)])  6.5 us
    dot_general x1, matrix products, local(): jnp.einsum('cthl,pcrl->tprh', expand, dense_w, preferred_element_type=jnp...  5.83 us
    unnamed x23, local copies, waits for them, and re-layouts  5.25 us
  transfers between devices with their start and end apart: 10, of which 6 were waited for; matrix products, arithmetic and copies ran while one was open for 51% of the time, Pallas kernels for 0%

profile of v9, /device:TPU:8, one launch (start us, length us, event | category | flops | bytes accessed | tf_op | source)
XLA Modules:
  0.0 143.0 jit_solution(17429247096014468244)
XLA Ops:
  7.2 0.9 copy.103
  8.1 1.6 %collective-permute-start.2 = (bf16[8,32,128]{2,1,0:T(8,128)(2,1)S(1)}, bf16[8,32,128]{2,1,0:T(8,128)(2,1)S(1)}, u32[]{:S(2)}, u32[]{:S(2)}) collective-permute-start(bf16[8,32,128]{2,1,0:T(8,128)(2,1)S(1)} %bitcast.106), channel_id=1, source_target_pairs={{0,2},{2,0},{4,6},{6,4},{1,3},{3,1},{5,7},{7,5},{8,10},{10,8},{12,... | collective-permute-start | bytes 196616 | tf_op jit(solution)/shard_map/ppermute | solution.py:44
  9.7 1.6 %copy.68 = bf16[1,128,4096]{1,2,0:T(8,128)(2,1)S(1)} copy(bf16[1,128,4096]{2,1,0:T(8,128)(2,1)} %param.7) | data formatting | bytes 2097152 | tf_op args[0]
  12.4 2.8 %collective-permute-start.3 = (bf16[16,32,128]{2,1,0:T(8,128)(2,1)S(1)}, bf16[16,32,128]{2,1,0:T(8,128)(2,1)S(1)}, u32[]{:S(2)}, u32[]{:S(2)}) collective-permute-start(bf16[16,32,128]{2,1,0:T(8,128)(2,1)S(1)} %pad_maximum_fusion.6), channel_id=1, source_target_pairs={{0,6},{2,4},{4,2},{6,0},{1,7},{3,5},{5,3},{7,1},{8,14},{10,12},{12... | collective-permute-start | bytes 393224 | tf_op jit(solution)/shard_map/ppermute | solution.py:45
  15.3 1.5 %fusion.11 = bf16[128,4096]{0,1:T(8,128)(2,1)} fusion(bf16[1,128,4096]{1,2,0:T(8,128)(2,1)S(1)} %copy.68, f32[4096]{0:T(1024)S(1)} %bitcast.112, f32[128]{0:T(128)S(1)} %get-tuple-element.19), kind=kLoop, calls=%fused_computation.18 | loop fusion | flops 2097152 | bytes 2114048 | tf_op jit(solution)/shard_map/convert_element_type | solution.py:76
  17.5 1.2 collective-permute-done.3
  18.7 0.7 pad_maximum_fusion.4
  21.1 1.7 %broadcast_in_dim.119 = bf16[16,2,256,128]{2,1,3,0:T(2,128)(2,1)S(1)} broadcast(bf16[16,256,128]{1,2,0:T(8,128)(2,1)S(1)} %pad_maximum_fusion.2), dimensions={0,2,3} | broadcast | bytes 3145728 | tf_op jit(solution)/shard_map/jit(_where)/broadcast_in_dim | solution.py:88
  22.8 2.7 %broadcast_in_dim.120 = bf16[16,512,128]{1,2,0:T(8,128)(2,1)} reshape(bf16[16,2,256,128]{2,1,3,0:T(2,128)(2,1)S(1)} %broadcast_in_dim.119) | data formatting | bytes 4194304 | tf_op jit(solution)/shard_map/jit(_where)/broadcast_in_dim | solution.py:88
  25.5 1.8 %pad_maximum_fusion.1 = bf16[256,4096]{0,1:T(8,128)(2,1)S(1)} fusion(bf16[128,4096]{0,1:T(8,128)(2,1)} %collective-permute-done, bf16[128,4096]{0,1:T(8,128)(2,1)} %fusion.11), kind=kLoop, calls=%fused_computation.11 | loop fusion | flops 4194304 | bytes 4194304 | tf_op jit(solution)/shard_map/concatenate | solution.py:78
  27.2 2.3 %reshape.412 = bf16[256,64,32,2]{0,3,2,1:T(2,128)(2,1)} reshape(bf16[256,4096]{0,1:T(8,128)(2,1)S(1)} %pad_maximum_fusion.1) | data formatting | bytes 4194304 | tf_op jit(solution)/shard_map/reshape | solution.py:89
  29.5 4.5 %reshape.413 = bf16[64,32,512]{2,1,0:T(8,128)(2,1)} reshape(bf16[64,32,2,256]{3,2,1,0:T(2,128)(2,1)} %bitcast.100) | data formatting | bytes 4194304 | tf_op jit(solution)/shard_map/reshape | solution.py:90
  34.0 9.6 %fusion.5 = f32[65,32,16,128]{3,1,2,0:T(8,128)} fusion(bf16[64,32,512]{2,1,0:T(8,128)(2,1)} %reshape.413, bf16[16,512,128]{1,2,0:T(8,128)(2,1)S(1)} %copy-done.1, pred[512,128]{0,1:T(8,128)(4,1)S(1)} %copy.71), kind=kOutput, calls=%fused_computation.8 | convolution fusion | flops 4363124736 | bytes 21299200 | tf_op jit(solution)/shard_map/dot_general | solution.py:93
  43.7 8.8 %gather_fusion = f32[256,32,128]{2,1,0:T(8,128)} fusion(f32[1040,32,128]{2,1,0:T(8,128)} %bitcast.105, s32[1024]{0:T(1024)S(1)} %pad_clamp_fusion), kind=kCustom, calls=%fused_computation | custom fusion | bytes 8389632 | tf_op jit(solution)/shard_map/gather | solution.py:110
  52.5 10.6 %all-gather.2.cloned.1.call-done = bf16[256,32,128]{2,1,0:T(8,128)(2,1)} async-done(((bf16[32,32,128]{2,1,0:T(8,128)(2,1)}), bf16[256,32,128]{2,1,0:T(8,128)(2,1)}) %all-gather.2.cloned.1.call-update) | async-done | bytes 2097168 | tf_op jit(solution)/shard_map/all_gather | solution.py:52
  65.1 2.3 %convert.4 = f32[128,64,32,2]{0,3,2,1:T(2,128)} convert(bf16[128,64,32,2]{0,3,2,1:T(2,128)(2,1)S(1)} %bitcast.97) | non-fusion elementwise | flops 524288 | bytes 3145728 | tf_op jit(solution)/shard_map/convert_element_type | solution.py:22
  67.6 1.0 copy.80
  69.8 1.0 mul.153
  71.3 4.6 %pad_maximum_fusion = bf16[512,32,128]{2,1,0:T(8,128)(2,1)} fusion(bf16[256,32,128]{2,1,0:T(8,128)(2,1)} %collective-permute-done.4, bf16[256,32,128]{2,1,0:T(8,128)(2,1)} %all-gather.2.cloned.1.call-done), kind=kLoop, calls=%fused_computation.6 | loop fusion | flops 2097152 | bytes 8388608 | tf_op jit(solution)/shard_map/concatenate | solution.py:112
  75.9 12.1 %gather_fusion.1 = bf16[1024,32,128]{2,1,0:T(8,128)(2,1)} fusion(bf16[512,32,128]{2,1,0:T(8,128)(2,1)} %pad_maximum_fusion, s32[1024]{0:T(1024)S(1)} %broadcast_clamp_fusion), kind=kCustom, calls=%fused_computation.1 | custom fusion | bytes 16781312 | tf_op jit(solution)/shard_map/gather | solution.py:134
  88.1 5.8 %fusion.15 = (f32[128]{0:T(128)S(1)}, f32[128,64,32,2]{0,2,3,1:T(8,128)S(1)}) fusion(f32[128,64,32,2]{0,3,2,1:T(2,128)S(1)} %copy-done, f32[64,32,2]{1,2,0:T(2,128)S(1)} %copy.82, pred[2,128]{1,0:T(4,128)(4,1)S(1)} %iota_compare_fusion.2, bf16[16,128,128]{2,1,0:T(8,128)(2,1)} %copy.80, bf16[64,16,32,128]{3,2,1,0:T(8,128)(2,1)} %bitcast.98, ...), kind=kOutput, calls=%fused_computation.23 | convolution fusion | flops 2153775104 | bytes 13125376 | tf_op jit(solution)/shard_map/cthl,pcrl->tprh/dot_general | solution.py:136
  93.9 1.9 %copy.81 = f32[128,64,32,2]{0,3,2,1:T(2,128)S(1)} copy(f32[128,64,32,2]{0,2,3,1:T(8,128)S(1)} %get-tuple-element.21) | data formatting | bytes 4194304 | tf_op jit(solution)/shard_map/cthl,pcrl->tprh/transpose | solution.py:136
  95.8 0.7 fusion.14
  96.6 2.5 %collective-permute-start.5 = (bf16[128,4096]{0,1:T(8,128)(2,1)S(1)}, bf16[128,4096]{0,1:T(8,128)(2,1)S(1)}, u32[]{:S(2)}, u32[]{:S(2)}) collective-permute-start(bf16[128,4096]{0,1:T(8,128)(2,1)S(1)} %fusion.14), channel_id=1, source_target_pairs={{64,0},{128,64},{192,128},{65,1},{129,65},{193,129},{66,2},{130,66... | collective-permute-start | bytes 3145736 | tf_op jit(solution)/shard_map/ppermute | solution.py:13
  99.1 20.5 %reduce-scatter.2.cloned.1.call-done = f32[32,32,128]{2,1,0:T(8,128)} async-done(((f32[256,32,128]{2,1,0:T(8,128)}), f32[32,32,128]{2,1,0:T(8,128)}) %reduce-scatter.2.cloned.1.call-update) | async-done | bytes 524304 | tf_op jit(solution)/shard_map/reduce_scatter | solution.py:113
  119.6 1.1 constant_dynamic-slice_fusion.2
  121.0 1.5 %collective-permute-start.6 = (f32[2,8,32,128]{3,1,2,0:T(8,128)S(1)}, f32[2,8,32,128]{3,1,2,0:T(8,128)S(1)}, u32[]{:S(2)}, u32[]{:S(2)}) collective-permute-start(f32[2,8,32,128]{3,1,2,0:T(8,128)S(1)} %pad_maximum_fusion.5), channel_id=1, source_target_pairs={{0,2},{2,0},{4,6},{6,4},{1,3},{3,1},{5,7},{7,5},{8,10},{10,8},{12,... | collective-permute-start | bytes 786440 | tf_op jit(solution)/shard_map/ppermute | solution.py:122
  122.5 6.5 %collective-permute-done.6 = f32[2,8,32,128]{3,1,2,0:T(8,128)S(1)} collective-permute-done((f32[2,8,32,128]{3,1,2,0:T(8,128)S(1)}, f32[2,8,32,128]{3,1,2,0:T(8,128)S(1)}, u32[]{:S(2)}, u32[]{:S(2)}) %collective-permute-start.6) | collective-permute-done | bytes 262176 | tf_op jit(solution)/shard_map/ppermute | solution.py:122
  129.1 2.8 %collective-permute-start.7 = (f32[8,32,128]{2,0,1:T(8,128)S(1)}, f32[8,32,128]{2,0,1:T(8,128)S(1)}, u32[]{:S(2)}, u32[]{:S(2)}) collective-permute-start(f32[8,32,128]{2,0,1:T(8,128)S(1)} %fusion.29), channel_id=1, source_target_pairs={{0,6},{2,4},{4,2},{6,0},{1,7},{3,5},{5,3},{7,1},{8,14},{10,12},{12... | collective-permute-start | bytes 393224 | tf_op jit(solution)/shard_map/ppermute | solution.py:125
  131.9 1.3 copy.88
  133.2 2.2 %collective-permute-done.7 = f32[8,32,128]{2,0,1:T(8,128)S(1)} collective-permute-done((f32[8,32,128]{2,0,1:T(8,128)S(1)}, f32[8,32,128]{2,0,1:T(8,128)S(1)}, u32[]{:S(2)}, u32[]{:S(2)}) %collective-permute-start.7) | collective-permute-done | bytes 131104 | tf_op jit(solution)/shard_map/ppermute | solution.py:125
  135.4 0.7 fusion.33
  (72 shorter events, 7.6 us)
Async XLA Ops:
  7.2 8.1 %copy-start.3 = (f32[1,4096]{1,0:T(1,128)S(1)}, f32[1,4096]{1,0:T(1,128)}, u32[]{:S(2)}) copy-start(f32[1,4096]{1,0:T(1,128)} %param.9) | copy-start | bytes 49156
  7.2 56.0 %all-gather.2.cloned.1.call-start = ((), (), s32[]{:S(2)}) async-start(), calls=%async_computation.1 | async-start | bytes 2359296 | tf_op jit(solution)/shard_map/all_gather | solution.py:52
  8.1 4.4 %collective-permute-start.2 = (bf16[8,32,128]{2,1,0:T(8,128)(2,1)S(1)}, bf16[8,32,128]{2,1,0:T(8,128)(2,1)S(1)}, u32[]{:S(2)}, u32[]{:S(2)}) collective-permute-start(bf16[8,32,128]{2,1,0:T(8,128)(2,1)S(1)} %bitcast.106), channel_id=1, source_target_pairs={{0,2},{2,0},{4,6},{6,4},{1,3},{3,1},{5,7},{7,5},{8,10},{10,8},{12,... | collective-permute-start | bytes 196616 | tf_op jit(solution)/shard_map/ppermute | solution.py:44
  11.3 5.5 %copy-start.2 = (bf16[1,128,1024]{2,1,0:T(8,128)(2,1)S(1)}, bf16[1,128,1024]{2,1,0:T(8,128)(2,1)}, u32[]{:S(2)}) copy-start(bf16[1,128,1024]{2,1,0:T(8,128)(2,1)} %param.8) | copy-start | bytes 786436
  11.8 8.2 %copy-start.6 = (s32[1,64]{1,0:T(1,128)S(1)}, s32[1,64]{1,0:T(1,128)}, u32[]{:S(2)}) copy-start(s32[1,64]{1,0:T(1,128)} %param.12) | copy-start | bytes 772
  11.8 8.3 %copy-start.4 = (s32[1,64,8]{1,2,0:T(8,128)S(1)}, s32[1,64,8]{1,2,0:T(8,128)}, u32[]{:S(2)}) copy-start(s32[1,64,8]{1,2,0:T(8,128)} %param.11) | copy-start | bytes 6148
  11.9 8.5 %copy-start.5 = (s32[1,512]{1,0:T(1,128)S(1)}, s32[1,512]{1,0:T(1,128)}, u32[]{:S(2)}) copy-start(s32[1,512]{1,0:T(1,128)} %param.13) | copy-start | bytes 6148
  12.4 6.3 %collective-permute-start.3 = (bf16[16,32,128]{2,1,0:T(8,128)(2,1)S(1)}, bf16[16,32,128]{2,1,0:T(8,128)(2,1)S(1)}, u32[]{:S(2)}, u32[]{:S(2)}) collective-permute-start(bf16[16,32,128]{2,1,0:T(8,128)(2,1)S(1)} %pad_maximum_fusion.6), channel_id=1, source_target_pairs={{0,6},{2,4},{4,2},{6,0},{1,7},{3,5},{5,3},{7,1},{8,14},{10,12},{12... | collective-permute-start | bytes 393224 | tf_op jit(solution)/shard_map/ppermute | solution.py:45
  16.8 8.7 %collective-permute-start = (bf16[128,4096]{0,1:T(8,128)(2,1)}, bf16[128,4096]{0,1:T(8,128)(2,1)}, u32[]{:S(2)}, u32[]{:S(2)}) collective-permute-start(bf16[128,4096]{0,1:T(8,128)(2,1)} %fusion.11), channel_id=1, source_target_pairs={{0,1},{1,0},{2,3},{3,2},{4,5},{5,4},{6,7},{7,6},{8,9},{9,8},{10,11... | collective-permute-start | bytes 3145736 | tf_op jit(solution)/shard_map/ppermute | solution.py:18
  16.9 3.9 %collective-permute-start.1 = (bf16[128,1024]{0,1:T(8,128)(2,1)S(1)}, bf16[128,1024]{0,1:T(8,128)(2,1)S(1)}, u32[]{:S(2)}, u32[]{:S(2)}) collective-permute-start(bf16[128,1024]{0,1:T(8,128)(2,1)S(1)} %bitcast.101), channel_id=1, source_target_pairs={{0,1},{1,0},{2,3},{3,2},{4,5},{5,4},{6,7},{7,6},{8,9},{9,8},{10,11... | collective-permute-start | bytes 786440 | tf_op jit(solution)/shard_map/ppermute | solution.py:18
  19.5 100.2 %reduce-scatter.2.cloned.1.call-start = ((), (), s32[]{:S(2)}) async-start(), calls=%async_computation.2 | async-start | bytes 4718592 | tf_op jit(solution)/shard_map/reduce_scatter | solution.py:113
  29.5 4.5 %copy-start.1 = (bf16[16,512,128]{1,2,0:T(8,128)(2,1)S(1)}, bf16[16,512,128]{1,2,0:T(8,128)(2,1)}, u32[]{:S(2)}) copy-start(bf16[16,512,128]{1,2,0:T(8,128)(2,1)} %broadcast_in_dim.120) | copy-start | bytes 6291460
  63.2 8.2 %collective-permute-start.4 = (bf16[256,32,128]{2,1,0:T(8,128)(2,1)}, bf16[256,32,128]{2,1,0:T(8,128)(2,1)}, u32[]{:S(2)}, u32[]{:S(2)}) collective-permute-start(bf16[256,32,128]{2,1,0:T(8,128)(2,1)} %all-gather.2.cloned.1.call-done), channel_id=1, source_target_pairs={{0,1},{1,0},{2,3},{3,2},{4,5},{5,4},{6,7},{7,6},{8,9},{9,8},{10,11... | collective-permute-start | bytes 6291464 | tf_op jit(solution)/shard_map/ppermute | solution.py:18
  75.9 12.1 %copy-start = (f32[128,64,32,2]{0,3,2,1:T(2,128)S(1)}, f32[128,64,32,2]{0,3,2,1:T(2,128)}, u32[]{:S(2)}) copy-start(f32[128,64,32,2]{0,3,2,1:T(2,128)} %convert.4) | copy-start | bytes 6291460
  96.6 35.3 %collective-permute-start.5 = (bf16[128,4096]{0,1:T(8,128)(2,1)S(1)}, bf16[128,4096]{0,1:T(8,128)(2,1)S(1)}, u32[]{:S(2)}, u32[]{:S(2)}) collective-permute-start(bf16[128,4096]{0,1:T(8,128)(2,1)S(1)} %fusion.14), channel_id=1, source_target_pairs={{64,0},{128,64},{192,128},{65,1},{129,65},{193,129},{66,2},{130,66... | collective-permute-start | bytes 3145736 | tf_op jit(solution)/shard_map/ppermute | solution.py:13
  121.0 8.1 %collective-permute-start.6 = (f32[2,8,32,128]{3,1,2,0:T(8,128)S(1)}, f32[2,8,32,128]{3,1,2,0:T(8,128)S(1)}, u32[]{:S(2)}, u32[]{:S(2)}) collective-permute-start(f32[2,8,32,128]{3,1,2,0:T(8,128)S(1)} %pad_maximum_fusion.5), channel_id=1, source_target_pairs={{0,2},{2,0},{4,6},{6,4},{1,3},{3,1},{5,7},{7,5},{8,10},{10,8},{12,... | collective-permute-start | bytes 786440 | tf_op jit(solution)/shard_map/ppermute | solution.py:122
  129.1 6.3 %collective-permute-start.7 = (f32[8,32,128]{2,0,1:T(8,128)S(1)}, f32[8,32,128]{2,0,1:T(8,128)S(1)}, u32[]{:S(2)}, u32[]{:S(2)}) collective-permute-start(f32[8,32,128]{2,0,1:T(8,128)S(1)} %fusion.29), channel_id=1, source_target_pairs={{0,6},{2,4},{4,2},{6,0},{1,7},{3,5},{5,3},{7,1},{8,14},{10,12},{12... | collective-permute-start | bytes 393224 | tf_op jit(solution)/shard_map/ppermute | solution.py:125
Sparse Core Ops, SparseCore 0:
  19.6 43.5 all-gather.1
  65.7 53.8 reduce-scatter.1

commit v10 on v7

--- a/solution.py
+++ b/solution.py
@@ -38,12 +38,9 @@
     grad_scale = (tok_rows * nz * nx * nc) ** (-0.5)
 
     own_tiles = tiles[0].reshape(slot_dev, half, lanes)
-    gathered = jnp.concatenate(
-        [own_tiles]
-        + [lax.ppermute(own_tiles, "x", [(src, (src + s) % nx) for src in range(nx)]) for s in range(1, nx)],
-        axis=0,
-    )
-    gathered = lax.all_gather(gathered, "z", axis=0, tiled=True)
+    padded = jnp.concatenate([own_tiles, jnp.zeros(((nx - 1) * slot_dev, half, lanes), own_tiles.dtype)], axis=0)
+    gathered_z = lax.all_gather(padded, "z", axis=0, tiled=True).reshape(nz, nx * slot_dev, half, lanes)
+    gathered_z = gathered_z[:, :slot_dev].reshape(nz * slot_dev, half, lanes)
     slot_ids = jnp.arange(store_slots, dtype=jnp.int32)
 
     my_core = lax.axis_index("core")
@@ -54,7 +51,7 @@
         half_of = (holder % nc - my_core) % nc
         chip = holder // nc
         shift = (my_x - chip % nx) % nx
-        return half_of * (nz * nx * slot_dev) + ((chip // nx) * nx + shift) * slot_dev + slot % slot_dev
+        return half_of * (nz * nx * slot_dev) + (shift * nz + chip // nx) * slot_dev + slot % slot_dev
 
     kept_grid = jnp.arange(most_kept)[None, :] < count_list[:, None]
     col_hit = (column_list[:, :, None] == jnp.arange(ncol)[None, None, :]) & kept_grid[:, :, None]
@@ -99,7 +96,12 @@
     term_index = jnp.sum(jnp.where(slot_match, pos_index[None, :], 0), axis=1)
     term_kept = jnp.any(slot_match & pos_kept[None, :], axis=1)
     terms = dense_terms[jnp.where(term_kept, term_index, panel_list * ncol)]
-    terms, gathered = lax.optimization_barrier((terms, gathered))
+    terms, gathered_z = lax.optimization_barrier((terms, gathered_z))
+    gathered = jnp.concatenate(
+        [gathered_z]
+        + [lax.ppermute(gathered_z, "x", [(src, (src + s) % nx) for src in range(nx)]) for s in range(1, nx)],
+        axis=0,
+    )
     gathered = jnp.concatenate([gathered, sibling(gathered)], axis=0)
     weight_grad = lax.psum_scatter(terms, "z", scatter_dimension=0, tiled=True)
     x_blocks = weight_grad.reshape(nx, slot_dev, half, lanes)

time: 137 us -> 157 us (1.15)
  waiting for transfers between devices: 32.3 us -> 46.6 us
  local copies, waits for them, and re-layouts: 43.9 us -> 53.5 us
  other arithmetic: 15.3 us -> 11.6 us
    reduce_scatter x1, waiting for transfers between devices: 20.5 us -> 0.02 us  [local(): weight_grad = lax.psum_scatter(terms, 'z', scatter_dimension=0, tiled=True)]
    ppermute x1, waiting for transfers between devices: 0.01 us -> 18.2 us  [shifted(): lax.ppermute(value, axis, [(source, source + steps) for source in range(l...]
    ppermute x3, waiting for transfers between devices: 0.01 us -> 17.2 us  [local(): lax.ppermute(gathered_z, 'x', [(src, (src + s) % nx) for src in range(nx)])]
    concatenate x0 -> x2, local copies, waits for them, and re-layouts: none -> 4.05 us  [the longest x1 3.29 us: local(): gathered = jnp.concatenate([gathered, sibling(gathered)], axis=0)]
    concatenate x2 -> x1, other arithmetic: 5.32 us -> 1.66 us  [local(): jnp.concatenate([gathered_z] + [lax.ppermute(gathered_z, 'x', [(src, (src...]
    all_gather x0 -> x1, local copies, waits for them, and re-layouts: none -> 2.94 us  [local(): lax.all_gather(padded, 'z', axis=0, tiled=True)]
    ppermute x3, waiting for transfers between devices: 2.87 us -> 0.01 us  [local(): lax.ppermute(outgoing, 'x', [(src, (src + s) % nx) for src in range(nx)])]
    unnamed x21 -> x34, local copies, waits for them, and re-layouts: 5.09 us -> 7.65 us
  transfers between devices with their start and end apart: 12 -> 12, of which waited for: 4 -> 5; matrix products, arithmetic and copies ran while one was open for 54% -> 47% of each run, Pallas kernels for 0% -> 0%
where the time goes in v10:
time: 157 us; the launch traced here: 156 us
  local copies, waits for them, and re-layouts  53.5 us (34%)
  waiting for transfers between devices  46.6 us (30%)
  matrix products  15.5 us (10%)
  between operations  14.4 us (9%)
  starting transfers between devices  14.2 us (9%)
  other arithmetic  11.6 us (7%)
    ppermute x1, waiting for transfers between devices, shifted(): lax.ppermute(value, axis, [(source, source + steps) for source in range(l...  18.2 us
    ppermute x3, waiting for transfers between devices, local(): lax.ppermute(gathered_z, 'x', [(src, (src + s) % nx) for src in range(nx)])  17.2 us
    gather x1, local copies, waits for them, and re-layouts, local(): gathered[dense_rows]  12.2 us
    all_gather x1, waiting for transfers between devices, local(): lax.all_gather(padded, 'z', axis=0, tiled=True)  10.8 us
    dot_general x1, matrix products, local(): jnp.dot(normed_pairs.reshape((panel_list + 1) * half, 2 * pair_tokens), e...  9.71 us
    gather x1, local copies, waits for them, and re-layouts, local(): terms = dense_terms[jnp.where(term_kept, term_index, panel_list * ncol)]  8.73 us
    unnamed x34, local copies, waits for them, and re-layouts  7.65 us
    dot_general x1, matrix products, local(): jnp.einsum('cthl,pcrl->tprh', expand, dense_w, preferred_element_type=jnp...  5.75 us
  transfers between devices with their start and end apart: 12, of which 5 were waited for; matrix products, arithmetic and copies ran while one was open for 47% of the time, Pallas kernels for 0%

profile of v10, /device:TPU:8, one launch (start us, length us, event | category | flops | bytes accessed | tf_op | source)
XLA Modules:
  0.0 155.7 jit_solution(10298898275754472040)
XLA Ops:
  7.2 1.6 %copy.54 = bf16[1,128,4096]{1,2,0:T(8,128)(2,1)S(1)} copy(bf16[1,128,4096]{2,1,0:T(8,128)(2,1)} %param.7) | data formatting | bytes 2097152 | tf_op args[0]
  9.5 1.5 fusion.11
  14.4 1.7 %broadcast_in_dim.113 = bf16[16,2,256,128]{2,1,3,0:T(2,128)(2,1)S(1)} broadcast(bf16[16,256,128]{1,2,0:T(8,128)(2,1)S(1)} %pad_maximum_fusion.2), dimensions={0,2,3} | broadcast | bytes 3145728 | tf_op jit(solution)/shard_map/jit(_where)/broadcast_in_dim | solution.py:76
  16.2 2.6 %broadcast_in_dim.114 = bf16[16,512,128]{1,2,0:T(8,128)(2,1)} reshape(bf16[16,2,256,128]{2,1,3,0:T(2,128)(2,1)S(1)} %broadcast_in_dim.113) | data formatting | bytes 4194304 | tf_op jit(solution)/shard_map/jit(_where)/broadcast_in_dim | solution.py:76
  18.8 1.8 %pad_maximum_fusion = bf16[256,4096]{0,1:T(8,128)(2,1)S(1)} fusion(bf16[128,4096]{0,1:T(8,128)(2,1)} %collective-permute-done, bf16[128,4096]{0,1:T(8,128)(2,1)} %fusion.11), kind=kLoop, calls=%fused_computation.10 | loop fusion | flops 4194304 | bytes 4194304 | tf_op jit(solution)/shard_map/concatenate | solution.py:66
  20.5 2.2 %reshape.422 = bf16[256,64,32,2]{0,3,2,1:T(2,128)(2,1)} reshape(bf16[256,4096]{0,1:T(8,128)(2,1)S(1)} %pad_maximum_fusion) | data formatting | bytes 4194304 | tf_op jit(solution)/shard_map/reshape | solution.py:77
  22.8 4.5 %reshape.423 = bf16[64,32,512]{2,1,0:T(8,128)(2,1)} reshape(bf16[64,32,2,256]{3,2,1,0:T(2,128)(2,1)} %bitcast.107) | data formatting | bytes 4194304 | tf_op jit(solution)/shard_map/reshape | solution.py:78
  27.3 9.7 %fusion.5 = f32[65,32,16,128]{3,1,2,0:T(8,128)} fusion(bf16[64,32,512]{2,1,0:T(8,128)(2,1)} %reshape.423, bf16[16,512,128]{1,2,0:T(8,128)(2,1)S(1)} %copy-done.1, pred[512,128]{0,1:T(8,128)(4,1)S(1)} %copy.57), kind=kOutput, calls=%fused_computation.7 | convolution fusion | flops 4363124736 | bytes 21299200 | tf_op jit(solution)/shard_map/dot_general | solution.py:81
  37.0 8.7 %gather_fusion = f32[256,32,128]{2,1,0:T(8,128)} fusion(f32[1040,32,128]{2,1,0:T(8,128)} %bitcast.118, s32[1024]{0:T(1024)S(1)} %pad_clamp_fusion), kind=kCustom, calls=%fused_computation | custom fusion | bytes 8389632 | tf_op jit(solution)/shard_map/gather | solution.py:98
  45.7 10.8 %all-gather.2.cloned.1.call-done = bf16[256,32,128]{2,0,1:T(8,128)(2,1)} async-done(((bf16[32,32,128]{2,0,1:T(8,128)(2,1)}), bf16[256,32,128]{2,0,1:T(8,128)(2,1)}) %all-gather.2.cloned.1.call-update) | async-done | bytes 2097168 | tf_op jit(solution)/shard_map/all_gather | solution.py:42
  56.5 2.9 %copy.61 = bf16[256,32,128]{2,1,0:T(8,128)(2,1)S(1)} copy(bf16[256,32,128]{2,0,1:T(8,128)(2,1)} %all-gather.2.cloned.1.call-done) | data formatting | bytes 4194304 | tf_op jit(solution)/shard_map/all_gather | solution.py:42
  59.5 1.6 %collective-permute-start.2 = (bf16[64,32,128]{2,1,0:T(8,128)(2,1)S(1)}, bf16[64,32,128]{2,1,0:T(8,128)(2,1)S(1)}, u32[]{:S(2)}, u32[]{:S(2)}) collective-permute-start(bf16[64,32,128]{2,1,0:T(8,128)(2,1)S(1)} %bitcast.108), channel_id=1, source_target_pairs={{0,2},{2,4},{4,6},{6,0},{1,3},{3,5},{5,7},{7,1},{8,10},{10,12},{12... | collective-permute-start | bytes 1572872 | tf_op jit(solution)/shard_map/ppermute | solution.py:102
  61.1 2.7 %collective-permute-start.3 = (bf16[64,32,128]{2,1,0:T(8,128)(2,1)S(1)}, bf16[64,32,128]{2,1,0:T(8,128)(2,1)S(1)}, u32[]{:S(2)}, u32[]{:S(2)}) collective-permute-start(bf16[64,32,128]{2,1,0:T(8,128)(2,1)S(1)} %bitcast.109), channel_id=1, source_target_pairs={{0,4},{2,6},{4,0},{6,2},{1,5},{3,7},{5,1},{7,3},{8,12},{10,14},{12... | collective-permute-start | bytes 1572872 | tf_op jit(solution)/shard_map/ppermute | solution.py:102
  63.8 1.5 collective-permute-start.4
  65.2 9.4 %collective-permute-done.2 = bf16[64,32,128]{2,1,0:T(8,128)(2,1)S(1)} collective-permute-done((bf16[64,32,128]{2,1,0:T(8,128)(2,1)S(1)}, bf16[64,32,128]{2,1,0:T(8,128)(2,1)S(1)}, u32[]{:S(2)}, u32[]{:S(2)}) %collective-permute-start.2) | collective-permute-done | bytes 524320 | tf_op jit(solution)/shard_map/ppermute | solution.py:102
  74.7 7.8 %collective-permute-done.3 = bf16[64,32,128]{2,1,0:T(8,128)(2,1)S(1)} collective-permute-done((bf16[64,32,128]{2,1,0:T(8,128)(2,1)S(1)}, bf16[64,32,128]{2,1,0:T(8,128)(2,1)S(1)}, u32[]{:S(2)}, u32[]{:S(2)}) %collective-permute-start.3) | collective-permute-done | bytes 524320 | tf_op jit(solution)/shard_map/ppermute | solution.py:102
  82.4 1.7 %pad_maximum_fusion.1 = bf16[256,32,128]{2,1,0:T(8,128)(2,1)} fusion(bf16[64,32,128]{2,1,0:T(8,128)(2,1)S(1)} %collective-permute-done.4, bf16[64,32,128]{2,1,0:T(8,128)(2,1)S(1)} %collective-permute-done.3, bf16[64,32,128]{2,1,0:T(8,128)(2,1)S(1)} %collective-permute-done.2, bf16[64,32,128]{2,1,0:T(8,128)(2,1)S(1)} %bitcast.111), kind=kLoop, calls=%fused_computation.11 | loop fusion | flops 3145728 | bytes 4194304 | tf_op jit(solution)/shard_map/concatenate | solution.py:100
  85.8 2.2 %convert.4 = f32[128,64,32,2]{0,3,2,1:T(2,128)} convert(bf16[128,64,32,2]{0,3,2,1:T(2,128)(2,1)S(1)} %bitcast.104) | non-fusion elementwise | flops 524288 | bytes 3145728 | tf_op jit(solution)/shard_map/convert_element_type | solution.py:22
  88.2 1.0 copy.67
  90.5 1.0 mul.151
  92.0 0.9 constant_dynamic-update-slice_fusion.4
  95.4 3.3 %constant_dynamic-update-slice_fusion = bf16[512,32,128]{2,1,0:T(8,128)(2,1)} fusion(bf16[512,32,128]{2,1,0:T(8,128)(2,1)} %constant_dynamic-update-slice_fusion.1, bf16[256,32,128]{2,1,0:T(8,128)(2,1)} %collective-permute-done.5), kind=kLoop, calls=%fused_computation.55 | loop fusion | bytes 4194304 | tf_op jit(solution)/shard_map/concatenate | solution.py:105
  98.7 12.2 %gather_fusion.1 = bf16[1024,32,128]{2,1,0:T(8,128)(2,1)} fusion(bf16[512,32,128]{2,1,0:T(8,128)(2,1)} %constant_dynamic-update-slice_fusion, s32[1024]{0:T(1024)S(1)} %broadcast_clamp_fusion), kind=kCustom, calls=%fused_computation.1 | custom fusion | bytes 16781312 | tf_op jit(solution)/shard_map/gather | solution.py:116
  110.9 5.8 %fusion.15 = (f32[128]{0:T(128)S(1)}, f32[128,64,32,2]{0,2,3,1:T(8,128)S(1)}) fusion(f32[128,64,32,2]{0,3,2,1:T(2,128)S(1)} %copy-done, f32[64,32,2]{1,2,0:T(2,128)S(1)} %copy.69, pred[2,128]{1,0:T(4,128)(4,1)S(1)} %iota_compare_fusion.2, bf16[16,128,128]{2,1,0:T(8,128)(2,1)} %copy.67, bf16[64,16,32,128]{3,2,1,0:T(8,128)(2,1)} %bitcast.105, ...), kind=kOutput, calls=%fused_computation.23 | convolution fusion | flops 2153775104 | bytes 13125376 | tf_op jit(solution)/shard_map/cthl,pcrl->tprh/dot_general | solution.py:118
  116.7 1.9 %copy.68 = f32[128,64,32,2]{0,3,2,1:T(2,128)S(1)} copy(f32[128,64,32,2]{0,2,3,1:T(8,128)S(1)} %get-tuple-element.19) | data formatting | bytes 4194304 | tf_op jit(solution)/shard_map/cthl,pcrl->tprh/transpose | solution.py:118
  119.3 2.4 %collective-permute-start.6 = (bf16[128,4096]{0,1:T(8,128)(2,1)S(1)}, bf16[128,4096]{0,1:T(8,128)(2,1)S(1)}, u32[]{:S(2)}, u32[]{:S(2)}) collective-permute-start(bf16[128,4096]{0,1:T(8,128)(2,1)S(1)} %fusion.14), channel_id=1, source_target_pairs={{64,0},{128,64},{192,128},{65,1},{129,65},{193,129},{66,2},{130,66... | collective-permute-start | bytes 3145736 | tf_op jit(solution)/shard_map/ppermute | solution.py:13
  121.8 1.1 constant_dynamic-slice_fusion.2
  123.0 1.3 collective-permute-start.7
  124.4 2.5 %collective-permute-start.8 = (f32[8,32,128]{2,0,1:T(8,128)S(1)}, f32[8,32,128]{2,0,1:T(8,128)S(1)}, u32[]{:S(2)}, u32[]{:S(2)}) collective-permute-start(f32[8,32,128]{2,0,1:T(8,128)S(1)} %bitcast.125), channel_id=1, source_target_pairs={{0,4},{2,6},{4,0},{6,2},{1,5},{3,7},{5,1},{7,3},{8,12},{10,14},{12... | collective-permute-start | bytes 393224 | tf_op jit(solution)/shard_map/ppermute | solution.py:111
  127.0 1.6 %collective-permute-start.9 = (f32[8,32,128]{2,0,1:T(8,128)S(1)}, f32[8,32,128]{2,0,1:T(8,128)S(1)}, u32[]{:S(2)}, u32[]{:S(2)}) collective-permute-start(f32[8,32,128]{2,0,1:T(8,128)S(1)} %bitcast.126), channel_id=1, source_target_pairs={{0,6},{2,0},{4,2},{6,4},{1,7},{3,1},{5,3},{7,5},{8,14},{10,8},{12,... | collective-permute-start | bytes 393224 | tf_op jit(solution)/shard_map/ppermute | solution.py:111
  128.6 18.2 %collective-permute-done.6 = bf16[128,4096]{0,1:T(8,128)(2,1)S(1)} collective-permute-done((bf16[128,4096]{0,1:T(8,128)(2,1)S(1)}, bf16[128,4096]{0,1:T(8,128)(2,1)S(1)}, u32[]{:S(2)}, u32[]{:S(2)}) %collective-permute-start.6) | collective-permute-done | bytes 1048608 | tf_op jit(solution)/shard_map/ppermute | solution.py:13
  146.8 1.3 copy.75
  (90 shorter events, 11.9 us)
Async XLA Ops:
  7.2 2.3 %copy-start.7 = (f32[1,4096]{1,0:T(1,128)S(1)}, f32[1,4096]{1,0:T(1,128)}, u32[]{:S(2)}) copy-start(f32[1,4096]{1,0:T(1,128)} %param.9) | copy-start | bytes 49156
  7.2 49.3 %all-gather.2.cloned.1.call-start = ((), (), s32[]{:S(2)}) async-start(), calls=%async_computation.1 | async-start | bytes 2359296 | tf_op jit(solution)/shard_map/all_gather | solution.py:42
  8.8 2.1 %copy-start.6 = (bf16[1,128,1024]{2,1,0:T(8,128)(2,1)S(1)}, bf16[1,128,1024]{2,1,0:T(8,128)(2,1)}, u32[]{:S(2)}) copy-start(bf16[1,128,1024]{2,1,0:T(8,128)(2,1)} %param.8) | copy-start | bytes 786436
  8.9 2.9 %copy-start.8 = (bf16[1,8,4096]{2,1,0:T(8,128)(2,1)S(1)}, bf16[1,8,4096]{2,1,0:T(8,128)(2,1)}, u32[]{:S(2)}) copy-start(bf16[1,8,4096]{2,1,0:T(8,128)(2,1)} %param.10) | copy-start | bytes 196612
  8.9 4.2 %copy-start.11 = (s32[1,64]{1,0:T(1,128)S(1)}, s32[1,64]{1,0:T(1,128)}, u32[]{:S(2)}) copy-start(s32[1,64]{1,0:T(1,128)} %param.12) | copy-start | bytes 772
  8.9 4.4 %copy-start.9 = (s32[1,64,8]{1,2,0:T(8,128)S(1)}, s32[1,64,8]{1,2,0:T(8,128)}, u32[]{:S(2)}) copy-start(s32[1,64,8]{1,2,0:T(8,128)} %param.11) | copy-start | bytes 6148
  8.9 4.6 %copy-start.10 = (s32[1,512]{1,0:T(1,128)S(1)}, s32[1,512]{1,0:T(1,128)}, u32[]{:S(2)}) copy-start(s32[1,512]{1,0:T(1,128)} %param.13) | copy-start | bytes 6148
  11.0 7.8 %collective-permute-start = (bf16[128,4096]{0,1:T(8,128)(2,1)}, bf16[128,4096]{0,1:T(8,128)(2,1)}, u32[]{:S(2)}, u32[]{:S(2)}) collective-permute-start(bf16[128,4096]{0,1:T(8,128)(2,1)} %fusion.11), channel_id=1, source_target_pairs={{0,1},{1,0},{2,3},{3,2},{4,5},{5,4},{6,7},{7,6},{8,9},{9,8},{10,11... | collective-permute-start | bytes 3145736 | tf_op jit(solution)/shard_map/ppermute | solution.py:18
  11.2 3.1 %collective-permute-start.1 = (bf16[128,1024]{0,1:T(8,128)(2,1)S(1)}, bf16[128,1024]{0,1:T(8,128)(2,1)S(1)}, u32[]{:S(2)}, u32[]{:S(2)}) collective-permute-start(bf16[128,1024]{0,1:T(8,128)(2,1)S(1)} %bitcast.114), channel_id=1, source_target_pairs={{0,1},{1,0},{2,3},{3,2},{4,5},{5,4},{6,7},{7,6},{8,9},{9,8},{10,11... | collective-permute-start | bytes 786440 | tf_op jit(solution)/shard_map/ppermute | solution.py:18
  12.5 109.3 %reduce-scatter.2.cloned.1.call-start = ((), (), s32[]{:S(2)}) async-start(), calls=%async_computation.2 | async-start | bytes 4718592 | tf_op jit(solution)/shard_map/reduce_scatter | solution.py:106
  22.8 4.5 %copy-start.1 = (bf16[16,512,128]{1,2,0:T(8,128)(2,1)S(1)}, bf16[16,512,128]{1,2,0:T(8,128)(2,1)}, u32[]{:S(2)}) copy-start(bf16[16,512,128]{1,2,0:T(8,128)(2,1)} %broadcast_in_dim.114) | copy-start | bytes 6291460
  59.5 15.2 %collective-permute-start.2 = (bf16[64,32,128]{2,1,0:T(8,128)(2,1)S(1)}, bf16[64,32,128]{2,1,0:T(8,128)(2,1)S(1)}, u32[]{:S(2)}, u32[]{:S(2)}) collective-permute-start(bf16[64,32,128]{2,1,0:T(8,128)(2,1)S(1)} %bitcast.108), channel_id=1, source_target_pairs={{0,2},{2,4},{4,6},{6,0},{1,3},{3,5},{5,7},{7,1},{8,10},{10,12},{12... | collective-permute-start | bytes 1572872 | tf_op jit(solution)/shard_map/ppermute | solution.py:102
  61.1 21.3 %collective-permute-start.3 = (bf16[64,32,128]{2,1,0:T(8,128)(2,1)S(1)}, bf16[64,32,128]{2,1,0:T(8,128)(2,1)S(1)}, u32[]{:S(2)}, u32[]{:S(2)}) collective-permute-start(bf16[64,32,128]{2,1,0:T(8,128)(2,1)S(1)} %bitcast.109), channel_id=1, source_target_pairs={{0,4},{2,6},{4,0},{6,2},{1,5},{3,7},{5,1},{7,3},{8,12},{10,14},{12... | collective-permute-start | bytes 1572872 | tf_op jit(solution)/shard_map/ppermute | solution.py:102
  63.8 18.7 %collective-permute-start.4 = (bf16[64,32,128]{2,1,0:T(8,128)(2,1)S(1)}, bf16[64,32,128]{2,1,0:T(8,128)(2,1)S(1)}, u32[]{:S(2)}, u32[]{:S(2)}) collective-permute-start(bf16[64,32,128]{2,1,0:T(8,128)(2,1)S(1)} %bitcast.110), channel_id=1, source_target_pairs={{0,6},{2,0},{4,2},{6,4},{1,7},{3,1},{5,3},{7,5},{8,14},{10,8},{12,... | collective-permute-start | bytes 1572872 | tf_op jit(solution)/shard_map/ppermute | solution.py:102
  82.4 1.7 %copy-start.2 = (bf16[64,32,128]{2,1,0:T(8,128)(2,1)}, bf16[64,32,128]{2,1,0:T(8,128)(2,1)S(1)}, u32[]{:S(2)}) copy-start(bf16[64,32,128]{2,1,0:T(8,128)(2,1)S(1)} %collective-permute-done.3) | copy-start | bytes 1572868
  82.4 1.7 %copy-start.4 = (bf16[64,32,128]{2,1,0:T(8,128)(2,1)}, bf16[64,32,128]{2,1,0:T(8,128)(2,1)S(1)}, u32[]{:S(2)}) copy-start(bf16[64,32,128]{2,1,0:T(8,128)(2,1)S(1)} %collective-permute-done.4) | copy-start | bytes 1572868
  84.1 11.3 %collective-permute-start.5 = (bf16[256,32,128]{2,1,0:T(8,128)(2,1)}, bf16[256,32,128]{2,1,0:T(8,128)(2,1)}, u32[]{:S(2)}, u32[]{:S(2)}) collective-permute-start(bf16[256,32,128]{2,1,0:T(8,128)(2,1)} %pad_maximum_fusion.1), channel_id=1, source_target_pairs={{0,1},{1,0},{2,3},{3,2},{4,5},{5,4},{6,7},{7,6},{8,9},{9,8},{10,11... | collective-permute-start | bytes 6291464 | tf_op jit(solution)/shard_map/ppermute | solution.py:18
  91.9 1.8 %copy-start.3 = (bf16[64,32,128]{2,1,0:T(8,128)(2,1)S(1)}, bf16[64,32,128]{2,1,0:T(8,128)(2,1)}, u32[]{:S(2)}) copy-start(bf16[64,32,128]{2,1,0:T(8,128)(2,1)} %copy-done.2) | copy-start | bytes 1572868
  91.9 2.6 %copy-start.5 = (bf16[64,32,128]{2,1,0:T(8,128)(2,1)S(1)}, bf16[64,32,128]{2,1,0:T(8,128)(2,1)}, u32[]{:S(2)}) copy-start(bf16[64,32,128]{2,1,0:T(8,128)(2,1)} %copy-done.4) | copy-start | bytes 1572868
  98.6 12.2 %copy-start = (f32[128,64,32,2]{0,3,2,1:T(2,128)S(1)}, f32[128,64,32,2]{0,3,2,1:T(2,128)}, u32[]{:S(2)}) copy-start(f32[128,64,32,2]{0,3,2,1:T(2,128)} %convert.4) | copy-start | bytes 6291460
  119.3 27.5 %collective-permute-start.6 = (bf16[128,4096]{0,1:T(8,128)(2,1)S(1)}, bf16[128,4096]{0,1:T(8,128)(2,1)S(1)}, u32[]{:S(2)}, u32[]{:S(2)}) collective-permute-start(bf16[128,4096]{0,1:T(8,128)(2,1)S(1)} %fusion.14), channel_id=1, source_target_pairs={{64,0},{128,64},{192,128},{65,1},{129,65},{193,129},{66,2},{130,66... | collective-permute-start | bytes 3145736 | tf_op jit(solution)/shard_map/ppermute | solution.py:13
  123.0 25.1 %collective-permute-start.7 = (f32[8,32,128]{2,0,1:T(8,128)S(1)}, f32[8,32,128]{2,0,1:T(8,128)S(1)}, u32[]{:S(2)}, u32[]{:S(2)}) collective-permute-start(f32[8,32,128]{2,0,1:T(8,128)S(1)} %bitcast.124), channel_id=1, source_target_pairs={{0,2},{2,4},{4,6},{6,0},{1,3},{3,5},{5,7},{7,1},{8,10},{10,12},{12... | collective-permute-start | bytes 393224 | tf_op jit(solution)/shard_map/ppermute | solution.py:111
  124.4 23.7 %collective-permute-start.8 = (f32[8,32,128]{2,0,1:T(8,128)S(1)}, f32[8,32,128]{2,0,1:T(8,128)S(1)}, u32[]{:S(2)}, u32[]{:S(2)}) collective-permute-start(f32[8,32,128]{2,0,1:T(8,128)S(1)} %bitcast.125), channel_id=1, source_target_pairs={{0,4},{2,6},{4,0},{6,2},{1,5},{3,7},{5,1},{7,3},{8,12},{10,14},{12... | collective-permute-start | bytes 393224 | tf_op jit(solution)/shard_map/ppermute | solution.py:111
  127.0 21.2 %collective-permute-start.9 = (f32[8,32,128]{2,0,1:T(8,128)S(1)}, f32[8,32,128]{2,0,1:T(8,128)S(1)}, u32[]{:S(2)}, u32[]{:S(2)}) collective-permute-start(f32[8,32,128]{2,0,1:T(8,128)S(1)} %bitcast.126), channel_id=1, source_target_pairs={{0,6},{2,0},{4,2},{6,4},{1,7},{3,1},{5,3},{7,5},{8,14},{10,8},{12,... | collective-permute-start | bytes 393224 | tf_op jit(solution)/shard_map/ppermute | solution.py:111
Sparse Core Ops, SparseCore 0:
  12.7 43.7 all-gather.1
  59.6 53.8 reduce-scatter.1

commit v11 on v6

--- a/solution.py
+++ b/solution.py
@@ -102,7 +102,8 @@
     terms, gathered = lax.optimization_barrier((terms, gathered))
     gathered = jnp.concatenate([gathered, sibling(gathered)], axis=0)
     weight_grad = lax.psum_scatter(terms, "z", scatter_dimension=0, tiled=True)
-    weight_grad = lax.psum_scatter(weight_grad, "x", scatter_dimension=0, tiled=True)
+    x_blocks = weight_grad.reshape(nx, slot_dev, half, lanes)
+    weight_grad = jnp.sum(lax.all_to_all(x_blocks, "x", 0, 0), axis=0)
     weight_grad = (weight_grad * grad_scale).reshape(slot_dev, blk * blk)
 
     dense_w = jnp.where(

time: 151 us -> 139 us (0.921)
  waiting for transfers between devices: 53.4 us -> 37.5 us
  starting transfers between devices: 9.21 us -> 13.4 us
    reduce_scatter x1 -> x0, waiting for transfers between devices: 19.7 us -> none  [local(): lax.psum_scatter(weight_grad, 'x', scatter_dimension=0, tiled=True)]
    all_to_all x0 -> x1, waiting for transfers between devices: none -> 8.02 us  [local(): weight_grad = jnp.sum(lax.all_to_all(x_blocks, 'x', 0, 0), axis=0)]
    ppermute x1, waiting for transfers between devices: 4.37 us -> 0.1 us  [shifted(): lax.ppermute(value, axis, [(source, source + steps) for source in range(l...]
    all_to_all x0 -> x1, starting transfers between devices: none -> 4.25 us  [local(): weight_grad = jnp.sum(lax.all_to_all(x_blocks, 'x', 0, 0), axis=0)]
  transfers between devices with their start and end apart: 10 -> 10, of which waited for: 5 -> 5; matrix products, arithmetic and copies ran while one was open for 48% -> 52% of each run, Pallas kernels for 0% -> 0%
where the time goes in v11:
time: 139 us
  local copies, waits for them, and re-layouts  43.3 us (31%)
  waiting for transfers between devices  37.5 us (27%)
  matrix products  15.5 us (11%)
  other arithmetic  14.6 us (11%)
  between operations  14.4 us (10%)
  starting transfers between devices  13.4 us (10%)
    reduce_scatter x1, waiting for transfers between devices, local(): weight_grad = lax.psum_scatter(terms, 'z', scatter_dimension=0, tiled=True)  20.6 us
    gather x1, local copies, waits for them, and re-layouts, local(): gathered[dense_rows]  12.1 us
    dot_general x1, matrix products, local(): jnp.dot(normed_pairs.reshape((panel_list + 1) * half, 2 * pair_tokens), e...  9.68 us
    gather x1, local copies, waits for them, and re-layouts, local(): terms = dense_terms[jnp.where(term_kept, term_index, panel_list * ncol)]  8.81 us
    all_gather x1, waiting for transfers between devices, local(): gathered = lax.all_gather(gathered, 'z', axis=0, tiled=True)  8.51 us
    all_to_all x1, waiting for transfers between devices, local(): weight_grad = jnp.sum(lax.all_to_all(x_blocks, 'x', 0, 0), axis=0)  8.02 us
    dot_general x1, matrix products, local(): jnp.einsum('cthl,pcrl->tprh', expand, dense_w, preferred_element_type=jnp...  5.83 us
    ppermute x3, starting transfers between devices, local(): lax.ppermute(own_tiles, 'x', [(src, (src + s) % nx) for src in range(nx)])  5.73 us
  transfers between devices with their start and end apart: 10, of which 5 were waited for; matrix products, arithmetic and copies ran while one was open for 52% of the time, Pallas kernels for 0%

profile of v11, /device:TPU:8, one launch (start us, length us, event | category | flops | bytes accessed | tf_op | source)
XLA Modules:
  0.0 138.7 jit_solution(3543617154658406379)
XLA Ops:
  7.2 0.9 copy.77
  8.1 1.6 %collective-permute-start.2 = (bf16[8,32,128]{2,1,0:T(8,128)(2,1)S(1)}, bf16[8,32,128]{2,1,0:T(8,128)(2,1)S(1)}, u32[]{:S(2)}, u32[]{:S(2)}) collective-permute-start(bf16[8,32,128]{2,1,0:T(8,128)(2,1)S(1)} %bitcast.97), channel_id=1, source_target_pairs={{0,2},{2,4},{4,6},{6,0},{1,3},{3,5},{5,7},{7,1},{8,10},{10,12},{12... | collective-permute-start | bytes 196616 | tf_op jit(solution)/shard_map/ppermute | solution.py:43
  9.6 2.7 %collective-permute-start.3 = (bf16[8,32,128]{2,1,0:T(8,128)(2,1)S(1)}, bf16[8,32,128]{2,1,0:T(8,128)(2,1)S(1)}, u32[]{:S(2)}, u32[]{:S(2)}) collective-permute-start(bf16[8,32,128]{2,1,0:T(8,128)(2,1)S(1)} %bitcast.98), channel_id=1, source_target_pairs={{0,4},{2,6},{4,0},{6,2},{1,5},{3,7},{5,1},{7,3},{8,12},{10,14},{12... | collective-permute-start | bytes 196616 | tf_op jit(solution)/shard_map/ppermute | solution.py:43
  12.4 1.4 %collective-permute-start.4 = (bf16[8,32,128]{2,1,0:T(8,128)(2,1)S(1)}, bf16[8,32,128]{2,1,0:T(8,128)(2,1)S(1)}, u32[]{:S(2)}, u32[]{:S(2)}) collective-permute-start(bf16[8,32,128]{2,1,0:T(8,128)(2,1)S(1)} %bitcast.99), channel_id=1, source_target_pairs={{0,6},{2,0},{4,2},{6,4},{1,7},{3,1},{5,3},{7,5},{8,14},{10,8},{12,... | collective-permute-start | bytes 196616 | tf_op jit(solution)/shard_map/ppermute | solution.py:43
  13.8 1.6 %copy.52 = bf16[1,128,4096]{1,2,0:T(8,128)(2,1)S(1)} copy(bf16[1,128,4096]{2,1,0:T(8,128)(2,1)} %param.7) | data formatting | bytes 2097152 | tf_op args[0]
  16.0 1.5 %fusion.11 = bf16[128,4096]{0,1:T(8,128)(2,1)} fusion(bf16[1,128,4096]{1,2,0:T(8,128)(2,1)S(1)} %copy.52, f32[4096]{0:T(1024)S(1)} %bitcast.101, f32[128]{0:T(128)S(1)} %get-tuple-element.15), kind=kLoop, calls=%fused_computation.18 | loop fusion | flops 2097152 | bytes 2114048 | tf_op jit(solution)/shard_map/convert_element_type | solution.py:67
  17.7 0.6 collective-permute-start.1
  18.3 0.7 pad_maximum_fusion.4
  21.0 1.7 %broadcast_in_dim.112 = bf16[16,2,256,128]{2,1,3,0:T(2,128)(2,1)S(1)} broadcast(bf16[16,256,128]{1,2,0:T(8,128)(2,1)S(1)} %pad_maximum_fusion.2), dimensions={0,2,3} | broadcast | bytes 3145728 | tf_op jit(solution)/shard_map/jit(_where)/broadcast_in_dim | solution.py:79
  22.7 2.7 %broadcast_in_dim.113 = bf16[16,512,128]{1,2,0:T(8,128)(2,1)} reshape(bf16[16,2,256,128]{2,1,3,0:T(2,128)(2,1)S(1)} %broadcast_in_dim.112) | data formatting | bytes 4194304 | tf_op jit(solution)/shard_map/jit(_where)/broadcast_in_dim | solution.py:79
  25.4 1.8 %pad_maximum_fusion.1 = bf16[256,4096]{0,1:T(8,128)(2,1)S(1)} fusion(bf16[128,4096]{0,1:T(8,128)(2,1)} %collective-permute-done, bf16[128,4096]{0,1:T(8,128)(2,1)} %fusion.11), kind=kLoop, calls=%fused_computation.11 | loop fusion | flops 4194304 | bytes 4194304 | tf_op jit(solution)/shard_map/concatenate | solution.py:69
  27.2 2.3 %reshape.428 = bf16[256,64,32,2]{0,3,2,1:T(2,128)(2,1)} reshape(bf16[256,4096]{0,1:T(8,128)(2,1)S(1)} %pad_maximum_fusion.1) | data formatting | bytes 4194304 | tf_op jit(solution)/shard_map/reshape | solution.py:80
  29.4 4.5 %reshape.429 = bf16[64,32,512]{2,1,0:T(8,128)(2,1)} reshape(bf16[64,32,2,256]{3,2,1,0:T(2,128)(2,1)} %bitcast.88) | data formatting | bytes 4194304 | tf_op jit(solution)/shard_map/reshape | solution.py:81
  34.0 9.7 %fusion.5 = f32[65,32,16,128]{3,1,2,0:T(8,128)} fusion(bf16[64,32,512]{2,1,0:T(8,128)(2,1)} %reshape.429, bf16[16,512,128]{1,2,0:T(8,128)(2,1)S(1)} %copy-done.1, pred[512,128]{0,1:T(8,128)(4,1)S(1)} %copy.55), kind=kOutput, calls=%fused_computation.8 | convolution fusion | flops 4363124736 | bytes 21299200 | tf_op jit(solution)/shard_map/dot_general | solution.py:84
  43.6 8.8 %gather_fusion = f32[256,32,128]{2,1,0:T(8,128)} fusion(f32[1040,32,128]{2,1,0:T(8,128)} %bitcast.93, s32[1024]{0:T(1024)S(1)} %pad_clamp_fusion), kind=kCustom, calls=%fused_computation | custom fusion | bytes 8389632 | tf_op jit(solution)/shard_map/gather | solution.py:101
  52.5 8.5 %all-gather.2.cloned.1.call-done = bf16[256,32,128]{2,1,0:T(8,128)(2,1)} async-done(((bf16[32,32,128]{2,1,0:T(8,128)(2,1)}), bf16[256,32,128]{2,1,0:T(8,128)(2,1)}) %all-gather.2.cloned.1.call-update) | async-done | bytes 2097168 | tf_op jit(solution)/shard_map/all_gather | solution.py:46
  61.9 0.7 reduce.7
  62.9 2.3 %convert.4 = f32[128,64,32,2]{0,3,2,1:T(2,128)} convert(bf16[128,64,32,2]{0,3,2,1:T(2,128)(2,1)S(1)} %bitcast.85) | non-fusion elementwise | flops 524288 | bytes 3145728 | tf_op jit(solution)/shard_map/convert_element_type | solution.py:22
  65.5 1.0 copy.64
  67.0 0.7 reduce.8
  67.7 1.0 mul.163
  69.2 4.6 %pad_maximum_fusion = bf16[512,32,128]{2,1,0:T(8,128)(2,1)} fusion(bf16[256,32,128]{2,1,0:T(8,128)(2,1)} %collective-permute-done.5, bf16[256,32,128]{2,1,0:T(8,128)(2,1)} %all-gather.2.cloned.1.call-done), kind=kLoop, calls=%fused_computation.6 | loop fusion | flops 2097152 | bytes 8388608 | tf_op jit(solution)/shard_map/concatenate | solution.py:103
  73.7 12.1 %gather_fusion.1 = bf16[1024,32,128]{2,1,0:T(8,128)(2,1)} fusion(bf16[512,32,128]{2,1,0:T(8,128)(2,1)} %pad_maximum_fusion, s32[1024]{0:T(1024)S(1)} %broadcast_clamp_fusion), kind=kCustom, calls=%fused_computation.1 | custom fusion | bytes 16781312 | tf_op jit(solution)/shard_map/gather | solution.py:110
  85.9 5.8 %fusion.15 = (f32[128]{0:T(128)S(1)}, f32[128,64,32,2]{0,2,3,1:T(8,128)S(1)}) fusion(f32[128,64,32,2]{0,3,2,1:T(2,128)S(1)} %copy-done, f32[64,32,2]{1,2,0:T(2,128)S(1)} %copy.66, pred[2,128]{1,0:T(4,128)(4,1)S(1)} %iota_compare_fusion.2, bf16[16,128,128]{2,1,0:T(8,128)(2,1)} %copy.64, bf16[64,16,32,128]{3,2,1,0:T(8,128)(2,1)} %bitcast.86, ...), kind=kOutput, calls=%fused_computation.23 | convolution fusion | flops 2153775104 | bytes 13125376 | tf_op jit(solution)/shard_map/cthl,pcrl->tprh/dot_general | solution.py:112
  91.7 1.9 %copy.65 = f32[128,64,32,2]{0,3,2,1:T(2,128)S(1)} copy(f32[128,64,32,2]{0,2,3,1:T(8,128)S(1)} %get-tuple-element.17) | data formatting | bytes 4194304 | tf_op jit(solution)/shard_map/cthl,pcrl->tprh/transpose | solution.py:112
  93.7 0.7 fusion.14
  94.4 2.5 %collective-permute-start.6 = (bf16[128,4096]{0,1:T(8,128)(2,1)S(1)}, bf16[128,4096]{0,1:T(8,128)(2,1)S(1)}, u32[]{:S(2)}, u32[]{:S(2)}) collective-permute-start(bf16[128,4096]{0,1:T(8,128)(2,1)S(1)} %fusion.14), channel_id=1, source_target_pairs={{64,0},{128,64},{192,128},{65,1},{129,65},{193,129},{66,2},{130,66... | collective-permute-start | bytes 3145736 | tf_op jit(solution)/shard_map/ppermute | solution.py:13
  96.9 20.6 %reduce-scatter.2.cloned.1.call-done = f32[32,32,128]{2,1,0:T(8,128)} async-done(((f32[256,32,128]{2,1,0:T(8,128)}), f32[32,32,128]{2,1,0:T(8,128)}) %reduce-scatter.2.cloned.1.call-update) | async-done | bytes 524304 | tf_op jit(solution)/shard_map/reduce_scatter | solution.py:104
  117.5 4.2 %all-to-all-start = ((f32[4,8,32,128]{3,2,1,0:T(8,128)}), f32[4,8,32,128]{3,2,1,0:T(8,128)S(1)}, u32[]{:S(2)}, u32[]{:S(2)}) async-start(f32[4,8,32,128]{3,2,1,0:T(8,128)} %bitcast.94), calls=%async_computation.1 | async-start | bytes 1048576 | tf_op jit(solution)/shard_map/all_to_all | solution.py:106
  121.8 1.3 copy.68
  123.1 8.0 %all-to-all-done = f32[4,8,32,128]{3,2,1,0:T(8,128)S(1)} async-done(((f32[4,8,32,128]{3,2,1,0:T(8,128)}), f32[4,8,32,128]{3,2,1,0:T(8,128)S(1)}, u32[]{:S(2)}, u32[]{:S(2)}) %all-to-all-start) | async-done | bytes 524320 | tf_op jit(solution)/shard_map/all_to_all | solution.py:106
  131.2 0.7 mul.171
  (68 shorter events, 5.3 us)
Async XLA Ops:
  7.2 8.9 %copy-start.3 = (f32[1,4096]{1,0:T(1,128)S(1)}, f32[1,4096]{1,0:T(1,128)}, u32[]{:S(2)}) copy-start(f32[1,4096]{1,0:T(1,128)} %param.9) | copy-start | bytes 49156
  7.2 53.8 %all-gather.2.cloned.1.call-start = ((), (), s32[]{:S(2)}) async-start(), calls=%async_computation.2 | async-start | bytes 2359296 | tf_op jit(solution)/shard_map/all_gather | solution.py:46
  8.1 10.2 %collective-permute-start.2 = (bf16[8,32,128]{2,1,0:T(8,128)(2,1)S(1)}, bf16[8,32,128]{2,1,0:T(8,128)(2,1)S(1)}, u32[]{:S(2)}, u32[]{:S(2)}) collective-permute-start(bf16[8,32,128]{2,1,0:T(8,128)(2,1)S(1)} %bitcast.97), channel_id=1, source_target_pairs={{0,2},{2,4},{4,6},{6,0},{1,3},{3,5},{5,7},{7,1},{8,10},{10,12},{12... | collective-permute-start | bytes 196616 | tf_op jit(solution)/shard_map/ppermute | solution.py:43
  9.6 8.7 %collective-permute-start.3 = (bf16[8,32,128]{2,1,0:T(8,128)(2,1)S(1)}, bf16[8,32,128]{2,1,0:T(8,128)(2,1)S(1)}, u32[]{:S(2)}, u32[]{:S(2)}) collective-permute-start(bf16[8,32,128]{2,1,0:T(8,128)(2,1)S(1)} %bitcast.98), channel_id=1, source_target_pairs={{0,4},{2,6},{4,0},{6,2},{1,5},{3,7},{5,1},{7,3},{8,12},{10,14},{12... | collective-permute-start | bytes 196616 | tf_op jit(solution)/shard_map/ppermute | solution.py:43
  12.4 6.0 %collective-permute-start.4 = (bf16[8,32,128]{2,1,0:T(8,128)(2,1)S(1)}, bf16[8,32,128]{2,1,0:T(8,128)(2,1)S(1)}, u32[]{:S(2)}, u32[]{:S(2)}) collective-permute-start(bf16[8,32,128]{2,1,0:T(8,128)(2,1)S(1)} %bitcast.99), channel_id=1, source_target_pairs={{0,6},{2,0},{4,2},{6,4},{1,7},{3,1},{5,3},{7,5},{8,14},{10,8},{12,... | collective-permute-start | bytes 196616 | tf_op jit(solution)/shard_map/ppermute | solution.py:43
  15.4 2.1 %copy-start.2 = (bf16[1,128,1024]{2,1,0:T(8,128)(2,1)S(1)}, bf16[1,128,1024]{2,1,0:T(8,128)(2,1)}, u32[]{:S(2)}) copy-start(bf16[1,128,1024]{2,1,0:T(8,128)(2,1)} %param.8) | copy-start | bytes 786436
  16.0 3.6 %copy-start.6 = (s32[1,64]{1,0:T(1,128)S(1)}, s32[1,64]{1,0:T(1,128)}, u32[]{:S(2)}) copy-start(s32[1,64]{1,0:T(1,128)} %param.12) | copy-start | bytes 772
  16.0 3.8 %copy-start.4 = (s32[1,64,8]{1,2,0:T(8,128)S(1)}, s32[1,64,8]{1,2,0:T(8,128)}, u32[]{:S(2)}) copy-start(s32[1,64,8]{1,2,0:T(8,128)} %param.11) | copy-start | bytes 6148
  16.0 4.0 %copy-start.5 = (s32[1,512]{1,0:T(1,128)S(1)}, s32[1,512]{1,0:T(1,128)}, u32[]{:S(2)}) copy-start(s32[1,512]{1,0:T(1,128)} %param.13) | copy-start | bytes 6148
  17.5 7.9 %collective-permute-start = (bf16[128,4096]{0,1:T(8,128)(2,1)}, bf16[128,4096]{0,1:T(8,128)(2,1)}, u32[]{:S(2)}, u32[]{:S(2)}) collective-permute-start(bf16[128,4096]{0,1:T(8,128)(2,1)} %fusion.11), channel_id=1, source_target_pairs={{0,1},{1,0},{2,3},{3,2},{4,5},{5,4},{6,7},{7,6},{8,9},{9,8},{10,11... | collective-permute-start | bytes 3145736 | tf_op jit(solution)/shard_map/ppermute | solution.py:18
  17.7 3.1 %collective-permute-start.1 = (bf16[128,1024]{0,1:T(8,128)(2,1)S(1)}, bf16[128,1024]{0,1:T(8,128)(2,1)S(1)}, u32[]{:S(2)}, u32[]{:S(2)}) collective-permute-start(bf16[128,1024]{0,1:T(8,128)(2,1)S(1)} %bitcast.89), channel_id=1, source_target_pairs={{0,1},{1,0},{2,3},{3,2},{4,5},{5,4},{6,7},{7,6},{8,9},{9,8},{10,11... | collective-permute-start | bytes 786440 | tf_op jit(solution)/shard_map/ppermute | solution.py:18
  19.1 98.4 %reduce-scatter.2.cloned.1.call-start = ((), (), s32[]{:S(2)}) async-start(), calls=%async_computation.3 | async-start | bytes 4718592 | tf_op jit(solution)/shard_map/reduce_scatter | solution.py:104
  29.4 4.5 %copy-start.1 = (bf16[16,512,128]{1,2,0:T(8,128)(2,1)S(1)}, bf16[16,512,128]{1,2,0:T(8,128)(2,1)}, u32[]{:S(2)}) copy-start(bf16[16,512,128]{1,2,0:T(8,128)(2,1)} %broadcast_in_dim.113) | copy-start | bytes 6291460
  61.0 8.2 %collective-permute-start.5 = (bf16[256,32,128]{2,1,0:T(8,128)(2,1)}, bf16[256,32,128]{2,1,0:T(8,128)(2,1)}, u32[]{:S(2)}, u32[]{:S(2)}) collective-permute-start(bf16[256,32,128]{2,1,0:T(8,128)(2,1)} %all-gather.2.cloned.1.call-done), channel_id=1, source_target_pairs={{0,1},{1,0},{2,3},{3,2},{4,5},{5,4},{6,7},{7,6},{8,9},{9,8},{10,11... | collective-permute-start | bytes 6291464 | tf_op jit(solution)/shard_map/ppermute | solution.py:18
  73.7 12.1 %copy-start = (f32[128,64,32,2]{0,3,2,1:T(2,128)S(1)}, f32[128,64,32,2]{0,3,2,1:T(2,128)}, u32[]{:S(2)}) copy-start(f32[128,64,32,2]{0,3,2,1:T(2,128)} %convert.4) | copy-start | bytes 6291460
  94.4 27.4 %collective-permute-start.6 = (bf16[128,4096]{0,1:T(8,128)(2,1)S(1)}, bf16[128,4096]{0,1:T(8,128)(2,1)S(1)}, u32[]{:S(2)}, u32[]{:S(2)}) collective-permute-start(bf16[128,4096]{0,1:T(8,128)(2,1)S(1)} %fusion.14), channel_id=1, source_target_pairs={{64,0},{128,64},{192,128},{65,1},{129,65},{193,129},{66,2},{130,66... | collective-permute-start | bytes 3145736 | tf_op jit(solution)/shard_map/ppermute | solution.py:13
  117.5 13.7 %all-to-all-start = ((f32[4,8,32,128]{3,2,1,0:T(8,128)}), f32[4,8,32,128]{3,2,1,0:T(8,128)S(1)}, u32[]{:S(2)}, u32[]{:S(2)}) async-start(f32[4,8,32,128]{3,2,1,0:T(8,128)} %bitcast.94), calls=%async_computation.1 | async-start | bytes 1048576 | tf_op jit(solution)/shard_map/all_to_all | solution.py:106
Sparse Core Ops, SparseCore 0:
  19.2 41.7 all-gather.1
  63.5 53.8 reduce-scatter.1

commit v12 on v11

--- a/solution.py
+++ b/solution.py
@@ -91,20 +91,22 @@
     oz = jnp.arange(nz)[:, None, None]
     ox = jnp.arange(nx)[None, :, None]
     oj = jnp.arange(slot_dev)[None, None, :]
-    rs_order = (((oz * nx + ox) * nc + my_core) * slot_dev + oj).reshape(-1)
+    rs_order = (((oz * nx + (ox + my_x) % nx) * nc + my_core) * slot_dev + oj).reshape(-1)
     slot_match = slot_lookup[None, :] == rs_order[:, None]
     pos_panel = jnp.arange(store_slots, dtype=jnp.int32) // most_kept
     pos_index = pos_panel * ncol + column_list.reshape(-1)
     pos_kept = kept_grid.reshape(-1)
     term_index = jnp.sum(jnp.where(slot_match, pos_index[None, :], 0), axis=1)
     term_kept = jnp.any(slot_match & pos_kept[None, :], axis=1)
-    terms = dense_terms[jnp.where(term_kept, term_index, panel_list * ncol)]
+    terms = dense_terms[jnp.where(term_kept, term_index, panel_list * ncol)] * grad_scale
     terms, gathered = lax.optimization_barrier((terms, gathered))
     gathered = jnp.concatenate([gathered, sibling(gathered)], axis=0)
     weight_grad = lax.psum_scatter(terms, "z", scatter_dimension=0, tiled=True)
     x_blocks = weight_grad.reshape(nx, slot_dev, half, lanes)
-    weight_grad = jnp.sum(lax.all_to_all(x_blocks, "x", 0, 0), axis=0)
-    weight_grad = (weight_grad * grad_scale).reshape(slot_dev, blk * blk)
+    own_sum = x_blocks[0]
+    for s in range(1, nx):
+        own_sum = own_sum + lax.ppermute(x_blocks[s], "x", [(src, (src + s) % nx) for src in range(nx)])
+    weight_grad = own_sum.reshape(slot_dev, blk * blk)
 
     dense_w = jnp.where(
         has_tile.reshape(-1)[:, None, None], gathered[dense_rows], jnp.zeros((), gathered.dtype)

time: 139 us -> 138 us (level)
  waiting for transfers between devices: 37.5 us -> 27.8 us
  other arithmetic: 14.6 us -> 20.3 us
  starting transfers between devices: 13.4 us -> 14.8 us
    all_to_all x1 -> x0, waiting for transfers between devices: 8.02 us -> none  [local(): weight_grad = jnp.sum(lax.all_to_all(x_blocks, 'x', 0, 0), axis=0)]
    ppermute x0 -> x3, starting transfers between devices: none -> 5.69 us  [local(): lax.ppermute(x_blocks[s], 'x', [(src, (src + s) % nx) for src in range(nx)])]
    all_gather x1, waiting for transfers between devices: 8.51 us -> 3.72 us  [local(): gathered = lax.all_gather(gathered, 'z', axis=0, tiled=True)]
    mul x3, other arithmetic: 0.1 us -> 4.85 us  [the longest x1 4.78 us: local(): dense_terms[jnp.where(term_kept, term_index, panel_list * ncol)]]
    all_to_all x1 -> x0, starting transfers between devices: 4.25 us -> none  [local(): weight_grad = jnp.sum(lax.all_to_all(x_blocks, 'x', 0, 0), axis=0)]
    ppermute x0 -> x3, waiting for transfers between devices: none -> 3.21 us  [local(): lax.ppermute(x_blocks[s], 'x', [(src, (src + s) % nx) for src in range(nx)])]
  transfers between devices with their start and end apart: 10 -> 12, of which waited for: 5 -> 4; matrix products, arithmetic and copies ran while one was open for 52% -> 57% of each run, Pallas kernels for 0% -> 0%
where the time goes in v12:
time: 138 us; the launch traced here: 137 us
  local copies, waits for them, and re-layouts  44.3 us (32%)
  waiting for transfers between devices  27.8 us (20%)
  other arithmetic  20.3 us (15%)
  matrix products  15.5 us (11%)
  starting transfers between devices  14.8 us (11%)
  between operations  14.4 us (10%)
    reduce_scatter x1, waiting for transfers between devices, local(): weight_grad = lax.psum_scatter(terms, 'z', scatter_dimension=0, tiled=True)  20.5 us
    gather x1, local copies, waits for them, and re-layouts, local(): gathered[dense_rows]  12.1 us
    dot_general x1, matrix products, local(): jnp.dot(normed_pairs.reshape((panel_list + 1) * half, 2 * pair_tokens), e...  9.68 us
    gather x1, local copies, waits for them, and re-layouts, local(): dense_terms[jnp.where(term_kept, term_index, panel_list * ncol)]  8.81 us
    dot_general x1, matrix products, local(): jnp.einsum('cthl,pcrl->tprh', expand, dense_w, preferred_element_type=jnp...  5.83 us
    ppermute x3, starting transfers between devices, local(): lax.ppermute(own_tiles, 'x', [(src, (src + s) % nx) for src in range(nx)])  5.73 us
    ppermute x3, starting transfers between devices, local(): lax.ppermute(x_blocks[s], 'x', [(src, (src + s) % nx) for src in range(nx)])  5.69 us
    unnamed x21, local copies, waits for them, and re-layouts  5.09 us
  transfers between devices with their start and end apart: 12, of which 4 were waited for; matrix products, arithmetic and copies ran while one was open for 57% of the time, Pallas kernels for 0%

profile of v12, /device:TPU:8, one launch (start us, length us, event | category | flops | bytes accessed | tf_op | source)
XLA Modules:
  0.0 137.1 jit_solution(7794441225490683994)
XLA Ops:
  7.2 0.9 copy.77
  8.1 1.6 %collective-permute-start.2 = (bf16[8,32,128]{2,1,0:T(8,128)(2,1)S(1)}, bf16[8,32,128]{2,1,0:T(8,128)(2,1)S(1)}, u32[]{:S(2)}, u32[]{:S(2)}) collective-permute-start(bf16[8,32,128]{2,1,0:T(8,128)(2,1)S(1)} %bitcast.95), channel_id=1, source_target_pairs={{0,2},{2,4},{4,6},{6,0},{1,3},{3,5},{5,7},{7,1},{8,10},{10,12},{12... | collective-permute-start | bytes 196616 | tf_op jit(solution)/shard_map/ppermute | solution.py:43
  9.6 2.7 %collective-permute-start.3 = (bf16[8,32,128]{2,1,0:T(8,128)(2,1)S(1)}, bf16[8,32,128]{2,1,0:T(8,128)(2,1)S(1)}, u32[]{:S(2)}, u32[]{:S(2)}) collective-permute-start(bf16[8,32,128]{2,1,0:T(8,128)(2,1)S(1)} %bitcast.96), channel_id=1, source_target_pairs={{0,4},{2,6},{4,0},{6,2},{1,5},{3,7},{5,1},{7,3},{8,12},{10,14},{12... | collective-permute-start | bytes 196616 | tf_op jit(solution)/shard_map/ppermute | solution.py:43
  12.4 1.4 %collective-permute-start.4 = (bf16[8,32,128]{2,1,0:T(8,128)(2,1)S(1)}, bf16[8,32,128]{2,1,0:T(8,128)(2,1)S(1)}, u32[]{:S(2)}, u32[]{:S(2)}) collective-permute-start(bf16[8,32,128]{2,1,0:T(8,128)(2,1)S(1)} %bitcast.97), channel_id=1, source_target_pairs={{0,6},{2,0},{4,2},{6,4},{1,7},{3,1},{5,3},{7,5},{8,14},{10,8},{12,... | collective-permute-start | bytes 196616 | tf_op jit(solution)/shard_map/ppermute | solution.py:43
  13.8 1.6 %copy.52 = bf16[1,128,4096]{1,2,0:T(8,128)(2,1)S(1)} copy(bf16[1,128,4096]{2,1,0:T(8,128)(2,1)} %param.7) | data formatting | bytes 2097152 | tf_op args[0]
  16.0 1.5 %fusion.11 = bf16[128,4096]{0,1:T(8,128)(2,1)} fusion(bf16[1,128,4096]{1,2,0:T(8,128)(2,1)S(1)} %copy.52, f32[4096]{0:T(1024)S(1)} %bitcast.99, f32[128]{0:T(128)S(1)} %get-tuple-element.18), kind=kLoop, calls=%fused_computation.18 | loop fusion | flops 2097152 | bytes 2114048 | tf_op jit(solution)/shard_map/convert_element_type | solution.py:67
  18.6 0.7 pad_maximum_fusion.4
  21.0 1.7 %broadcast_in_dim.112 = bf16[16,2,256,128]{2,1,3,0:T(2,128)(2,1)S(1)} broadcast(bf16[16,256,128]{1,2,0:T(8,128)(2,1)S(1)} %pad_maximum_fusion.2), dimensions={0,2,3} | broadcast | bytes 3145728 | tf_op jit(solution)/shard_map/jit(_where)/broadcast_in_dim | solution.py:79
  22.7 2.7 %broadcast_in_dim.113 = bf16[16,512,128]{1,2,0:T(8,128)(2,1)} reshape(bf16[16,2,256,128]{2,1,3,0:T(2,128)(2,1)S(1)} %broadcast_in_dim.112) | data formatting | bytes 4194304 | tf_op jit(solution)/shard_map/jit(_where)/broadcast_in_dim | solution.py:79
  25.4 1.8 %pad_maximum_fusion.1 = bf16[256,4096]{0,1:T(8,128)(2,1)S(1)} fusion(bf16[128,4096]{0,1:T(8,128)(2,1)} %collective-permute-done, bf16[128,4096]{0,1:T(8,128)(2,1)} %fusion.11), kind=kLoop, calls=%fused_computation.11 | loop fusion | flops 4194304 | bytes 4194304 | tf_op jit(solution)/shard_map/concatenate | solution.py:69
  27.2 2.3 %reshape.452 = bf16[256,64,32,2]{0,3,2,1:T(2,128)(2,1)} reshape(bf16[256,4096]{0,1:T(8,128)(2,1)S(1)} %pad_maximum_fusion.1) | data formatting | bytes 4194304 | tf_op jit(solution)/shard_map/reshape | solution.py:80
  29.4 4.5 %reshape.453 = bf16[64,32,512]{2,1,0:T(8,128)(2,1)} reshape(bf16[64,32,2,256]{3,2,1,0:T(2,128)(2,1)} %bitcast.87) | data formatting | bytes 4194304 | tf_op jit(solution)/shard_map/reshape | solution.py:81
  34.0 9.7 %fusion.5 = f32[65,32,16,128]{3,1,2,0:T(8,128)} fusion(bf16[64,32,512]{2,1,0:T(8,128)(2,1)} %reshape.453, bf16[16,512,128]{1,2,0:T(8,128)(2,1)S(1)} %copy-done.1, pred[512,128]{0,1:T(8,128)(4,1)S(1)} %copy.55), kind=kOutput, calls=%fused_computation.8 | convolution fusion | flops 4363124736 | bytes 21299200 | tf_op jit(solution)/shard_map/dot_general | solution.py:84
  43.6 8.8 %gather_fusion = f32[256,32,128]{2,1,0:T(8,128)} fusion(f32[1040,32,128]{2,1,0:T(8,128)} %bitcast.92, s32[1024]{0:T(1024)S(1)} %pad_clamp_fusion), kind=kCustom, calls=%fused_computation | custom fusion | bytes 8389632 | tf_op jit(solution)/shard_map/gather | solution.py:101
  52.5 4.8 %broadcast_multiply_fusion = f32[256,32,128]{2,1,0:T(8,128)} fusion(f32[256,32,128]{2,1,0:T(8,128)} %gather_fusion), kind=kLoop, calls=%fused_computation.24 | loop fusion | flops 1048576 | bytes 8388608 | tf_op jit(solution)/shard_map/mul | solution.py:101
  57.2 3.7 %all-gather.2.cloned.1.call-done = bf16[256,32,128]{2,1,0:T(8,128)(2,1)} async-done(((bf16[32,32,128]{2,1,0:T(8,128)(2,1)}), bf16[256,32,128]{2,1,0:T(8,128)(2,1)}) %all-gather.2.cloned.1.call-update) | async-done | bytes 2097168 | tf_op jit(solution)/shard_map/all_gather | solution.py:46
  62.9 2.3 %convert.4 = f32[128,64,32,2]{0,3,2,1:T(2,128)} convert(bf16[128,64,32,2]{0,3,2,1:T(2,128)(2,1)S(1)} %bitcast.84) | non-fusion elementwise | flops 524288 | bytes 3145728 | tf_op jit(solution)/shard_map/convert_element_type | solution.py:22
  65.4 1.0 copy.64
  67.6 1.0 mul.155
  69.2 4.6 %pad_maximum_fusion = bf16[512,32,128]{2,1,0:T(8,128)(2,1)} fusion(bf16[256,32,128]{2,1,0:T(8,128)(2,1)} %collective-permute-done.5, bf16[256,32,128]{2,1,0:T(8,128)(2,1)} %all-gather.2.cloned.1.call-done), kind=kLoop, calls=%fused_computation.6 | loop fusion | flops 2097152 | bytes 8388608 | tf_op jit(solution)/shard_map/concatenate | solution.py:103
  73.7 12.1 %gather_fusion.1 = bf16[1024,32,128]{2,1,0:T(8,128)(2,1)} fusion(bf16[512,32,128]{2,1,0:T(8,128)(2,1)} %pad_maximum_fusion, s32[1024]{0:T(1024)S(1)} %broadcast_clamp_fusion), kind=kCustom, calls=%fused_computation.1 | custom fusion | bytes 16781312 | tf_op jit(solution)/shard_map/gather | solution.py:112
  85.9 5.8 %fusion.15 = (f32[128]{0:T(128)S(1)}, f32[128,64,32,2]{0,2,3,1:T(8,128)S(1)}) fusion(f32[128,64,32,2]{0,3,2,1:T(2,128)S(1)} %copy-done, f32[64,32,2]{1,2,0:T(2,128)S(1)} %copy.66, pred[2,128]{1,0:T(4,128)(4,1)S(1)} %iota_compare_fusion.2, bf16[16,128,128]{2,1,0:T(8,128)(2,1)} %copy.64, bf16[64,16,32,128]{3,2,1,0:T(8,128)(2,1)} %bitcast.85, ...), kind=kOutput, calls=%fused_computation.23 | convolution fusion | flops 2153775104 | bytes 13125376 | tf_op jit(solution)/shard_map/cthl,pcrl->tprh/dot_general | solution.py:114
  91.7 1.9 %copy.65 = f32[128,64,32,2]{0,3,2,1:T(2,128)S(1)} copy(f32[128,64,32,2]{0,2,3,1:T(8,128)S(1)} %get-tuple-element.20) | data formatting | bytes 4194304 | tf_op jit(solution)/shard_map/cthl,pcrl->tprh/transpose | solution.py:114
  94.4 2.5 %collective-permute-start.6 = (bf16[128,4096]{0,1:T(8,128)(2,1)S(1)}, bf16[128,4096]{0,1:T(8,128)(2,1)S(1)}, u32[]{:S(2)}, u32[]{:S(2)}) collective-permute-start(bf16[128,4096]{0,1:T(8,128)(2,1)S(1)} %fusion.14), channel_id=1, source_target_pairs={{64,0},{128,64},{192,128},{65,1},{129,65},{193,129},{66,2},{130,66... | collective-permute-start | bytes 3145736 | tf_op jit(solution)/shard_map/ppermute | solution.py:13
  96.8 20.5 %reduce-scatter.2.cloned.1.call-done = f32[32,32,128]{2,1,0:T(8,128)} async-done(((f32[256,32,128]{2,1,0:T(8,128)}), f32[32,32,128]{2,1,0:T(8,128)}) %reduce-scatter.2.cloned.1.call-update) | async-done | bytes 524304 | tf_op jit(solution)/shard_map/reduce_scatter | solution.py:104
  117.4 1.1 fusion.56
  118.4 1.5 %collective-permute-start.7 = (f32[8,32,128]{2,1,0:T(8,128)S(1)}, f32[8,32,128]{2,1,0:T(8,128)S(1)}, u32[]{:S(2)}, u32[]{:S(2)}) collective-permute-start(f32[8,32,128]{2,1,0:T(8,128)S(1)} %get-tuple-element.14), channel_id=1, source_target_pairs={{0,2},{2,4},{4,6},{6,0},{1,3},{3,5},{5,7},{7,1},{8,10},{10,12},{12... | collective-permute-start | bytes 393224 | tf_op jit(solution)/shard_map/ppermute | solution.py:108
  120.0 2.7 %collective-permute-start.8 = (f32[8,32,128]{2,1,0:T(8,128)S(1)}, f32[8,32,128]{2,1,0:T(8,128)S(1)}, u32[]{:S(2)}, u32[]{:S(2)}) collective-permute-start(f32[8,32,128]{2,1,0:T(8,128)S(1)} %get-tuple-element.16), channel_id=1, source_target_pairs={{0,4},{2,6},{4,0},{6,2},{1,5},{3,7},{5,1},{7,3},{8,12},{10,14},{12... | collective-permute-start | bytes 393224 | tf_op jit(solution)/shard_map/ppermute | solution.py:108
  122.7 1.5 %collective-permute-start.9 = (f32[8,32,128]{2,1,0:T(8,128)S(1)}, f32[8,32,128]{2,1,0:T(8,128)S(1)}, u32[]{:S(2)}, u32[]{:S(2)}) collective-permute-start(f32[8,32,128]{2,1,0:T(8,128)S(1)} %get-tuple-element.15), channel_id=1, source_target_pairs={{0,6},{2,0},{4,2},{6,4},{1,7},{3,1},{5,3},{7,5},{8,14},{10,8},{12,... | collective-permute-start | bytes 393224 | tf_op jit(solution)/shard_map/ppermute | solution.py:108
  124.1 1.3 copy.68
  125.4 3.2 %collective-permute-done.8 = f32[8,32,128]{2,1,0:T(8,128)S(1)} collective-permute-done((f32[8,32,128]{2,1,0:T(8,128)S(1)}, f32[8,32,128]{2,1,0:T(8,128)S(1)}, u32[]{:S(2)}, u32[]{:S(2)}) %collective-permute-start.8) | collective-permute-done | bytes 131104 | tf_op jit(solution)/shard_map/ppermute | solution.py:108
  128.6 0.9 fusion.30
  (74 shorter events, 8.5 us)
Async XLA Ops:
  7.2 8.9 %copy-start.3 = (f32[1,4096]{1,0:T(1,128)S(1)}, f32[1,4096]{1,0:T(1,128)}, u32[]{:S(2)}) copy-start(f32[1,4096]{1,0:T(1,128)} %param.9) | copy-start | bytes 49156
  7.2 53.8 %all-gather.2.cloned.1.call-start = ((), (), s32[]{:S(2)}) async-start(), calls=%async_computation.1 | async-start | bytes 2359296 | tf_op jit(solution)/shard_map/all_gather | solution.py:46
  8.1 10.5 %collective-permute-start.2 = (bf16[8,32,128]{2,1,0:T(8,128)(2,1)S(1)}, bf16[8,32,128]{2,1,0:T(8,128)(2,1)S(1)}, u32[]{:S(2)}, u32[]{:S(2)}) collective-permute-start(bf16[8,32,128]{2,1,0:T(8,128)(2,1)S(1)} %bitcast.95), channel_id=1, source_target_pairs={{0,2},{2,4},{4,6},{6,0},{1,3},{3,5},{5,7},{7,1},{8,10},{10,12},{12... | collective-permute-start | bytes 196616 | tf_op jit(solution)/shard_map/ppermute | solution.py:43
  9.6 8.9 %collective-permute-start.3 = (bf16[8,32,128]{2,1,0:T(8,128)(2,1)S(1)}, bf16[8,32,128]{2,1,0:T(8,128)(2,1)S(1)}, u32[]{:S(2)}, u32[]{:S(2)}) collective-permute-start(bf16[8,32,128]{2,1,0:T(8,128)(2,1)S(1)} %bitcast.96), channel_id=1, source_target_pairs={{0,4},{2,6},{4,0},{6,2},{1,5},{3,7},{5,1},{7,3},{8,12},{10,14},{12... | collective-permute-start | bytes 196616 | tf_op jit(solution)/shard_map/ppermute | solution.py:43
  12.4 6.2 %collective-permute-start.4 = (bf16[8,32,128]{2,1,0:T(8,128)(2,1)S(1)}, bf16[8,32,128]{2,1,0:T(8,128)(2,1)S(1)}, u32[]{:S(2)}, u32[]{:S(2)}) collective-permute-start(bf16[8,32,128]{2,1,0:T(8,128)(2,1)S(1)} %bitcast.97), channel_id=1, source_target_pairs={{0,6},{2,0},{4,2},{6,4},{1,7},{3,1},{5,3},{7,5},{8,14},{10,8},{12,... | collective-permute-start | bytes 196616 | tf_op jit(solution)/shard_map/ppermute | solution.py:43
  15.4 2.1 %copy-start.2 = (bf16[1,128,1024]{2,1,0:T(8,128)(2,1)S(1)}, bf16[1,128,1024]{2,1,0:T(8,128)(2,1)}, u32[]{:S(2)}) copy-start(bf16[1,128,1024]{2,1,0:T(8,128)(2,1)} %param.8) | copy-start | bytes 786436
  16.0 3.6 %copy-start.6 = (s32[1,64]{1,0:T(1,128)S(1)}, s32[1,64]{1,0:T(1,128)}, u32[]{:S(2)}) copy-start(s32[1,64]{1,0:T(1,128)} %param.12) | copy-start | bytes 772
  16.0 3.8 %copy-start.4 = (s32[1,64,8]{1,2,0:T(8,128)S(1)}, s32[1,64,8]{1,2,0:T(8,128)}, u32[]{:S(2)}) copy-start(s32[1,64,8]{1,2,0:T(8,128)} %param.11) | copy-start | bytes 6148
  16.0 4.0 %copy-start.5 = (s32[1,512]{1,0:T(1,128)S(1)}, s32[1,512]{1,0:T(1,128)}, u32[]{:S(2)}) copy-start(s32[1,512]{1,0:T(1,128)} %param.13) | copy-start | bytes 6148
  17.5 7.8 %collective-permute-start = (bf16[128,4096]{0,1:T(8,128)(2,1)}, bf16[128,4096]{0,1:T(8,128)(2,1)}, u32[]{:S(2)}, u32[]{:S(2)}) collective-permute-start(bf16[128,4096]{0,1:T(8,128)(2,1)} %fusion.11), channel_id=1, source_target_pairs={{0,1},{1,0},{2,3},{3,2},{4,5},{5,4},{6,7},{7,6},{8,9},{9,8},{10,11... | collective-permute-start | bytes 3145736 | tf_op jit(solution)/shard_map/ppermute | solution.py:18
  17.7 3.1 %collective-permute-start.1 = (bf16[128,1024]{0,1:T(8,128)(2,1)S(1)}, bf16[128,1024]{0,1:T(8,128)(2,1)S(1)}, u32[]{:S(2)}, u32[]{:S(2)}) collective-permute-start(bf16[128,1024]{0,1:T(8,128)(2,1)S(1)} %bitcast.88), channel_id=1, source_target_pairs={{0,1},{1,0},{2,3},{3,2},{4,5},{5,4},{6,7},{7,6},{8,9},{9,8},{10,11... | collective-permute-start | bytes 786440 | tf_op jit(solution)/shard_map/ppermute | solution.py:18
  19.3 98.0 %reduce-scatter.2.cloned.1.call-start = ((), (), s32[]{:S(2)}) async-start(), calls=%async_computation.2 | async-start | bytes 4718592 | tf_op jit(solution)/shard_map/reduce_scatter | solution.py:104
  29.4 4.5 %copy-start.1 = (bf16[16,512,128]{1,2,0:T(8,128)(2,1)S(1)}, bf16[16,512,128]{1,2,0:T(8,128)(2,1)}, u32[]{:S(2)}) copy-start(bf16[16,512,128]{1,2,0:T(8,128)(2,1)} %broadcast_in_dim.113) | copy-start | bytes 6291460
  61.0 8.2 %collective-permute-start.5 = (bf16[256,32,128]{2,1,0:T(8,128)(2,1)}, bf16[256,32,128]{2,1,0:T(8,128)(2,1)}, u32[]{:S(2)}, u32[]{:S(2)}) collective-permute-start(bf16[256,32,128]{2,1,0:T(8,128)(2,1)} %all-gather.2.cloned.1.call-done), channel_id=1, source_target_pairs={{0,1},{1,0},{2,3},{3,2},{4,5},{5,4},{6,7},{7,6},{8,9},{9,8},{10,11... | collective-permute-start | bytes 6291464 | tf_op jit(solution)/shard_map/ppermute | solution.py:18
  73.7 12.1 %copy-start = (f32[128,64,32,2]{0,3,2,1:T(2,128)S(1)}, f32[128,64,32,2]{0,3,2,1:T(2,128)}, u32[]{:S(2)}) copy-start(f32[128,64,32,2]{0,3,2,1:T(2,128)} %convert.4) | copy-start | bytes 6291460
  94.4 29.8 %collective-permute-start.6 = (bf16[128,4096]{0,1:T(8,128)(2,1)S(1)}, bf16[128,4096]{0,1:T(8,128)(2,1)S(1)}, u32[]{:S(2)}, u32[]{:S(2)}) collective-permute-start(bf16[128,4096]{0,1:T(8,128)(2,1)S(1)} %fusion.14), channel_id=1, source_target_pairs={{64,0},{128,64},{192,128},{65,1},{129,65},{193,129},{66,2},{130,66... | collective-permute-start | bytes 3145736 | tf_op jit(solution)/shard_map/ppermute | solution.py:13
  118.4 7.0 %collective-permute-start.7 = (f32[8,32,128]{2,1,0:T(8,128)S(1)}, f32[8,32,128]{2,1,0:T(8,128)S(1)}, u32[]{:S(2)}, u32[]{:S(2)}) collective-permute-start(f32[8,32,128]{2,1,0:T(8,128)S(1)} %get-tuple-element.14), channel_id=1, source_target_pairs={{0,2},{2,4},{4,6},{6,0},{1,3},{3,5},{5,7},{7,1},{8,10},{10,12},{12... | collective-permute-start | bytes 393224 | tf_op jit(solution)/shard_map/ppermute | solution.py:108
  120.0 8.7 %collective-permute-start.8 = (f32[8,32,128]{2,1,0:T(8,128)S(1)}, f32[8,32,128]{2,1,0:T(8,128)S(1)}, u32[]{:S(2)}, u32[]{:S(2)}) collective-permute-start(f32[8,32,128]{2,1,0:T(8,128)S(1)} %get-tuple-element.16), channel_id=1, source_target_pairs={{0,4},{2,6},{4,0},{6,2},{1,5},{3,7},{5,1},{7,3},{8,12},{10,14},{12... | collective-permute-start | bytes 393224 | tf_op jit(solution)/shard_map/ppermute | solution.py:108
  122.7 6.0 %collective-permute-start.9 = (f32[8,32,128]{2,1,0:T(8,128)S(1)}, f32[8,32,128]{2,1,0:T(8,128)S(1)}, u32[]{:S(2)}, u32[]{:S(2)}) collective-permute-start(f32[8,32,128]{2,1,0:T(8,128)S(1)} %get-tuple-element.15), channel_id=1, source_target_pairs={{0,6},{2,0},{4,2},{6,4},{1,7},{3,1},{5,3},{7,5},{8,14},{10,8},{12,... | collective-permute-start | bytes 393224 | tf_op jit(solution)/shard_map/ppermute | solution.py:108
Sparse Core Ops, SparseCore 0:
  19.5 41.4 all-gather.1
  63.5 53.8 reduce-scatter.1

commit v13 on v7

--- a/solution.py
+++ b/solution.py
@@ -38,11 +38,8 @@
     grad_scale = (tok_rows * nz * nx * nc) ** (-0.5)
 
     own_tiles = tiles[0].reshape(slot_dev, half, lanes)
-    gathered = jnp.concatenate(
-        [own_tiles]
-        + [lax.ppermute(own_tiles, "x", [(src, (src + s) % nx) for src in range(nx)]) for s in range(1, nx)],
-        axis=0,
-    )
+    copies = jnp.broadcast_to(own_tiles[None], (nx,) + own_tiles.shape)
+    gathered = lax.all_to_all(copies, "x", 0, 0).reshape(nx * slot_dev, half, lanes)
     gathered = lax.all_gather(gathered, "z", axis=0, tiled=True)
     slot_ids = jnp.arange(store_slots, dtype=jnp.int32)
 
@@ -53,7 +50,7 @@
         holder = slot // slot_dev
         half_of = (holder % nc - my_core) % nc
         chip = holder // nc
-        shift = (my_x - chip % nx) % nx
+        shift = chip % nx
         return half_of * (nz * nx * slot_dev) + ((chip // nx) * nx + shift) * slot_dev + slot % slot_dev
 
     kept_grid = jnp.arange(most_kept)[None, :] < count_list[:, None]

time: 137 us -> 139 us (1.015)
  waiting for transfers between devices: 32.3 us -> 34.9 us
  local copies, waits for them, and re-layouts: 43.9 us -> 45.4 us
  starting transfers between devices: 15 us -> 13.5 us
    ppermute x3 -> x0, starting transfers between devices: 5.73 us -> none  [local(): lax.ppermute(own_tiles, 'x', [(src, (src + s) % nx) for src in range(nx)])]
    all_to_all x0 -> x1, starting transfers between devices: none -> 4.29 us  [local(): lax.all_to_all(copies, 'x', 0, 0).reshape(nx * slot_dev, half, lanes)]
    all_to_all x0 -> x1, waiting for transfers between devices: none -> 2.17 us  [local(): lax.all_to_all(copies, 'x', 0, 0).reshape(nx * slot_dev, half, lanes)]
    broadcast_in_dim x0 -> x2, local copies, waits for them, and re-layouts: none -> 1.59 us  [local(): copies = jnp.broadcast_to(own_tiles[None], (nx,) + own_tiles.shape)]
    unnamed x21 -> x22, local copies, waits for them, and re-layouts: 5.09 us -> 4.94 us
  transfers between devices with their start and end apart: 12 -> 10, of which waited for: 4 -> 4; matrix products, arithmetic and copies ran while one was open for 54% -> 52% of each run, Pallas kernels for 0% -> 0%
where the time goes in v13:
time: 139 us; the launch traced here: 138 us
  local copies, waits for them, and re-layouts  45.4 us (33%)
  waiting for transfers between devices  34.9 us (25%)
  matrix products  15.5 us (11%)
  other arithmetic  14.6 us (11%)
  between operations  14.4 us (10%)
  starting transfers between devices  13.5 us (10%)
    reduce_scatter x1, waiting for transfers between devices, local(): weight_grad = lax.psum_scatter(terms, 'z', scatter_dimension=0, tiled=True)  20.5 us
    gather x1, local copies, waits for them, and re-layouts, local(): gathered[dense_rows]  12.1 us
    dot_general x1, matrix products, local(): jnp.dot(normed_pairs.reshape((panel_list + 1) * half, 2 * pair_tokens), e...  9.65 us
    all_gather x1, waiting for transfers between devices, local(): gathered = lax.all_gather(gathered, 'z', axis=0, tiled=True)  9.26 us
    gather x1, local copies, waits for them, and re-layouts, local(): terms = dense_terms[jnp.where(term_kept, term_index, panel_list * ncol)]  8.79 us
    ppermute x3, starting transfers between devices, local(): lax.ppermute(outgoing, 'x', [(src, (src + s) % nx) for src in range(nx)])  5.85 us
    dot_general x1, matrix products, local(): jnp.einsum('cthl,pcrl->tprh', expand, dense_w, preferred_element_type=jnp...  5.83 us
    unnamed x22, local copies, waits for them, and re-layouts  4.94 us
  transfers between devices with their start and end apart: 10, of which 4 were waited for; matrix products, arithmetic and copies ran while one was open for 52% of the time, Pallas kernels for 0%

profile of v13, /device:TPU:8, one launch (start us, length us, event | category | flops | bytes accessed | tf_op | source)
XLA Modules:
  0.0 138.2 jit_solution(11518170044273608706)
XLA Ops:
  7.2 0.9 copy.78
  8.0 0.7 broadcast_in_dim.126
  8.8 4.3 %all-to-all-start = ((bf16[4,8,32,128]{3,2,1,0:T(8,128)(2,1)}), bf16[4,8,32,128]{3,2,1,0:T(8,128)(2,1)S(1)}, u32[]{:S(2)}, u32[]{:S(2)}) async-start(bf16[4,8,32,128]{3,2,1,0:T(8,128)(2,1)} %broadcast_in_dim.126), calls=%async_computation | async-start | bytes 524288 | tf_op jit(solution)/shard_map/all_to_all | solution.py:42
  13.1 1.6 %copy.71 = bf16[1,128,4096]{1,2,0:T(8,128)(2,1)S(1)} copy(bf16[1,128,4096]{2,1,0:T(8,128)(2,1)} %param.7) | data formatting | bytes 2097152 | tf_op args[0]
  15.3 1.5 %fusion.11 = bf16[128,4096]{0,1:T(8,128)(2,1)} fusion(bf16[1,128,4096]{1,2,0:T(8,128)(2,1)S(1)} %copy.71, f32[4096]{0:T(1024)S(1)} %bitcast.116, f32[128]{0:T(128)S(1)} %get-tuple-element.19), kind=kLoop, calls=%fused_computation.18 | loop fusion | flops 2097152 | bytes 2114048 | tf_op jit(solution)/shard_map/convert_element_type | solution.py:64
  17.6 2.2 %all-to-all-done = bf16[4,8,32,128]{3,2,1,0:T(8,128)(2,1)S(1)} async-done(((bf16[4,8,32,128]{3,2,1,0:T(8,128)(2,1)}), bf16[4,8,32,128]{3,2,1,0:T(8,128)(2,1)S(1)}, u32[]{:S(2)}, u32[]{:S(2)}) %all-to-all-start) | async-done | bytes 262176 | tf_op jit(solution)/shard_map/all_to_all | solution.py:42
  19.7 0.7 copy-done.2
  22.1 1.7 %broadcast_in_dim.119 = bf16[16,2,256,128]{2,1,3,0:T(2,128)(2,1)S(1)} broadcast(bf16[16,256,128]{1,2,0:T(8,128)(2,1)S(1)} %pad_maximum_fusion.2), dimensions={0,2,3} | broadcast | bytes 3145728 | tf_op jit(solution)/shard_map/jit(_where)/broadcast_in_dim | solution.py:76
  23.8 2.7 %broadcast_in_dim.120 = bf16[16,512,128]{1,2,0:T(8,128)(2,1)} reshape(bf16[16,2,256,128]{2,1,3,0:T(2,128)(2,1)S(1)} %broadcast_in_dim.119) | data formatting | bytes 4194304 | tf_op jit(solution)/shard_map/jit(_where)/broadcast_in_dim | solution.py:76
  26.5 1.8 %pad_maximum_fusion.1 = bf16[256,4096]{0,1:T(8,128)(2,1)S(1)} fusion(bf16[128,4096]{0,1:T(8,128)(2,1)} %collective-permute-done, bf16[128,4096]{0,1:T(8,128)(2,1)} %fusion.11), kind=kLoop, calls=%fused_computation.11 | loop fusion | flops 4194304 | bytes 4194304 | tf_op jit(solution)/shard_map/concatenate | solution.py:66
  28.2 2.3 %reshape.408 = bf16[256,64,32,2]{0,3,2,1:T(2,128)(2,1)} reshape(bf16[256,4096]{0,1:T(8,128)(2,1)S(1)} %pad_maximum_fusion.1) | data formatting | bytes 4194304 | tf_op jit(solution)/shard_map/reshape | solution.py:77
  30.5 4.5 %reshape.409 = bf16[64,32,512]{2,1,0:T(8,128)(2,1)} reshape(bf16[64,32,2,256]{3,2,1,0:T(2,128)(2,1)} %bitcast.106) | data formatting | bytes 4194304 | tf_op jit(solution)/shard_map/reshape | solution.py:78
  35.0 9.7 %fusion.5 = f32[65,32,16,128]{3,1,2,0:T(8,128)} fusion(bf16[64,32,512]{2,1,0:T(8,128)(2,1)} %reshape.409, bf16[16,512,128]{1,2,0:T(8,128)(2,1)S(1)} %copy-done.1, pred[512,128]{0,1:T(8,128)(4,1)S(1)} %copy.74), kind=kOutput, calls=%fused_computation.8 | convolution fusion | flops 4363124736 | bytes 21299200 | tf_op jit(solution)/shard_map/dot_general | solution.py:81
  44.7 8.8 %gather_fusion = f32[256,32,128]{2,1,0:T(8,128)} fusion(f32[1040,32,128]{2,1,0:T(8,128)} %bitcast.112, s32[1024]{0:T(1024)S(1)} %pad_clamp_fusion), kind=kCustom, calls=%fused_computation | custom fusion | bytes 8389632 | tf_op jit(solution)/shard_map/gather | solution.py:98
  53.5 9.3 %all-gather.2.cloned.1.call-done = bf16[256,32,128]{2,1,0:T(8,128)(2,1)} async-done(((bf16[32,32,128]{2,1,0:T(8,128)(2,1)}), bf16[256,32,128]{2,1,0:T(8,128)(2,1)}) %all-gather.2.cloned.1.call-update) | async-done | bytes 2097168 | tf_op jit(solution)/shard_map/all_gather | solution.py:43
  64.7 2.3 %convert.4 = f32[128,64,32,2]{0,3,2,1:T(2,128)} convert(bf16[128,64,32,2]{0,3,2,1:T(2,128)(2,1)S(1)} %bitcast.103) | non-fusion elementwise | flops 524288 | bytes 3145728 | tf_op jit(solution)/shard_map/convert_element_type | solution.py:22
  67.2 1.0 copy.84
  69.4 1.0 mul.153
  70.9 4.6 %pad_maximum_fusion = bf16[512,32,128]{2,1,0:T(8,128)(2,1)} fusion(bf16[256,32,128]{2,1,0:T(8,128)(2,1)} %collective-permute-done.2, bf16[256,32,128]{2,1,0:T(8,128)(2,1)} %all-gather.2.cloned.1.call-done), kind=kLoop, calls=%fused_computation.6 | loop fusion | flops 2097152 | bytes 8388608 | tf_op jit(solution)/shard_map/concatenate | solution.py:100
  75.5 12.1 %gather_fusion.1 = bf16[1024,32,128]{2,1,0:T(8,128)(2,1)} fusion(bf16[512,32,128]{2,1,0:T(8,128)(2,1)} %pad_maximum_fusion, s32[1024]{0:T(1024)S(1)} %broadcast_clamp_fusion), kind=kCustom, calls=%fused_computation.1 | custom fusion | bytes 16781312 | tf_op jit(solution)/shard_map/gather | solution.py:111
  87.7 5.8 %fusion.15 = (f32[128]{0:T(128)S(1)}, f32[128,64,32,2]{0,2,3,1:T(8,128)S(1)}) fusion(f32[128,64,32,2]{0,3,2,1:T(2,128)S(1)} %copy-done, f32[64,32,2]{1,2,0:T(2,128)S(1)} %copy.86, pred[2,128]{1,0:T(4,128)(4,1)S(1)} %iota_compare_fusion.2, bf16[16,128,128]{2,1,0:T(8,128)(2,1)} %copy.84, bf16[64,16,32,128]{3,2,1,0:T(8,128)(2,1)} %bitcast.104, ...), kind=kOutput, calls=%fused_computation.23 | convolution fusion | flops 2153775104 | bytes 13125376 | tf_op jit(solution)/shard_map/cthl,pcrl->tprh/dot_general | solution.py:113
  93.5 1.9 %copy.85 = f32[128,64,32,2]{0,3,2,1:T(2,128)S(1)} copy(f32[128,64,32,2]{0,2,3,1:T(8,128)S(1)} %get-tuple-element.21) | data formatting | bytes 4194304 | tf_op jit(solution)/shard_map/cthl,pcrl->tprh/transpose | solution.py:113
  95.4 0.7 fusion.14
  96.2 2.5 %collective-permute-start.3 = (bf16[128,4096]{0,1:T(8,128)(2,1)S(1)}, bf16[128,4096]{0,1:T(8,128)(2,1)S(1)}, u32[]{:S(2)}, u32[]{:S(2)}) collective-permute-start(bf16[128,4096]{0,1:T(8,128)(2,1)S(1)} %fusion.14), channel_id=1, source_target_pairs={{64,0},{128,64},{192,128},{65,1},{129,65},{193,129},{66,2},{130,66... | collective-permute-start | bytes 3145736 | tf_op jit(solution)/shard_map/ppermute | solution.py:13
  98.7 20.5 %reduce-scatter.2.cloned.1.call-done = f32[32,32,128]{2,1,0:T(8,128)} async-done(((f32[256,32,128]{2,1,0:T(8,128)}), f32[32,32,128]{2,1,0:T(8,128)}) %reduce-scatter.2.cloned.1.call-update) | async-done | bytes 524304 | tf_op jit(solution)/shard_map/reduce_scatter | solution.py:101
  119.2 1.1 constant_dynamic-slice_fusion.2
  120.5 1.5 %collective-permute-start.4 = (f32[8,32,128]{2,0,1:T(8,128)S(1)}, f32[8,32,128]{2,0,1:T(8,128)S(1)}, u32[]{:S(2)}, u32[]{:S(2)}) collective-permute-start(f32[8,32,128]{2,0,1:T(8,128)S(1)} %bitcast.118), channel_id=1, source_target_pairs={{0,2},{2,4},{4,6},{6,0},{1,3},{3,5},{5,7},{7,1},{8,10},{10,12},{12... | collective-permute-start | bytes 393224 | tf_op jit(solution)/shard_map/ppermute | solution.py:106
  122.1 2.8 %collective-permute-start.5 = (f32[8,32,128]{2,0,1:T(8,128)S(1)}, f32[8,32,128]{2,0,1:T(8,128)S(1)}, u32[]{:S(2)}, u32[]{:S(2)}) collective-permute-start(f32[8,32,128]{2,0,1:T(8,128)S(1)} %bitcast.119), channel_id=1, source_target_pairs={{0,4},{2,6},{4,0},{6,2},{1,5},{3,7},{5,1},{7,3},{8,12},{10,14},{12... | collective-permute-start | bytes 393224 | tf_op jit(solution)/shard_map/ppermute | solution.py:106
  124.9 1.5 %collective-permute-start.6 = (f32[8,32,128]{2,0,1:T(8,128)S(1)}, f32[8,32,128]{2,0,1:T(8,128)S(1)}, u32[]{:S(2)}, u32[]{:S(2)}) collective-permute-start(f32[8,32,128]{2,0,1:T(8,128)S(1)} %bitcast.120), channel_id=1, source_target_pairs={{0,6},{2,0},{4,2},{6,4},{1,7},{3,1},{5,3},{7,5},{8,14},{10,8},{12,... | collective-permute-start | bytes 393224 | tf_op jit(solution)/shard_map/ppermute | solution.py:106
  126.5 1.3 copy.92
  127.8 2.9 %collective-permute-done.5 = f32[8,32,128]{2,0,1:T(8,128)S(1)} collective-permute-done((f32[8,32,128]{2,0,1:T(8,128)S(1)}, f32[8,32,128]{2,0,1:T(8,128)S(1)}, u32[]{:S(2)}, u32[]{:S(2)}) %collective-permute-start.5) | collective-permute-done | bytes 131104 | tf_op jit(solution)/shard_map/ppermute | solution.py:106
  130.6 0.8 fusion.32
  (72 shorter events, 7.0 us)
Async XLA Ops:
  7.2 8.1 %copy-start.4 = (f32[1,4096]{1,0:T(1,128)S(1)}, f32[1,4096]{1,0:T(1,128)}, u32[]{:S(2)}) copy-start(f32[1,4096]{1,0:T(1,128)} %param.9) | copy-start | bytes 49156
  8.8 11.0 %all-to-all-start = ((bf16[4,8,32,128]{3,2,1,0:T(8,128)(2,1)}), bf16[4,8,32,128]{3,2,1,0:T(8,128)(2,1)S(1)}, u32[]{:S(2)}, u32[]{:S(2)}) async-start(bf16[4,8,32,128]{3,2,1,0:T(8,128)(2,1)} %broadcast_in_dim.126), calls=%async_computation | async-start | bytes 524288 | tf_op jit(solution)/shard_map/all_to_all | solution.py:42
  13.1 49.7 %all-gather.2.cloned.1.call-start = ((), (), s32[]{:S(2)}) async-start(), calls=%async_computation.2 | async-start | bytes 2359296 | tf_op jit(solution)/shard_map/all_gather | solution.py:43
  14.7 2.1 %copy-start.3 = (bf16[1,128,1024]{2,1,0:T(8,128)(2,1)S(1)}, bf16[1,128,1024]{2,1,0:T(8,128)(2,1)}, u32[]{:S(2)}) copy-start(bf16[1,128,1024]{2,1,0:T(8,128)(2,1)} %param.8) | copy-start | bytes 786436
  14.7 6.3 %copy-start.7 = (s32[1,64]{1,0:T(1,128)S(1)}, s32[1,64]{1,0:T(1,128)}, u32[]{:S(2)}) copy-start(s32[1,64]{1,0:T(1,128)} %param.12) | copy-start | bytes 772
  14.7 6.5 %copy-start.5 = (s32[1,64,8]{1,2,0:T(8,128)S(1)}, s32[1,64,8]{1,2,0:T(8,128)}, u32[]{:S(2)}) copy-start(s32[1,64,8]{1,2,0:T(8,128)} %param.11) | copy-start | bytes 6148
  14.7 6.7 %copy-start.6 = (s32[1,512]{1,0:T(1,128)S(1)}, s32[1,512]{1,0:T(1,128)}, u32[]{:S(2)}) copy-start(s32[1,512]{1,0:T(1,128)} %param.13) | copy-start | bytes 6148
  16.8 9.7 %collective-permute-start = (bf16[128,4096]{0,1:T(8,128)(2,1)}, bf16[128,4096]{0,1:T(8,128)(2,1)}, u32[]{:S(2)}, u32[]{:S(2)}) collective-permute-start(bf16[128,4096]{0,1:T(8,128)(2,1)} %fusion.11), channel_id=1, source_target_pairs={{0,1},{1,0},{2,3},{3,2},{4,5},{5,4},{6,7},{7,6},{8,9},{9,8},{10,11... | collective-permute-start | bytes 3145736 | tf_op jit(solution)/shard_map/ppermute | solution.py:18
  17.0 4.9 %collective-permute-start.1 = (bf16[128,1024]{0,1:T(8,128)(2,1)S(1)}, bf16[128,1024]{0,1:T(8,128)(2,1)S(1)}, u32[]{:S(2)}, u32[]{:S(2)}) collective-permute-start(bf16[128,1024]{0,1:T(8,128)(2,1)S(1)} %bitcast.107), channel_id=1, source_target_pairs={{0,1},{1,0},{2,3},{3,2},{4,5},{5,4},{6,7},{7,6},{8,9},{9,8},{10,11... | collective-permute-start | bytes 786440 | tf_op jit(solution)/shard_map/ppermute | solution.py:18
  19.7 0.7 copy-start.2
  20.5 98.8 %reduce-scatter.2.cloned.1.call-start = ((), (), s32[]{:S(2)}) async-start(), calls=%async_computation.3 | async-start | bytes 4718592 | tf_op jit(solution)/shard_map/reduce_scatter | solution.py:101
  30.5 4.5 %copy-start.1 = (bf16[16,512,128]{1,2,0:T(8,128)(2,1)S(1)}, bf16[16,512,128]{1,2,0:T(8,128)(2,1)}, u32[]{:S(2)}) copy-start(bf16[16,512,128]{1,2,0:T(8,128)(2,1)} %broadcast_in_dim.120) | copy-start | bytes 6291460
  62.8 8.2 %collective-permute-start.2 = (bf16[256,32,128]{2,1,0:T(8,128)(2,1)}, bf16[256,32,128]{2,1,0:T(8,128)(2,1)}, u32[]{:S(2)}, u32[]{:S(2)}) collective-permute-start(bf16[256,32,128]{2,1,0:T(8,128)(2,1)} %all-gather.2.cloned.1.call-done), channel_id=1, source_target_pairs={{0,1},{1,0},{2,3},{3,2},{4,5},{5,4},{6,7},{7,6},{8,9},{9,8},{10,11... | collective-permute-start | bytes 6291464 | tf_op jit(solution)/shard_map/ppermute | solution.py:18
  75.5 12.1 %copy-start = (f32[128,64,32,2]{0,3,2,1:T(2,128)S(1)}, f32[128,64,32,2]{0,3,2,1:T(2,128)}, u32[]{:S(2)}) copy-start(f32[128,64,32,2]{0,3,2,1:T(2,128)} %convert.4) | copy-start | bytes 6291460
  96.2 30.3 %collective-permute-start.3 = (bf16[128,4096]{0,1:T(8,128)(2,1)S(1)}, bf16[128,4096]{0,1:T(8,128)(2,1)S(1)}, u32[]{:S(2)}, u32[]{:S(2)}) collective-permute-start(bf16[128,4096]{0,1:T(8,128)(2,1)S(1)} %fusion.14), channel_id=1, source_target_pairs={{64,0},{128,64},{192,128},{65,1},{129,65},{193,129},{66,2},{130,66... | collective-permute-start | bytes 3145736 | tf_op jit(solution)/shard_map/ppermute | solution.py:13
  120.5 7.3 %collective-permute-start.4 = (f32[8,32,128]{2,0,1:T(8,128)S(1)}, f32[8,32,128]{2,0,1:T(8,128)S(1)}, u32[]{:S(2)}, u32[]{:S(2)}) collective-permute-start(f32[8,32,128]{2,0,1:T(8,128)S(1)} %bitcast.118), channel_id=1, source_target_pairs={{0,2},{2,4},{4,6},{6,0},{1,3},{3,5},{5,7},{7,1},{8,10},{10,12},{12... | collective-permute-start | bytes 393224 | tf_op jit(solution)/shard_map/ppermute | solution.py:106
  122.1 8.5 %collective-permute-start.5 = (f32[8,32,128]{2,0,1:T(8,128)S(1)}, f32[8,32,128]{2,0,1:T(8,128)S(1)}, u32[]{:S(2)}, u32[]{:S(2)}) collective-permute-start(f32[8,32,128]{2,0,1:T(8,128)S(1)} %bitcast.119), channel_id=1, source_target_pairs={{0,4},{2,6},{4,0},{6,2},{1,5},{3,7},{5,1},{7,3},{8,12},{10,14},{12... | collective-permute-start | bytes 393224 | tf_op jit(solution)/shard_map/ppermute | solution.py:106
  124.9 5.7 %collective-permute-start.6 = (f32[8,32,128]{2,0,1:T(8,128)S(1)}, f32[8,32,128]{2,0,1:T(8,128)S(1)}, u32[]{:S(2)}, u32[]{:S(2)}) collective-permute-start(f32[8,32,128]{2,0,1:T(8,128)S(1)} %bitcast.120), channel_id=1, source_target_pairs={{0,6},{2,0},{4,2},{6,4},{1,7},{3,1},{5,3},{7,5},{8,14},{10,8},{12,... | collective-permute-start | bytes 393224 | tf_op jit(solution)/shard_map/ppermute | solution.py:106
Sparse Core Ops, SparseCore 0:
  20.6 42.1 all-gather.1
  65.3 53.8 reduce-scatter.1

commit v14 on v13

--- a/solution.py
+++ b/solution.py
@@ -38,8 +38,9 @@
     grad_scale = (tok_rows * nz * nx * nc) ** (-0.5)
 
     own_tiles = tiles[0].reshape(slot_dev, half, lanes)
-    copies = jnp.broadcast_to(own_tiles[None], (nx,) + own_tiles.shape)
-    gathered = lax.all_to_all(copies, "x", 0, 0).reshape(nx * slot_dev, half, lanes)
+    shift_order = sorted(range(1, nx), key=lambda s: -min(s, nx - s))
+    moved = {s: lax.ppermute(own_tiles, "x", [(src, (src + s) % nx) for src in range(nx)]) for s in shift_order}
+    gathered = jnp.concatenate([own_tiles] + [moved[s] for s in range(1, nx)], axis=0)
     gathered = lax.all_gather(gathered, "z", axis=0, tiled=True)
     slot_ids = jnp.arange(store_slots, dtype=jnp.int32)
 
@@ -50,7 +51,7 @@
         holder = slot // slot_dev
         half_of = (holder % nc - my_core) % nc
         chip = holder // nc
-        shift = chip % nx
+        shift = (my_x - chip % nx) % nx
         return half_of * (nz * nx * slot_dev) + ((chip // nx) * nx + shift) * slot_dev + slot % slot_dev
 
     kept_grid = jnp.arange(most_kept)[None, :] < count_list[:, None]
@@ -101,7 +102,7 @@
     weight_grad = lax.psum_scatter(terms, "z", scatter_dimension=0, tiled=True)
     x_blocks = weight_grad.reshape(nx, slot_dev, half, lanes)
     own_sum = lax.dynamic_index_in_dim(x_blocks, my_x, axis=0, keepdims=False)
-    for s in range(1, nx):
+    for s in shift_order:
         outgoing = lax.dynamic_index_in_dim(x_blocks, (my_x + s) % nx, axis=0, keepdims=False)
         own_sum = own_sum + lax.ppermute(outgoing, "x", [(src, (src + s) % nx) for src in range(nx)])
     weight_grad = own_sum

time: 139 us -> 137 us (0.986)
  waiting for transfers between devices: 34.9 us -> 31.4 us
  starting transfers between devices: 13.5 us -> 15.6 us
  local copies, waits for them, and re-layouts: 45.4 us -> 43.9 us
    ppermute x0 -> x3, starting transfers between devices: none -> 5.73 us  [local(): lax.ppermute(own_tiles, 'x', [(src, (src + s) % nx) for src in range(nx)])]
    all_to_all x1 -> x0, starting transfers between devices: 4.29 us -> none  [local(): lax.all_to_all(copies, 'x', 0, 0).reshape(nx * slot_dev, half, lanes)]
    all_to_all x1 -> x0, waiting for transfers between devices: 2.17 us -> none  [local(): lax.all_to_all(copies, 'x', 0, 0).reshape(nx * slot_dev, half, lanes)]
    broadcast_in_dim x2 -> x0, local copies, waits for them, and re-layouts: 1.59 us -> none  [local(): copies = jnp.broadcast_to(own_tiles[None], (nx,) + own_tiles.shape)]
    unnamed x22 -> x21, local copies, waits for them, and re-layouts: 4.94 us -> 5.09 us
  transfers between devices with their start and end apart: 10 -> 12, of which waited for: 4 -> 4; matrix products, arithmetic and copies ran while one was open for 52% -> 54% of each run, Pallas kernels for 0% -> 0%
where the time goes in v14:
time: 137 us; the launch traced here: 136 us
  local copies, waits for them, and re-layouts  43.9 us (32%)
  waiting for transfers between devices  31.4 us (23%)
  starting transfers between devices  15.6 us (11%)
  matrix products  15.5 us (11%)
  other arithmetic  15.3 us (11%)
  between operations  14.4 us (11%)
    reduce_scatter x1, waiting for transfers between devices, local(): weight_grad = lax.psum_scatter(terms, 'z', scatter_dimension=0, tiled=True)  20.5 us
    gather x1, local copies, waits for them, and re-layouts, local(): gathered[dense_rows]  12.1 us
    dot_general x1, matrix products, local(): jnp.dot(normed_pairs.reshape((panel_list + 1) * half, 2 * pair_tokens), e...  9.68 us
    gather x1, local copies, waits for them, and re-layouts, local(): terms = dense_terms[jnp.where(term_kept, term_index, panel_list * ncol)]  8.81 us
    all_gather x1, waiting for transfers between devices, local(): gathered = lax.all_gather(gathered, 'z', axis=0, tiled=True)  8.53 us
    ppermute x3, starting transfers between devices, local(): lax.ppermute(outgoing, 'x', [(src, (src + s) % nx) for src in range(nx)])  6.46 us
    dot_general x1, matrix products, local(): jnp.einsum('cthl,pcrl->tprh', expand, dense_w, preferred_element_type=jnp...  5.83 us
    ppermute x3, starting transfers between devices, local(): lax.ppermute(own_tiles, 'x', [(src, (src + s) % nx) for src in range(nx)])  5.73 us
  transfers between devices with their start and end apart: 12, of which 4 were waited for; matrix products, arithmetic and copies ran while one was open for 54% of the time, Pallas kernels for 0%

profile of v14, /device:TPU:8, one launch (start us, length us, event | category | flops | bytes accessed | tf_op | source)
XLA Modules:
  0.0 136.1 jit_solution(6663685089566928612)
XLA Ops:
  7.2 0.9 copy.104
  8.1 1.6 %collective-permute-start.2 = (bf16[8,32,128]{2,1,0:T(8,128)(2,1)S(1)}, bf16[8,32,128]{2,1,0:T(8,128)(2,1)S(1)}, u32[]{:S(2)}, u32[]{:S(2)}) collective-permute-start(bf16[8,32,128]{2,1,0:T(8,128)(2,1)S(1)} %bitcast.118), channel_id=1, source_target_pairs={{0,2},{2,4},{4,6},{6,0},{1,3},{3,5},{5,7},{7,1},{8,10},{10,12},{12... | collective-permute-start | bytes 196616 | tf_op jit(solution)/shard_map/ppermute | solution.py:42
  9.6 2.7 %collective-permute-start.3 = (bf16[8,32,128]{2,1,0:T(8,128)(2,1)S(1)}, bf16[8,32,128]{2,1,0:T(8,128)(2,1)S(1)}, u32[]{:S(2)}, u32[]{:S(2)}) collective-permute-start(bf16[8,32,128]{2,1,0:T(8,128)(2,1)S(1)} %bitcast.119), channel_id=1, source_target_pairs={{0,4},{2,6},{4,0},{6,2},{1,5},{3,7},{5,1},{7,3},{8,12},{10,14},{12... | collective-permute-start | bytes 196616 | tf_op jit(solution)/shard_map/ppermute | solution.py:42
  12.4 1.4 %collective-permute-start.4 = (bf16[8,32,128]{2,1,0:T(8,128)(2,1)S(1)}, bf16[8,32,128]{2,1,0:T(8,128)(2,1)S(1)}, u32[]{:S(2)}, u32[]{:S(2)}) collective-permute-start(bf16[8,32,128]{2,1,0:T(8,128)(2,1)S(1)} %bitcast.120), channel_id=1, source_target_pairs={{0,6},{2,0},{4,2},{6,4},{1,7},{3,1},{5,3},{7,5},{8,14},{10,8},{12,... | collective-permute-start | bytes 196616 | tf_op jit(solution)/shard_map/ppermute | solution.py:42
  13.8 1.6 %copy.68 = bf16[1,128,4096]{1,2,0:T(8,128)(2,1)S(1)} copy(bf16[1,128,4096]{2,1,0:T(8,128)(2,1)} %param.7) | data formatting | bytes 2097152 | tf_op args[0]
  16.0 1.5 %fusion.11 = bf16[128,4096]{0,1:T(8,128)(2,1)} fusion(bf16[1,128,4096]{1,2,0:T(8,128)(2,1)S(1)} %copy.68, f32[4096]{0:T(1024)S(1)} %bitcast.122, f32[128]{0:T(128)S(1)} %get-tuple-element.19), kind=kLoop, calls=%fused_computation.18 | loop fusion | flops 2097152 | bytes 2114048 | tf_op jit(solution)/shard_map/convert_element_type | solution.py:65
  18.3 0.7 pad_maximum_fusion.4
  21.0 1.7 %broadcast_in_dim.112 = bf16[16,2,256,128]{2,1,3,0:T(2,128)(2,1)S(1)} broadcast(bf16[16,256,128]{1,2,0:T(8,128)(2,1)S(1)} %pad_maximum_fusion.2), dimensions={0,2,3} | broadcast | bytes 3145728 | tf_op jit(solution)/shard_map/jit(_where)/broadcast_in_dim | solution.py:77
  22.7 2.7 %broadcast_in_dim.113 = bf16[16,512,128]{1,2,0:T(8,128)(2,1)} reshape(bf16[16,2,256,128]{2,1,3,0:T(2,128)(2,1)S(1)} %broadcast_in_dim.112) | data formatting | bytes 4194304 | tf_op jit(solution)/shard_map/jit(_where)/broadcast_in_dim | solution.py:77
  25.4 1.8 %pad_maximum_fusion.1 = bf16[256,4096]{0,1:T(8,128)(2,1)S(1)} fusion(bf16[128,4096]{0,1:T(8,128)(2,1)} %collective-permute-done, bf16[128,4096]{0,1:T(8,128)(2,1)} %fusion.11), kind=kLoop, calls=%fused_computation.11 | loop fusion | flops 4194304 | bytes 4194304 | tf_op jit(solution)/shard_map/concatenate | solution.py:67
  27.2 2.3 %reshape.416 = bf16[256,64,32,2]{0,3,2,1:T(2,128)(2,1)} reshape(bf16[256,4096]{0,1:T(8,128)(2,1)S(1)} %pad_maximum_fusion.1) | data formatting | bytes 4194304 | tf_op jit(solution)/shard_map/reshape | solution.py:78
  29.4 4.5 %reshape.417 = bf16[64,32,512]{2,1,0:T(8,128)(2,1)} reshape(bf16[64,32,2,256]{3,2,1,0:T(2,128)(2,1)} %bitcast.109) | data formatting | bytes 4194304 | tf_op jit(solution)/shard_map/reshape | solution.py:79
  34.0 9.7 %fusion.5 = f32[65,32,16,128]{3,1,2,0:T(8,128)} fusion(bf16[64,32,512]{2,1,0:T(8,128)(2,1)} %reshape.417, bf16[16,512,128]{1,2,0:T(8,128)(2,1)S(1)} %copy-done.1, pred[512,128]{0,1:T(8,128)(4,1)S(1)} %copy.71), kind=kOutput, calls=%fused_computation.8 | convolution fusion | flops 4363124736 | bytes 21299200 | tf_op jit(solution)/shard_map/dot_general | solution.py:82
  43.6 8.8 %gather_fusion = f32[256,32,128]{2,1,0:T(8,128)} fusion(f32[1040,32,128]{2,1,0:T(8,128)} %bitcast.114, s32[1024]{0:T(1024)S(1)} %pad_clamp_fusion), kind=kCustom, calls=%fused_computation | custom fusion | bytes 8389632 | tf_op jit(solution)/shard_map/gather | solution.py:99
  52.5 8.5 %all-gather.2.cloned.1.call-done = bf16[256,32,128]{2,1,0:T(8,128)(2,1)} async-done(((bf16[32,32,128]{2,1,0:T(8,128)(2,1)}), bf16[256,32,128]{2,1,0:T(8,128)(2,1)}) %all-gather.2.cloned.1.call-update) | async-done | bytes 2097168 | tf_op jit(solution)/shard_map/all_gather | solution.py:44
  63.0 2.3 %convert.4 = f32[128,64,32,2]{0,3,2,1:T(2,128)} convert(bf16[128,64,32,2]{0,3,2,1:T(2,128)(2,1)S(1)} %bitcast.106) | non-fusion elementwise | flops 524288 | bytes 3145728 | tf_op jit(solution)/shard_map/convert_element_type | solution.py:22
  65.5 1.0 copy.80
  67.0 0.7 reduce.8
  67.7 1.0 mul.153
  69.2 4.6 %pad_maximum_fusion = bf16[512,32,128]{2,1,0:T(8,128)(2,1)} fusion(bf16[256,32,128]{2,1,0:T(8,128)(2,1)} %collective-permute-done.5, bf16[256,32,128]{2,1,0:T(8,128)(2,1)} %all-gather.2.cloned.1.call-done), kind=kLoop, calls=%fused_computation.6 | loop fusion | flops 2097152 | bytes 8388608 | tf_op jit(solution)/shard_map/concatenate | solution.py:101
  73.8 12.1 %gather_fusion.1 = bf16[1024,32,128]{2,1,0:T(8,128)(2,1)} fusion(bf16[512,32,128]{2,1,0:T(8,128)(2,1)} %pad_maximum_fusion, s32[1024]{0:T(1024)S(1)} %broadcast_clamp_fusion), kind=kCustom, calls=%fused_computation.1 | custom fusion | bytes 16781312 | tf_op jit(solution)/shard_map/gather | solution.py:112
  85.9 5.8 %fusion.15 = (f32[128]{0:T(128)S(1)}, f32[128,64,32,2]{0,2,3,1:T(8,128)S(1)}) fusion(f32[128,64,32,2]{0,3,2,1:T(2,128)S(1)} %copy-done, f32[64,32,2]{1,2,0:T(2,128)S(1)} %copy.82, pred[2,128]{1,0:T(4,128)(4,1)S(1)} %iota_compare_fusion.2, bf16[16,128,128]{2,1,0:T(8,128)(2,1)} %copy.80, bf16[64,16,32,128]{3,2,1,0:T(8,128)(2,1)} %bitcast.107, ...), kind=kOutput, calls=%fused_computation.23 | convolution fusion | flops 2153775104 | bytes 13125376 | tf_op jit(solution)/shard_map/cthl,pcrl->tprh/dot_general | solution.py:114
  91.8 1.9 %copy.81 = f32[128,64,32,2]{0,3,2,1:T(2,128)S(1)} copy(f32[128,64,32,2]{0,2,3,1:T(8,128)S(1)} %get-tuple-element.21) | data formatting | bytes 4194304 | tf_op jit(solution)/shard_map/cthl,pcrl->tprh/transpose | solution.py:114
  93.7 0.7 fusion.14
  94.4 2.4 %collective-permute-start.6 = (bf16[128,4096]{0,1:T(8,128)(2,1)S(1)}, bf16[128,4096]{0,1:T(8,128)(2,1)S(1)}, u32[]{:S(2)}, u32[]{:S(2)}) collective-permute-start(bf16[128,4096]{0,1:T(8,128)(2,1)S(1)} %fusion.14), channel_id=1, source_target_pairs={{64,0},{128,64},{192,128},{65,1},{129,65},{193,129},{66,2},{130,66... | collective-permute-start | bytes 3145736 | tf_op jit(solution)/shard_map/ppermute | solution.py:13
  96.9 20.5 %reduce-scatter.2.cloned.1.call-done = f32[32,32,128]{2,1,0:T(8,128)} async-done(((f32[256,32,128]{2,1,0:T(8,128)}), f32[32,32,128]{2,1,0:T(8,128)}) %reduce-scatter.2.cloned.1.call-update) | async-done | bytes 524304 | tf_op jit(solution)/shard_map/reduce_scatter | solution.py:102
  117.4 1.1 constant_dynamic-slice_fusion.2
  118.7 3.1 %collective-permute-start.7 = (f32[8,32,128]{2,0,1:T(8,128)S(1)}, f32[8,32,128]{2,0,1:T(8,128)S(1)}, u32[]{:S(2)}, u32[]{:S(2)}) collective-permute-start(f32[8,32,128]{2,0,1:T(8,128)S(1)} %bitcast.124), channel_id=1, source_target_pairs={{0,4},{2,6},{4,0},{6,2},{1,5},{3,7},{5,1},{7,3},{8,12},{10,14},{12... | collective-permute-start | bytes 393224 | tf_op jit(solution)/shard_map/ppermute | solution.py:107
  122.5 2.7 %collective-permute-start.9 = (f32[8,32,128]{2,0,1:T(8,128)S(1)}, f32[8,32,128]{2,0,1:T(8,128)S(1)}, u32[]{:S(2)}, u32[]{:S(2)}) collective-permute-start(f32[8,32,128]{2,0,1:T(8,128)S(1)} %bitcast.126), channel_id=1, source_target_pairs={{0,6},{2,0},{4,2},{6,4},{1,7},{3,1},{5,3},{7,5},{8,14},{10,8},{12,... | collective-permute-start | bytes 393224 | tf_op jit(solution)/shard_map/ppermute | solution.py:107
  125.3 1.3 copy.88
  126.6 1.9 %collective-permute-done.8 = f32[8,32,128]{2,0,1:T(8,128)S(1)} collective-permute-done((f32[8,32,128]{2,0,1:T(8,128)S(1)}, f32[8,32,128]{2,0,1:T(8,128)S(1)}, u32[]{:S(2)}, u32[]{:S(2)}) %collective-permute-start.8) | collective-permute-done | bytes 131104 | tf_op jit(solution)/shard_map/ppermute | solution.py:107
  128.5 0.8 fusion.32
  (74 shorter events, 7.3 us)
Async XLA Ops:
  7.2 8.9 %copy-start.3 = (f32[1,4096]{1,0:T(1,128)S(1)}, f32[1,4096]{1,0:T(1,128)}, u32[]{:S(2)}) copy-start(f32[1,4096]{1,0:T(1,128)} %param.9) | copy-start | bytes 49156
  7.2 53.8 %all-gather.2.cloned.1.call-start = ((), (), s32[]{:S(2)}) async-start(), calls=%async_computation.1 | async-start | bytes 2359296 | tf_op jit(solution)/shard_map/all_gather | solution.py:44
  8.1 10.2 %collective-permute-start.2 = (bf16[8,32,128]{2,1,0:T(8,128)(2,1)S(1)}, bf16[8,32,128]{2,1,0:T(8,128)(2,1)S(1)}, u32[]{:S(2)}, u32[]{:S(2)}) collective-permute-start(bf16[8,32,128]{2,1,0:T(8,128)(2,1)S(1)} %bitcast.118), channel_id=1, source_target_pairs={{0,2},{2,4},{4,6},{6,0},{1,3},{3,5},{5,7},{7,1},{8,10},{10,12},{12... | collective-permute-start | bytes 196616 | tf_op jit(solution)/shard_map/ppermute | solution.py:42
  9.6 8.7 %collective-permute-start.3 = (bf16[8,32,128]{2,1,0:T(8,128)(2,1)S(1)}, bf16[8,32,128]{2,1,0:T(8,128)(2,1)S(1)}, u32[]{:S(2)}, u32[]{:S(2)}) collective-permute-start(bf16[8,32,128]{2,1,0:T(8,128)(2,1)S(1)} %bitcast.119), channel_id=1, source_target_pairs={{0,4},{2,6},{4,0},{6,2},{1,5},{3,7},{5,1},{7,3},{8,12},{10,14},{12... | collective-permute-start | bytes 196616 | tf_op jit(solution)/shard_map/ppermute | solution.py:42
  12.4 6.0 %collective-permute-start.4 = (bf16[8,32,128]{2,1,0:T(8,128)(2,1)S(1)}, bf16[8,32,128]{2,1,0:T(8,128)(2,1)S(1)}, u32[]{:S(2)}, u32[]{:S(2)}) collective-permute-start(bf16[8,32,128]{2,1,0:T(8,128)(2,1)S(1)} %bitcast.120), channel_id=1, source_target_pairs={{0,6},{2,0},{4,2},{6,4},{1,7},{3,1},{5,3},{7,5},{8,14},{10,8},{12,... | collective-permute-start | bytes 196616 | tf_op jit(solution)/shard_map/ppermute | solution.py:42
  15.4 2.1 %copy-start.2 = (bf16[1,128,1024]{2,1,0:T(8,128)(2,1)S(1)}, bf16[1,128,1024]{2,1,0:T(8,128)(2,1)}, u32[]{:S(2)}) copy-start(bf16[1,128,1024]{2,1,0:T(8,128)(2,1)} %param.8) | copy-start | bytes 786436
  16.0 3.6 %copy-start.6 = (s32[1,64]{1,0:T(1,128)S(1)}, s32[1,64]{1,0:T(1,128)}, u32[]{:S(2)}) copy-start(s32[1,64]{1,0:T(1,128)} %param.12) | copy-start | bytes 772
  16.0 3.8 %copy-start.4 = (s32[1,64,8]{1,2,0:T(8,128)S(1)}, s32[1,64,8]{1,2,0:T(8,128)}, u32[]{:S(2)}) copy-start(s32[1,64,8]{1,2,0:T(8,128)} %param.11) | copy-start | bytes 6148
  16.0 4.0 %copy-start.5 = (s32[1,512]{1,0:T(1,128)S(1)}, s32[1,512]{1,0:T(1,128)}, u32[]{:S(2)}) copy-start(s32[1,512]{1,0:T(1,128)} %param.13) | copy-start | bytes 6148
  17.5 7.8 %collective-permute-start = (bf16[128,4096]{0,1:T(8,128)(2,1)}, bf16[128,4096]{0,1:T(8,128)(2,1)}, u32[]{:S(2)}, u32[]{:S(2)}) collective-permute-start(bf16[128,4096]{0,1:T(8,128)(2,1)} %fusion.11), channel_id=1, source_target_pairs={{0,1},{1,0},{2,3},{3,2},{4,5},{5,4},{6,7},{7,6},{8,9},{9,8},{10,11... | collective-permute-start | bytes 3145736 | tf_op jit(solution)/shard_map/ppermute | solution.py:18
  17.7 3.1 %collective-permute-start.1 = (bf16[128,1024]{0,1:T(8,128)(2,1)S(1)}, bf16[128,1024]{0,1:T(8,128)(2,1)S(1)}, u32[]{:S(2)}, u32[]{:S(2)}) collective-permute-start(bf16[128,1024]{0,1:T(8,128)(2,1)S(1)} %bitcast.110), channel_id=1, source_target_pairs={{0,1},{1,0},{2,3},{3,2},{4,5},{5,4},{6,7},{7,6},{8,9},{9,8},{10,11... | collective-permute-start | bytes 786440 | tf_op jit(solution)/shard_map/ppermute | solution.py:18
  19.1 98.3 %reduce-scatter.2.cloned.1.call-start = ((), (), s32[]{:S(2)}) async-start(), calls=%async_computation.2 | async-start | bytes 4718592 | tf_op jit(solution)/shard_map/reduce_scatter | solution.py:102
  29.4 4.5 %copy-start.1 = (bf16[16,512,128]{1,2,0:T(8,128)(2,1)S(1)}, bf16[16,512,128]{1,2,0:T(8,128)(2,1)}, u32[]{:S(2)}) copy-start(bf16[16,512,128]{1,2,0:T(8,128)(2,1)} %broadcast_in_dim.113) | copy-start | bytes 6291460
  61.0 8.2 %collective-permute-start.5 = (bf16[256,32,128]{2,1,0:T(8,128)(2,1)}, bf16[256,32,128]{2,1,0:T(8,128)(2,1)}, u32[]{:S(2)}, u32[]{:S(2)}) collective-permute-start(bf16[256,32,128]{2,1,0:T(8,128)(2,1)} %all-gather.2.cloned.1.call-done), channel_id=1, source_target_pairs={{0,1},{1,0},{2,3},{3,2},{4,5},{5,4},{6,7},{7,6},{8,9},{9,8},{10,11... | collective-permute-start | bytes 6291464 | tf_op jit(solution)/shard_map/ppermute | solution.py:18
  73.8 12.1 %copy-start = (f32[128,64,32,2]{0,3,2,1:T(2,128)S(1)}, f32[128,64,32,2]{0,3,2,1:T(2,128)}, u32[]{:S(2)}) copy-start(f32[128,64,32,2]{0,3,2,1:T(2,128)} %convert.4) | copy-start | bytes 6291460
  94.4 30.9 %collective-permute-start.6 = (bf16[128,4096]{0,1:T(8,128)(2,1)S(1)}, bf16[128,4096]{0,1:T(8,128)(2,1)S(1)}, u32[]{:S(2)}, u32[]{:S(2)}) collective-permute-start(bf16[128,4096]{0,1:T(8,128)(2,1)S(1)} %fusion.14), channel_id=1, source_target_pairs={{64,0},{128,64},{192,128},{65,1},{129,65},{193,129},{66,2},{130,66... | collective-permute-start | bytes 3145736 | tf_op jit(solution)/shard_map/ppermute | solution.py:13
  118.7 7.9 %collective-permute-start.7 = (f32[8,32,128]{2,0,1:T(8,128)S(1)}, f32[8,32,128]{2,0,1:T(8,128)S(1)}, u32[]{:S(2)}, u32[]{:S(2)}) collective-permute-start(f32[8,32,128]{2,0,1:T(8,128)S(1)} %bitcast.124), channel_id=1, source_target_pairs={{0,4},{2,6},{4,0},{6,2},{1,5},{3,7},{5,1},{7,3},{8,12},{10,14},{12... | collective-permute-start | bytes 393224 | tf_op jit(solution)/shard_map/ppermute | solution.py:107
  121.8 6.7 %collective-permute-start.8 = (f32[8,32,128]{2,0,1:T(8,128)S(1)}, f32[8,32,128]{2,0,1:T(8,128)S(1)}, u32[]{:S(2)}, u32[]{:S(2)}) collective-permute-start(f32[8,32,128]{2,0,1:T(8,128)S(1)} %bitcast.125), channel_id=1, source_target_pairs={{0,2},{2,4},{4,6},{6,0},{1,3},{3,5},{5,7},{7,1},{8,10},{10,12},{12... | collective-permute-start | bytes 393224 | tf_op jit(solution)/shard_map/ppermute | solution.py:107
  122.5 6.0 %collective-permute-start.9 = (f32[8,32,128]{2,0,1:T(8,128)S(1)}, f32[8,32,128]{2,0,1:T(8,128)S(1)}, u32[]{:S(2)}, u32[]{:S(2)}) collective-permute-start(f32[8,32,128]{2,0,1:T(8,128)S(1)} %bitcast.126), channel_id=1, source_target_pairs={{0,6},{2,0},{4,2},{6,4},{1,7},{3,1},{5,3},{7,5},{8,14},{10,8},{12,... | collective-permute-start | bytes 393224 | tf_op jit(solution)/shard_map/ppermute | solution.py:107
Sparse Core Ops, SparseCore 0:
  19.2 41.7 all-gather.1
  63.5 53.8 reduce-scatter.1

commit v15 on v14

--- a/solution.py
+++ b/solution.py
@@ -64,8 +64,9 @@
     recip = lax.rsqrt(mean_sq + EPS)
     normed = (inputs_f * recip * gain_row[None, :]).astype(jnp.bfloat16)
     pair_tokens = nc * tok_rows
-    normed_pair = jnp.concatenate([normed, sibling(normed)], axis=0)
-    og_pair = jnp.concatenate([key_grad, sibling(key_grad)], axis=0)
+    both = sibling(jnp.concatenate([normed, key_grad], axis=1))
+    normed_pair = jnp.concatenate([normed, both[:, :width]], axis=0)
+    og_pair = jnp.concatenate([key_grad, both[:, width:]], axis=0)
 
     og_blocks = key_grad.reshape(tok_rows, ncol, blk).transpose(1, 0, 2)
     diag = (jnp.arange(2)[:, None] == jnp.arange(lanes)[None, :] // blk)

time: 137 us -> 137 us (level)
    slice x0 -> x2, local copies, waits for them, and re-layouts: none -> 2.26 us  [the longest x1 1.29 us: local(): normed_pair = jnp.concatenate([normed, both[:, :width]], axis=0)]
    all_gather x1, waiting for transfers between devices: 8.53 us -> 6.56 us  [local(): gathered = lax.all_gather(gathered, 'z', axis=0, tiled=True)]
    reshape x1, local copies, waits for them, and re-layouts: 4.54 us -> 2.62 us  [local(): normed_pairs = normed_pairs.reshape(panel_list, half, 2 * pair_tokens)]
    unnamed x21 -> x19, local copies, waits for them, and re-layouts: 5.09 us -> 5.12 us
  transfers between devices with their start and end apart: 12 -> 11, of which waited for: 4 -> 4; matrix products, arithmetic and copies ran while one was open for 54% -> 55% of each run, Pallas kernels for 0% -> 0%
where the time goes in v15:
time: 137 us; the launch traced here: 136 us
  local copies, waits for them, and re-layouts  44.8 us (33%)
  waiting for transfers between devices  30.2 us (22%)
  matrix products  16.2 us (12%)
  other arithmetic  15.4 us (11%)
  starting transfers between devices  15 us (11%)
  between operations  14.4 us (11%)
    reduce_scatter x1, waiting for transfers between devices, local(): weight_grad = lax.psum_scatter(terms, 'z', scatter_dimension=0, tiled=True)  20.5 us
    gather x1, local copies, waits for them, and re-layouts, local(): gathered[dense_rows]  12.2 us
    dot_general x1, matrix products, local(): jnp.dot(normed_pairs.reshape((panel_list + 1) * half, 2 * pair_tokens), e...  10.4 us
    gather x1, local copies, waits for them, and re-layouts, local(): terms = dense_terms[jnp.where(term_kept, term_index, panel_list * ncol)]  8.74 us
    all_gather x1, waiting for transfers between devices, local(): gathered = lax.all_gather(gathered, 'z', axis=0, tiled=True)  6.56 us
    ppermute x3, starting transfers between devices, local(): lax.ppermute(outgoing, 'x', [(src, (src + s) % nx) for src in range(nx)])  6.46 us
    dot_general x1, matrix products, local(): jnp.einsum('cthl,pcrl->tprh', expand, dense_w, preferred_element_type=jnp...  5.83 us
    ppermute x3, starting transfers between devices, local(): lax.ppermute(own_tiles, 'x', [(src, (src + s) % nx) for src in range(nx)])  5.73 us
  transfers between devices with their start and end apart: 11, of which 4 were waited for; matrix products, arithmetic and copies ran while one was open for 55% of the time, Pallas kernels for 0%

profile of v15, /device:TPU:8, one launch (start us, length us, event | category | flops | bytes accessed | tf_op | source)
XLA Modules:
  0.0 136.2 jit_solution(8831332667193075024)
XLA Ops:
  7.2 0.9 copy.104
  8.1 1.6 %collective-permute-start.1 = (bf16[8,32,128]{2,1,0:T(8,128)(2,1)S(1)}, bf16[8,32,128]{2,1,0:T(8,128)(2,1)S(1)}, u32[]{:S(2)}, u32[]{:S(2)}) collective-permute-start(bf16[8,32,128]{2,1,0:T(8,128)(2,1)S(1)} %bitcast.118), channel_id=1, source_target_pairs={{0,2},{2,4},{4,6},{6,0},{1,3},{3,5},{5,7},{7,1},{8,10},{10,12},{12... | collective-permute-start | bytes 196616 | tf_op jit(solution)/shard_map/ppermute | solution.py:42
  9.7 2.7 %collective-permute-start.2 = (bf16[8,32,128]{2,1,0:T(8,128)(2,1)S(1)}, bf16[8,32,128]{2,1,0:T(8,128)(2,1)S(1)}, u32[]{:S(2)}, u32[]{:S(2)}) collective-permute-start(bf16[8,32,128]{2,1,0:T(8,128)(2,1)S(1)} %bitcast.119), channel_id=1, source_target_pairs={{0,4},{2,6},{4,0},{6,2},{1,5},{3,7},{5,1},{7,3},{8,12},{10,14},{12... | collective-permute-start | bytes 196616 | tf_op jit(solution)/shard_map/ppermute | solution.py:42
  12.4 1.4 %collective-permute-start.3 = (bf16[8,32,128]{2,1,0:T(8,128)(2,1)S(1)}, bf16[8,32,128]{2,1,0:T(8,128)(2,1)S(1)}, u32[]{:S(2)}, u32[]{:S(2)}) collective-permute-start(bf16[8,32,128]{2,1,0:T(8,128)(2,1)S(1)} %bitcast.120), channel_id=1, source_target_pairs={{0,6},{2,0},{4,2},{6,4},{1,7},{3,1},{5,3},{7,5},{8,14},{10,8},{12,... | collective-permute-start | bytes 196616 | tf_op jit(solution)/shard_map/ppermute | solution.py:42
  13.8 1.6 %copy.68 = bf16[1,128,4096]{1,2,0:T(8,128)(2,1)S(1)} copy(bf16[1,128,4096]{2,1,0:T(8,128)(2,1)} %param.7) | data formatting | bytes 2097152 | tf_op args[0]
  17.0 1.1 pad_maximum_fusion.2
  20.3 1.2 collective-permute-done
  21.5 1.3 slice.12
  22.8 1.6 %pad_maximum_fusion.1 = bf16[256,4096]{0,1:T(8,128)(2,1)} fusion(bf16[128,4096]{0,1:T(8,128)(2,1)S(1)} %slice.12, bf16[128,4096]{0,1:T(8,128)(2,1)S(1)} %fusion.11), kind=kLoop, calls=%fused_computation.11 | loop fusion | flops 4194304 | bytes 4194304 | tf_op jit(solution)/shard_map/concatenate | solution.py:68
  24.4 2.7 %reshape.416 = bf16[256,64,32,2]{0,3,2,1:T(2,128)(2,1)S(1)} reshape(bf16[256,4096]{0,1:T(8,128)(2,1)} %pad_maximum_fusion.1) | data formatting | bytes 4194304 | tf_op jit(solution)/shard_map/reshape | solution.py:79
  27.1 2.6 %reshape.417 = bf16[64,32,512]{2,1,0:T(8,128)(2,1)} reshape(bf16[64,32,2,256]{3,2,1,0:T(2,128)(2,1)S(1)} %bitcast.109) | data formatting | bytes 4194304 | tf_op jit(solution)/shard_map/reshape | solution.py:80
  29.8 1.0 slice.13
  30.9 1.7 %broadcast_in_dim.112 = bf16[16,2,256,128]{2,1,3,0:T(2,128)(2,1)S(1)} broadcast(bf16[16,256,128]{1,2,0:T(8,128)(2,1)S(1)} %pad_maximum_fusion.3), dimensions={0,2,3} | broadcast | bytes 3145728 | tf_op jit(solution)/shard_map/jit(_where)/broadcast_in_dim | solution.py:78
  32.7 2.6 %broadcast_in_dim.113 = bf16[16,512,128]{1,2,0:T(8,128)(2,1)} reshape(bf16[16,2,256,128]{2,1,3,0:T(2,128)(2,1)S(1)} %broadcast_in_dim.112) | data formatting | bytes 4194304 | tf_op jit(solution)/shard_map/jit(_where)/broadcast_in_dim | solution.py:78
  35.3 10.4 %fusion.5 = f32[65,32,16,128]{3,1,2,0:T(8,128)} fusion(bf16[64,32,512]{2,1,0:T(8,128)(2,1)} %reshape.417, bf16[16,512,128]{1,2,0:T(8,128)(2,1)} %broadcast_in_dim.113, pred[512,128]{0,1:T(8,128)(4,1)S(1)} %copy.72), kind=kOutput, calls=%fused_computation.8 | convolution fusion | flops 4363124736 | bytes 21299200 | tf_op jit(solution)/shard_map/dot_general | solution.py:83
  45.7 8.7 %gather_fusion = f32[256,32,128]{2,1,0:T(8,128)} fusion(f32[1040,32,128]{2,1,0:T(8,128)} %bitcast.115, s32[1024]{0:T(1024)S(1)} %pad_clamp_fusion), kind=kCustom, calls=%fused_computation | custom fusion | bytes 8389632 | tf_op jit(solution)/shard_map/gather | solution.py:100
  54.4 6.6 %all-gather.2.cloned.1.call-done = bf16[256,32,128]{2,1,0:T(8,128)(2,1)} async-done(((bf16[32,32,128]{2,1,0:T(8,128)(2,1)}), bf16[256,32,128]{2,1,0:T(8,128)(2,1)}) %all-gather.2.cloned.1.call-update) | async-done | bytes 2097168 | tf_op jit(solution)/shard_map/all_gather | solution.py:44
  63.0 2.2 %convert.4 = f32[128,64,32,2]{0,3,2,1:T(2,128)} convert(bf16[128,64,32,2]{0,3,2,1:T(2,128)(2,1)S(1)} %bitcast.106) | non-fusion elementwise | flops 524288 | bytes 3145728 | tf_op jit(solution)/shard_map/convert_element_type | solution.py:22
  65.5 1.0 copy.80
  67.7 1.0 mul.153
  69.2 4.6 %pad_maximum_fusion = bf16[512,32,128]{2,1,0:T(8,128)(2,1)} fusion(bf16[256,32,128]{2,1,0:T(8,128)(2,1)} %collective-permute-done.4, bf16[256,32,128]{2,1,0:T(8,128)(2,1)} %all-gather.2.cloned.1.call-done), kind=kLoop, calls=%fused_computation.6 | loop fusion | flops 2097152 | bytes 8388608 | tf_op jit(solution)/shard_map/concatenate | solution.py:102
  73.7 12.2 %gather_fusion.1 = bf16[1024,32,128]{2,1,0:T(8,128)(2,1)} fusion(bf16[512,32,128]{2,1,0:T(8,128)(2,1)} %pad_maximum_fusion, s32[1024]{0:T(1024)S(1)} %broadcast_clamp_fusion), kind=kCustom, calls=%fused_computation.1 | custom fusion | bytes 16781312 | tf_op jit(solution)/shard_map/gather | solution.py:113
  86.0 5.8 %fusion.15 = (f32[128]{0:T(128)S(1)}, f32[128,64,32,2]{0,2,3,1:T(8,128)S(1)}) fusion(f32[128,64,32,2]{0,3,2,1:T(2,128)S(1)} %copy-done, f32[64,32,2]{1,2,0:T(2,128)S(1)} %copy.82, pred[2,128]{1,0:T(4,128)(4,1)S(1)} %iota_compare_fusion.2, bf16[16,128,128]{2,1,0:T(8,128)(2,1)} %copy.80, bf16[64,16,32,128]{3,2,1,0:T(8,128)(2,1)} %bitcast.107, ...), kind=kOutput, calls=%fused_computation.23 | convolution fusion | flops 2153775104 | bytes 13125376 | tf_op jit(solution)/shard_map/cthl,pcrl->tprh/dot_general | solution.py:115
  91.8 1.9 %copy.81 = f32[128,64,32,2]{0,3,2,1:T(2,128)S(1)} copy(f32[128,64,32,2]{0,2,3,1:T(8,128)S(1)} %get-tuple-element.21) | data formatting | bytes 4194304 | tf_op jit(solution)/shard_map/cthl,pcrl->tprh/transpose | solution.py:115
  94.5 2.5 %collective-permute-start.5 = (bf16[128,4096]{0,1:T(8,128)(2,1)S(1)}, bf16[128,4096]{0,1:T(8,128)(2,1)S(1)}, u32[]{:S(2)}, u32[]{:S(2)}) collective-permute-start(bf16[128,4096]{0,1:T(8,128)(2,1)S(1)} %fusion.14), channel_id=1, source_target_pairs={{64,0},{128,64},{192,128},{65,1},{129,65},{193,129},{66,2},{130,66... | collective-permute-start | bytes 3145736 | tf_op jit(solution)/shard_map/ppermute | solution.py:13
  97.0 20.5 %reduce-scatter.2.cloned.1.call-done = f32[32,32,128]{2,1,0:T(8,128)} async-done(((f32[256,32,128]{2,1,0:T(8,128)}), f32[32,32,128]{2,1,0:T(8,128)}) %reduce-scatter.2.cloned.1.call-update) | async-done | bytes 524304 | tf_op jit(solution)/shard_map/reduce_scatter | solution.py:103
  117.5 1.1 constant_dynamic-slice_fusion.2
  118.7 3.1 %collective-permute-start.6 = (f32[8,32,128]{2,0,1:T(8,128)S(1)}, f32[8,32,128]{2,0,1:T(8,128)S(1)}, u32[]{:S(2)}, u32[]{:S(2)}) collective-permute-start(f32[8,32,128]{2,0,1:T(8,128)S(1)} %bitcast.124), channel_id=1, source_target_pairs={{0,4},{2,6},{4,0},{6,2},{1,5},{3,7},{5,1},{7,3},{8,12},{10,14},{12... | collective-permute-start | bytes 393224 | tf_op jit(solution)/shard_map/ppermute | solution.py:108
  122.6 2.8 %collective-permute-start.8 = (f32[8,32,128]{2,0,1:T(8,128)S(1)}, f32[8,32,128]{2,0,1:T(8,128)S(1)}, u32[]{:S(2)}, u32[]{:S(2)}) collective-permute-start(f32[8,32,128]{2,0,1:T(8,128)S(1)} %bitcast.126), channel_id=1, source_target_pairs={{0,6},{2,0},{4,2},{6,4},{1,7},{3,1},{5,3},{7,5},{8,14},{10,8},{12,... | collective-permute-start | bytes 393224 | tf_op jit(solution)/shard_map/ppermute | solution.py:108
  125.3 1.3 copy.88
  126.6 1.9 %collective-permute-done.7 = f32[8,32,128]{2,0,1:T(8,128)S(1)} collective-permute-done((f32[8,32,128]{2,0,1:T(8,128)S(1)}, f32[8,32,128]{2,0,1:T(8,128)S(1)}, u32[]{:S(2)}, u32[]{:S(2)}) %collective-permute-start.7) | collective-permute-done | bytes 131104 | tf_op jit(solution)/shard_map/ppermute | solution.py:108
  128.6 0.8 fusion.32
  (73 shorter events, 9.2 us)
Async XLA Ops:
  7.2 8.9 %copy-start.1 = (bf16[1,128,1024]{2,1,0:T(8,128)(2,1)S(1)}, bf16[1,128,1024]{2,1,0:T(8,128)(2,1)}, u32[]{:S(2)}) copy-start(bf16[1,128,1024]{2,1,0:T(8,128)(2,1)} %param.8) | copy-start | bytes 786436
  7.2 9.0 %copy-start.2 = (f32[1,4096]{1,0:T(1,128)S(1)}, f32[1,4096]{1,0:T(1,128)}, u32[]{:S(2)}) copy-start(f32[1,4096]{1,0:T(1,128)} %param.9) | copy-start | bytes 49156
  7.2 53.8 %all-gather.2.cloned.1.call-start = ((), (), s32[]{:S(2)}) async-start(), calls=%async_computation.1 | async-start | bytes 2359296 | tf_op jit(solution)/shard_map/all_gather | solution.py:44
  8.1 10.0 %collective-permute-start.1 = (bf16[8,32,128]{2,1,0:T(8,128)(2,1)S(1)}, bf16[8,32,128]{2,1,0:T(8,128)(2,1)S(1)}, u32[]{:S(2)}, u32[]{:S(2)}) collective-permute-start(bf16[8,32,128]{2,1,0:T(8,128)(2,1)S(1)} %bitcast.118), channel_id=1, source_target_pairs={{0,2},{2,4},{4,6},{6,0},{1,3},{3,5},{5,7},{7,1},{8,10},{10,12},{12... | collective-permute-start | bytes 196616 | tf_op jit(solution)/shard_map/ppermute | solution.py:42
  9.7 8.5 %collective-permute-start.2 = (bf16[8,32,128]{2,1,0:T(8,128)(2,1)S(1)}, bf16[8,32,128]{2,1,0:T(8,128)(2,1)S(1)}, u32[]{:S(2)}, u32[]{:S(2)}) collective-permute-start(bf16[8,32,128]{2,1,0:T(8,128)(2,1)S(1)} %bitcast.119), channel_id=1, source_target_pairs={{0,4},{2,6},{4,0},{6,2},{1,5},{3,7},{5,1},{7,3},{8,12},{10,14},{12... | collective-permute-start | bytes 196616 | tf_op jit(solution)/shard_map/ppermute | solution.py:42
  12.4 5.7 %collective-permute-start.3 = (bf16[8,32,128]{2,1,0:T(8,128)(2,1)S(1)}, bf16[8,32,128]{2,1,0:T(8,128)(2,1)S(1)}, u32[]{:S(2)}, u32[]{:S(2)}) collective-permute-start(bf16[8,32,128]{2,1,0:T(8,128)(2,1)S(1)} %bitcast.120), channel_id=1, source_target_pairs={{0,6},{2,0},{4,2},{6,4},{1,7},{3,1},{5,3},{7,5},{8,14},{10,8},{12,... | collective-permute-start | bytes 196616 | tf_op jit(solution)/shard_map/ppermute | solution.py:42
  16.9 2.5 %copy-start.5 = (s32[1,64]{1,0:T(1,128)S(1)}, s32[1,64]{1,0:T(1,128)}, u32[]{:S(2)}) copy-start(s32[1,64]{1,0:T(1,128)} %param.12) | copy-start | bytes 772
  17.0 2.7 %copy-start.3 = (s32[1,64,8]{1,2,0:T(8,128)S(1)}, s32[1,64,8]{1,2,0:T(8,128)}, u32[]{:S(2)}) copy-start(s32[1,64,8]{1,2,0:T(8,128)} %param.11) | copy-start | bytes 6148
  17.0 2.9 %copy-start.4 = (s32[1,512]{1,0:T(1,128)S(1)}, s32[1,512]{1,0:T(1,128)}, u32[]{:S(2)}) copy-start(s32[1,512]{1,0:T(1,128)} %param.13) | copy-start | bytes 6148
  18.1 3.4 %collective-permute-start = (bf16[128,5120]{0,1:T(8,128)(2,1)}, bf16[128,5120]{0,1:T(8,128)(2,1)}, u32[]{:S(2)}, u32[]{:S(2)}) collective-permute-start(bf16[128,5120]{0,1:T(8,128)(2,1)} %pad_maximum_fusion.2), channel_id=1, source_target_pairs={{0,1},{1,0},{2,3},{3,2},{4,5},{5,4},{6,7},{7,6},{8,9},{9,8},{10,11... | collective-permute-start | bytes 3932168 | tf_op jit(solution)/shard_map/ppermute | solution.py:18
  18.9 98.5 %reduce-scatter.2.cloned.1.call-start = ((), (), s32[]{:S(2)}) async-start(), calls=%async_computation.2 | async-start | bytes 4718592 | tf_op jit(solution)/shard_map/reduce_scatter | solution.py:103
  61.0 8.1 %collective-permute-start.4 = (bf16[256,32,128]{2,1,0:T(8,128)(2,1)}, bf16[256,32,128]{2,1,0:T(8,128)(2,1)}, u32[]{:S(2)}, u32[]{:S(2)}) collective-permute-start(bf16[256,32,128]{2,1,0:T(8,128)(2,1)} %all-gather.2.cloned.1.call-done), channel_id=1, source_target_pairs={{0,1},{1,0},{2,3},{3,2},{4,5},{5,4},{6,7},{7,6},{8,9},{9,8},{10,11... | collective-permute-start | bytes 6291464 | tf_op jit(solution)/shard_map/ppermute | solution.py:18
  73.7 12.2 %copy-start = (f32[128,64,32,2]{0,3,2,1:T(2,128)S(1)}, f32[128,64,32,2]{0,3,2,1:T(2,128)}, u32[]{:S(2)}) copy-start(f32[128,64,32,2]{0,3,2,1:T(2,128)} %convert.4) | copy-start | bytes 6291460
  94.5 30.8 %collective-permute-start.5 = (bf16[128,4096]{0,1:T(8,128)(2,1)S(1)}, bf16[128,4096]{0,1:T(8,128)(2,1)S(1)}, u32[]{:S(2)}, u32[]{:S(2)}) collective-permute-start(bf16[128,4096]{0,1:T(8,128)(2,1)S(1)} %fusion.14), channel_id=1, source_target_pairs={{64,0},{128,64},{192,128},{65,1},{129,65},{193,129},{66,2},{130,66... | collective-permute-start | bytes 3145736 | tf_op jit(solution)/shard_map/ppermute | solution.py:13
  118.7 7.9 %collective-permute-start.6 = (f32[8,32,128]{2,0,1:T(8,128)S(1)}, f32[8,32,128]{2,0,1:T(8,128)S(1)}, u32[]{:S(2)}, u32[]{:S(2)}) collective-permute-start(f32[8,32,128]{2,0,1:T(8,128)S(1)} %bitcast.124), channel_id=1, source_target_pairs={{0,4},{2,6},{4,0},{6,2},{1,5},{3,7},{5,1},{7,3},{8,12},{10,14},{12... | collective-permute-start | bytes 393224 | tf_op jit(solution)/shard_map/ppermute | solution.py:108
  121.8 6.7 %collective-permute-start.7 = (f32[8,32,128]{2,0,1:T(8,128)S(1)}, f32[8,32,128]{2,0,1:T(8,128)S(1)}, u32[]{:S(2)}, u32[]{:S(2)}) collective-permute-start(f32[8,32,128]{2,0,1:T(8,128)S(1)} %bitcast.125), channel_id=1, source_target_pairs={{0,2},{2,4},{4,6},{6,0},{1,3},{3,5},{5,7},{7,1},{8,10},{10,12},{12... | collective-permute-start | bytes 393224 | tf_op jit(solution)/shard_map/ppermute | solution.py:108
  122.6 6.0 %collective-permute-start.8 = (f32[8,32,128]{2,0,1:T(8,128)S(1)}, f32[8,32,128]{2,0,1:T(8,128)S(1)}, u32[]{:S(2)}, u32[]{:S(2)}) collective-permute-start(f32[8,32,128]{2,0,1:T(8,128)S(1)} %bitcast.126), channel_id=1, source_target_pairs={{0,6},{2,0},{4,2},{6,4},{1,7},{3,1},{5,3},{7,5},{8,14},{10,8},{12,... | collective-permute-start | bytes 393224 | tf_op jit(solution)/shard_map/ppermute | solution.py:108
Sparse Core Ops, SparseCore 0:
  19.0 41.9 all-gather.1
  63.5 53.8 reduce-scatter.1

commit v16 on v15

--- a/solution.py
+++ b/solution.py
@@ -90,24 +90,22 @@
     oz = jnp.arange(nz)[:, None, None]
     ox = jnp.arange(nx)[None, :, None]
     oj = jnp.arange(slot_dev)[None, None, :]
-    rs_order = (((oz * nx + ox) * nc + my_core) * slot_dev + oj).reshape(-1)
+    rs_order = (((oz * nx + (ox + my_x) % nx) * nc + my_core) * slot_dev + oj).reshape(-1)
     slot_match = slot_lookup[None, :] == rs_order[:, None]
     pos_panel = jnp.arange(store_slots, dtype=jnp.int32) // most_kept
     pos_index = pos_panel * ncol + column_list.reshape(-1)
     pos_kept = kept_grid.reshape(-1)
     term_index = jnp.sum(jnp.where(slot_match, pos_index[None, :], 0), axis=1)
     term_kept = jnp.any(slot_match & pos_kept[None, :], axis=1)
-    terms = dense_terms[jnp.where(term_kept, term_index, panel_list * ncol)]
+    terms = dense_terms[jnp.where(term_kept, term_index, panel_list * ncol)] * grad_scale
     terms, gathered = lax.optimization_barrier((terms, gathered))
     gathered = jnp.concatenate([gathered, sibling(gathered)], axis=0)
     weight_grad = lax.psum_scatter(terms, "z", scatter_dimension=0, tiled=True)
     x_blocks = weight_grad.reshape(nx, slot_dev, half, lanes)
-    own_sum = lax.dynamic_index_in_dim(x_blocks, my_x, axis=0, keepdims=False)
+    own_sum = x_blocks[0]
     for s in shift_order:
-        outgoing = lax.dynamic_index_in_dim(x_blocks, (my_x + s) % nx, axis=0, keepdims=False)
-        own_sum = own_sum + lax.ppermute(outgoing, "x", [(src, (src + s) % nx) for src in range(nx)])
-    weight_grad = own_sum
-    weight_grad = (weight_grad * grad_scale).reshape(slot_dev, blk * blk)
+        own_sum = own_sum + lax.ppermute(x_blocks[s], "x", [(src, (src + s) % nx) for src in range(nx)])
+    weight_grad = own_sum.reshape(slot_dev, blk * blk)
 
     dense_w = jnp.where(
         has_tile.reshape(-1)[:, None, None], gathered[dense_rows], jnp.zeros((), gathered.dtype)

time: 137 us -> 138 us (level)
  other arithmetic: 15.4 us -> 20.3 us
  waiting for transfers between devices: 30.2 us -> 25.9 us
    all_gather x1, waiting for transfers between devices: 6.56 us -> 1.86 us  [local(): gathered = lax.all_gather(gathered, 'z', axis=0, tiled=True)]
    mul x2 -> x3, other arithmetic: 0.08 us -> 4.75 us  [the longest x1 4.67 us: local(): dense_terms[jnp.where(term_kept, term_index, panel_list * ncol)]]
  transfers between devices with their start and end apart: 11 -> 11, of which waited for: 4 -> 5; matrix products, arithmetic and copies ran while one was open for 55% -> 58% of each run, Pallas kernels for 0% -> 0%
where the time goes in v16:
time: 138 us; the launch traced here: 137 us
  local copies, waits for them, and re-layouts  45.2 us (33%)
  waiting for transfers between devices  25.9 us (19%)
  other arithmetic  20.3 us (15%)
  matrix products  16.2 us (12%)
  starting transfers between devices  14.9 us (11%)
  between operations  14.4 us (10%)
    reduce_scatter x1, waiting for transfers between devices, local(): weight_grad = lax.psum_scatter(terms, 'z', scatter_dimension=0, tiled=True)  20.5 us
    gather x1, local copies, waits for them, and re-layouts, local(): gathered[dense_rows]  12.2 us
    dot_general x1, matrix products, local(): jnp.dot(normed_pairs.reshape((panel_list + 1) * half, 2 * pair_tokens), e...  10.4 us
    gather x1, local copies, waits for them, and re-layouts, local(): dense_terms[jnp.where(term_kept, term_index, panel_list * ncol)]  8.74 us
    ppermute x3, starting transfers between devices, local(): lax.ppermute(x_blocks[s], 'x', [(src, (src + s) % nx) for src in range(nx)])  6.31 us
    dot_general x1, matrix products, local(): jnp.einsum('cthl,pcrl->tprh', expand, dense_w, preferred_element_type=jnp...  5.83 us
    ppermute x3, starting transfers between devices, local(): lax.ppermute(own_tiles, 'x', [(src, (src + s) % nx) for src in range(nx)])  5.73 us
    unnamed x19, local copies, waits for them, and re-layouts  5.12 us
  transfers between devices with their start and end apart: 11, of which 5 were waited for; matrix products, arithmetic and copies ran while one was open for 58% of the time, Pallas kernels for 0%

profile of v16, /device:TPU:8, one launch (start us, length us, event | category | flops | bytes accessed | tf_op | source)
XLA Modules:
  0.0 136.9 jit_solution(15647614937642796410)
XLA Ops:
  8.1 1.6 %collective-permute-start.1 = (bf16[8,32,128]{2,1,0:T(8,128)(2,1)S(1)}, bf16[8,32,128]{2,1,0:T(8,128)(2,1)S(1)}, u32[]{:S(2)}, u32[]{:S(2)}) collective-permute-start(bf16[8,32,128]{2,1,0:T(8,128)(2,1)S(1)} %bitcast.95), channel_id=1, source_target_pairs={{0,2},{2,4},{4,6},{6,0},{1,3},{3,5},{5,7},{7,1},{8,10},{10,12},{12... | collective-permute-start | bytes 196616 | tf_op jit(solution)/shard_map/ppermute | solution.py:42
  9.7 2.7 %collective-permute-start.2 = (bf16[8,32,128]{2,1,0:T(8,128)(2,1)S(1)}, bf16[8,32,128]{2,1,0:T(8,128)(2,1)S(1)}, u32[]{:S(2)}, u32[]{:S(2)}) collective-permute-start(bf16[8,32,128]{2,1,0:T(8,128)(2,1)S(1)} %bitcast.96), channel_id=1, source_target_pairs={{0,4},{2,6},{4,0},{6,2},{1,5},{3,7},{5,1},{7,3},{8,12},{10,14},{12... | collective-permute-start | bytes 196616 | tf_op jit(solution)/shard_map/ppermute | solution.py:42
  12.4 1.4 %collective-permute-start.3 = (bf16[8,32,128]{2,1,0:T(8,128)(2,1)S(1)}, bf16[8,32,128]{2,1,0:T(8,128)(2,1)S(1)}, u32[]{:S(2)}, u32[]{:S(2)}) collective-permute-start(bf16[8,32,128]{2,1,0:T(8,128)(2,1)S(1)} %bitcast.97), channel_id=1, source_target_pairs={{0,6},{2,0},{4,2},{6,4},{1,7},{3,1},{5,3},{7,5},{8,14},{10,8},{12,... | collective-permute-start | bytes 196616 | tf_op jit(solution)/shard_map/ppermute | solution.py:42
  13.8 1.6 %copy.52 = bf16[1,128,4096]{1,2,0:T(8,128)(2,1)S(1)} copy(bf16[1,128,4096]{2,1,0:T(8,128)(2,1)} %param.7) | data formatting | bytes 2097152 | tf_op args[0]
  17.0 1.1 pad_maximum_fusion.2
  20.3 1.2 collective-permute-done
  21.5 1.3 slice.32
  22.8 1.6 %pad_maximum_fusion.1 = bf16[256,4096]{0,1:T(8,128)(2,1)} fusion(bf16[128,4096]{0,1:T(8,128)(2,1)S(1)} %slice.32, bf16[128,4096]{0,1:T(8,128)(2,1)S(1)} %fusion.11), kind=kLoop, calls=%fused_computation.11 | loop fusion | flops 4194304 | bytes 4194304 | tf_op jit(solution)/shard_map/concatenate | solution.py:68
  24.4 2.7 %reshape.452 = bf16[256,64,32,2]{0,3,2,1:T(2,128)(2,1)S(1)} reshape(bf16[256,4096]{0,1:T(8,128)(2,1)} %pad_maximum_fusion.1) | data formatting | bytes 4194304 | tf_op jit(solution)/shard_map/reshape | solution.py:79
  27.1 2.6 %reshape.453 = bf16[64,32,512]{2,1,0:T(8,128)(2,1)} reshape(bf16[64,32,2,256]{3,2,1,0:T(2,128)(2,1)S(1)} %bitcast.87) | data formatting | bytes 4194304 | tf_op jit(solution)/shard_map/reshape | solution.py:80
  29.8 1.0 slice.33
  30.9 1.7 %broadcast_in_dim.112 = bf16[16,2,256,128]{2,1,3,0:T(2,128)(2,1)S(1)} broadcast(bf16[16,256,128]{1,2,0:T(8,128)(2,1)S(1)} %pad_maximum_fusion.3), dimensions={0,2,3} | broadcast | bytes 3145728 | tf_op jit(solution)/shard_map/jit(_where)/broadcast_in_dim | solution.py:78
  32.7 2.6 %broadcast_in_dim.113 = bf16[16,512,128]{1,2,0:T(8,128)(2,1)} reshape(bf16[16,2,256,128]{2,1,3,0:T(2,128)(2,1)S(1)} %broadcast_in_dim.112) | data formatting | bytes 4194304 | tf_op jit(solution)/shard_map/jit(_where)/broadcast_in_dim | solution.py:78
  35.3 10.4 %fusion.5 = f32[65,32,16,128]{3,1,2,0:T(8,128)} fusion(bf16[64,32,512]{2,1,0:T(8,128)(2,1)} %reshape.453, bf16[16,512,128]{1,2,0:T(8,128)(2,1)} %broadcast_in_dim.113, pred[512,128]{0,1:T(8,128)(4,1)S(1)} %copy.56), kind=kOutput, calls=%fused_computation.8 | convolution fusion | flops 4363124736 | bytes 21299200 | tf_op jit(solution)/shard_map/dot_general | solution.py:83
  45.7 8.7 %gather_fusion = f32[256,32,128]{2,1,0:T(8,128)} fusion(f32[1040,32,128]{2,1,0:T(8,128)} %bitcast.93, s32[1024]{0:T(1024)S(1)} %pad_clamp_fusion), kind=kCustom, calls=%fused_computation | custom fusion | bytes 8389632 | tf_op jit(solution)/shard_map/gather | solution.py:100
  54.4 4.7 %broadcast_multiply_fusion = f32[256,32,128]{2,1,0:T(8,128)} fusion(f32[256,32,128]{2,1,0:T(8,128)} %gather_fusion), kind=kLoop, calls=%fused_computation.24 | loop fusion | flops 1048576 | bytes 8388608 | tf_op jit(solution)/shard_map/mul | solution.py:100
  59.1 1.9 %all-gather.2.cloned.1.call-done = bf16[256,32,128]{2,1,0:T(8,128)(2,1)} async-done(((bf16[32,32,128]{2,1,0:T(8,128)(2,1)}), bf16[256,32,128]{2,1,0:T(8,128)(2,1)}) %all-gather.2.cloned.1.call-update) | async-done | bytes 2097168 | tf_op jit(solution)/shard_map/all_gather | solution.py:44
  62.9 2.2 %convert.4 = f32[128,64,32,2]{0,3,2,1:T(2,128)} convert(bf16[128,64,32,2]{0,3,2,1:T(2,128)(2,1)S(1)} %bitcast.84) | non-fusion elementwise | flops 524288 | bytes 3145728 | tf_op jit(solution)/shard_map/convert_element_type | solution.py:22
  65.4 1.0 copy.64
  67.6 1.0 mul.155
  69.1 4.6 %pad_maximum_fusion = bf16[512,32,128]{2,1,0:T(8,128)(2,1)} fusion(bf16[256,32,128]{2,1,0:T(8,128)(2,1)} %collective-permute-done.4, bf16[256,32,128]{2,1,0:T(8,128)(2,1)} %all-gather.2.cloned.1.call-done), kind=kLoop, calls=%fused_computation.6 | loop fusion | flops 2097152 | bytes 8388608 | tf_op jit(solution)/shard_map/concatenate | solution.py:102
  73.7 12.2 %gather_fusion.1 = bf16[1024,32,128]{2,1,0:T(8,128)(2,1)} fusion(bf16[512,32,128]{2,1,0:T(8,128)(2,1)} %pad_maximum_fusion, s32[1024]{0:T(1024)S(1)} %broadcast_clamp_fusion), kind=kCustom, calls=%fused_computation.1 | custom fusion | bytes 16781312 | tf_op jit(solution)/shard_map/gather | solution.py:111
  85.9 5.8 %fusion.15 = (f32[128]{0:T(128)S(1)}, f32[128,64,32,2]{0,2,3,1:T(8,128)S(1)}) fusion(f32[128,64,32,2]{0,3,2,1:T(2,128)S(1)} %copy-done, f32[64,32,2]{1,2,0:T(2,128)S(1)} %copy.66, pred[2,128]{1,0:T(4,128)(4,1)S(1)} %iota_compare_fusion.2, bf16[16,128,128]{2,1,0:T(8,128)(2,1)} %copy.64, bf16[64,16,32,128]{3,2,1,0:T(8,128)(2,1)} %bitcast.85, ...), kind=kOutput, calls=%fused_computation.23 | convolution fusion | flops 2153775104 | bytes 13125376 | tf_op jit(solution)/shard_map/cthl,pcrl->tprh/dot_general | solution.py:113
  91.8 1.9 %copy.65 = f32[128,64,32,2]{0,3,2,1:T(2,128)S(1)} copy(f32[128,64,32,2]{0,2,3,1:T(8,128)S(1)} %get-tuple-element.20) | data formatting | bytes 4194304 | tf_op jit(solution)/shard_map/cthl,pcrl->tprh/transpose | solution.py:113
  94.5 2.5 %collective-permute-start.5 = (bf16[128,4096]{0,1:T(8,128)(2,1)S(1)}, bf16[128,4096]{0,1:T(8,128)(2,1)S(1)}, u32[]{:S(2)}, u32[]{:S(2)}) collective-permute-start(bf16[128,4096]{0,1:T(8,128)(2,1)S(1)} %fusion.14), channel_id=1, source_target_pairs={{64,0},{128,64},{192,128},{65,1},{129,65},{193,129},{66,2},{130,66... | collective-permute-start | bytes 3145736 | tf_op jit(solution)/shard_map/ppermute | solution.py:13
  96.9 20.5 %reduce-scatter.2.cloned.1.call-done = f32[32,32,128]{2,1,0:T(8,128)} async-done(((f32[256,32,128]{2,1,0:T(8,128)}), f32[32,32,128]{2,1,0:T(8,128)}) %reduce-scatter.2.cloned.1.call-update) | async-done | bytes 524304 | tf_op jit(solution)/shard_map/reduce_scatter | solution.py:103
  117.4 1.1 fusion.56
  118.5 3.1 %collective-permute-start.6 = (f32[8,32,128]{2,1,0:T(8,128)S(1)}, f32[8,32,128]{2,1,0:T(8,128)S(1)}, u32[]{:S(2)}, u32[]{:S(2)}) collective-permute-start(f32[8,32,128]{2,1,0:T(8,128)S(1)} %get-tuple-element.14), channel_id=1, source_target_pairs={{0,4},{2,6},{4,0},{6,2},{1,5},{3,7},{5,1},{7,3},{8,12},{10,14},{12... | collective-permute-start | bytes 393224 | tf_op jit(solution)/shard_map/ppermute | solution.py:107
  122.1 2.7 %collective-permute-start.8 = (f32[8,32,128]{2,1,0:T(8,128)S(1)}, f32[8,32,128]{2,1,0:T(8,128)S(1)}, u32[]{:S(2)}, u32[]{:S(2)}) collective-permute-start(f32[8,32,128]{2,1,0:T(8,128)S(1)} %get-tuple-element.15), channel_id=1, source_target_pairs={{0,6},{2,0},{4,2},{6,4},{1,7},{3,1},{5,3},{7,5},{8,14},{10,8},{12,... | collective-permute-start | bytes 393224 | tf_op jit(solution)/shard_map/ppermute | solution.py:107
  124.8 1.3 copy.68
  126.3 2.1 %collective-permute-done.7 = f32[8,32,128]{2,1,0:T(8,128)S(1)} collective-permute-done((f32[8,32,128]{2,1,0:T(8,128)S(1)}, f32[8,32,128]{2,1,0:T(8,128)S(1)}, u32[]{:S(2)}, u32[]{:S(2)}) %collective-permute-start.7) | collective-permute-done | bytes 131104 | tf_op jit(solution)/shard_map/ppermute | solution.py:107
  128.4 0.9 fusion.30
  (73 shorter events, 10.7 us)
Async XLA Ops:
  7.2 8.9 %copy-start.1 = (bf16[1,128,1024]{2,1,0:T(8,128)(2,1)S(1)}, bf16[1,128,1024]{2,1,0:T(8,128)(2,1)}, u32[]{:S(2)}) copy-start(bf16[1,128,1024]{2,1,0:T(8,128)(2,1)} %param.8) | copy-start | bytes 786436
  7.2 9.0 %copy-start.2 = (f32[1,4096]{1,0:T(1,128)S(1)}, f32[1,4096]{1,0:T(1,128)}, u32[]{:S(2)}) copy-start(f32[1,4096]{1,0:T(1,128)} %param.9) | copy-start | bytes 49156
  7.2 53.8 %all-gather.2.cloned.1.call-start = ((), (), s32[]{:S(2)}) async-start(), calls=%async_computation.1 | async-start | bytes 2359296 | tf_op jit(solution)/shard_map/all_gather | solution.py:44
  8.1 10.1 %collective-permute-start.1 = (bf16[8,32,128]{2,1,0:T(8,128)(2,1)S(1)}, bf16[8,32,128]{2,1,0:T(8,128)(2,1)S(1)}, u32[]{:S(2)}, u32[]{:S(2)}) collective-permute-start(bf16[8,32,128]{2,1,0:T(8,128)(2,1)S(1)} %bitcast.95), channel_id=1, source_target_pairs={{0,2},{2,4},{4,6},{6,0},{1,3},{3,5},{5,7},{7,1},{8,10},{10,12},{12... | collective-permute-start | bytes 196616 | tf_op jit(solution)/shard_map/ppermute | solution.py:42
  9.7 8.5 %collective-permute-start.2 = (bf16[8,32,128]{2,1,0:T(8,128)(2,1)S(1)}, bf16[8,32,128]{2,1,0:T(8,128)(2,1)S(1)}, u32[]{:S(2)}, u32[]{:S(2)}) collective-permute-start(bf16[8,32,128]{2,1,0:T(8,128)(2,1)S(1)} %bitcast.96), channel_id=1, source_target_pairs={{0,4},{2,6},{4,0},{6,2},{1,5},{3,7},{5,1},{7,3},{8,12},{10,14},{12... | collective-permute-start | bytes 196616 | tf_op jit(solution)/shard_map/ppermute | solution.py:42
  12.4 5.8 %collective-permute-start.3 = (bf16[8,32,128]{2,1,0:T(8,128)(2,1)S(1)}, bf16[8,32,128]{2,1,0:T(8,128)(2,1)S(1)}, u32[]{:S(2)}, u32[]{:S(2)}) collective-permute-start(bf16[8,32,128]{2,1,0:T(8,128)(2,1)S(1)} %bitcast.97), channel_id=1, source_target_pairs={{0,6},{2,0},{4,2},{6,4},{1,7},{3,1},{5,3},{7,5},{8,14},{10,8},{12,... | collective-permute-start | bytes 196616 | tf_op jit(solution)/shard_map/ppermute | solution.py:42
  16.9 2.5 %copy-start.5 = (s32[1,64]{1,0:T(1,128)S(1)}, s32[1,64]{1,0:T(1,128)}, u32[]{:S(2)}) copy-start(s32[1,64]{1,0:T(1,128)} %param.12) | copy-start | bytes 772
  17.0 2.7 %copy-start.3 = (s32[1,64,8]{1,2,0:T(8,128)S(1)}, s32[1,64,8]{1,2,0:T(8,128)}, u32[]{:S(2)}) copy-start(s32[1,64,8]{1,2,0:T(8,128)} %param.11) | copy-start | bytes 6148
  17.0 2.8 %copy-start.4 = (s32[1,512]{1,0:T(1,128)S(1)}, s32[1,512]{1,0:T(1,128)}, u32[]{:S(2)}) copy-start(s32[1,512]{1,0:T(1,128)} %param.13) | copy-start | bytes 6148
  18.1 3.4 %collective-permute-start = (bf16[128,5120]{0,1:T(8,128)(2,1)}, bf16[128,5120]{0,1:T(8,128)(2,1)}, u32[]{:S(2)}, u32[]{:S(2)}) collective-permute-start(bf16[128,5120]{0,1:T(8,128)(2,1)} %pad_maximum_fusion.2), channel_id=1, source_target_pairs={{0,1},{1,0},{2,3},{3,2},{4,5},{5,4},{6,7},{7,6},{8,9},{9,8},{10,11... | collective-permute-start | bytes 3932168 | tf_op jit(solution)/shard_map/ppermute | solution.py:18
  19.0 98.4 %reduce-scatter.2.cloned.1.call-start = ((), (), s32[]{:S(2)}) async-start(), calls=%async_computation.2 | async-start | bytes 4718592 | tf_op jit(solution)/shard_map/reduce_scatter | solution.py:103
  61.0 8.1 %collective-permute-start.4 = (bf16[256,32,128]{2,1,0:T(8,128)(2,1)}, bf16[256,32,128]{2,1,0:T(8,128)(2,1)}, u32[]{:S(2)}, u32[]{:S(2)}) collective-permute-start(bf16[256,32,128]{2,1,0:T(8,128)(2,1)} %all-gather.2.cloned.1.call-done), channel_id=1, source_target_pairs={{0,1},{1,0},{2,3},{3,2},{4,5},{5,4},{6,7},{7,6},{8,9},{9,8},{10,11... | collective-permute-start | bytes 6291464 | tf_op jit(solution)/shard_map/ppermute | solution.py:18
  73.7 12.2 %copy-start = (f32[128,64,32,2]{0,3,2,1:T(2,128)S(1)}, f32[128,64,32,2]{0,3,2,1:T(2,128)}, u32[]{:S(2)}) copy-start(f32[128,64,32,2]{0,3,2,1:T(2,128)} %convert.4) | copy-start | bytes 6291460
  94.5 30.4 %collective-permute-start.5 = (bf16[128,4096]{0,1:T(8,128)(2,1)S(1)}, bf16[128,4096]{0,1:T(8,128)(2,1)S(1)}, u32[]{:S(2)}, u32[]{:S(2)}) collective-permute-start(bf16[128,4096]{0,1:T(8,128)(2,1)S(1)} %fusion.14), channel_id=1, source_target_pairs={{64,0},{128,64},{192,128},{65,1},{129,65},{193,129},{66,2},{130,66... | collective-permute-start | bytes 3145736 | tf_op jit(solution)/shard_map/ppermute | solution.py:13
  118.5 7.8 %collective-permute-start.6 = (f32[8,32,128]{2,1,0:T(8,128)S(1)}, f32[8,32,128]{2,1,0:T(8,128)S(1)}, u32[]{:S(2)}, u32[]{:S(2)}) collective-permute-start(f32[8,32,128]{2,1,0:T(8,128)S(1)} %get-tuple-element.14), channel_id=1, source_target_pairs={{0,4},{2,6},{4,0},{6,2},{1,5},{3,7},{5,1},{7,3},{8,12},{10,14},{12... | collective-permute-start | bytes 393224 | tf_op jit(solution)/shard_map/ppermute | solution.py:107
  121.6 6.8 %collective-permute-start.7 = (f32[8,32,128]{2,1,0:T(8,128)S(1)}, f32[8,32,128]{2,1,0:T(8,128)S(1)}, u32[]{:S(2)}, u32[]{:S(2)}) collective-permute-start(f32[8,32,128]{2,1,0:T(8,128)S(1)} %get-tuple-element.16), channel_id=1, source_target_pairs={{0,2},{2,4},{4,6},{6,0},{1,3},{3,5},{5,7},{7,1},{8,10},{10,12},{12... | collective-permute-start | bytes 393224 | tf_op jit(solution)/shard_map/ppermute | solution.py:107
  122.1 6.3 %collective-permute-start.8 = (f32[8,32,128]{2,1,0:T(8,128)S(1)}, f32[8,32,128]{2,1,0:T(8,128)S(1)}, u32[]{:S(2)}, u32[]{:S(2)}) collective-permute-start(f32[8,32,128]{2,1,0:T(8,128)S(1)} %get-tuple-element.15), channel_id=1, source_target_pairs={{0,6},{2,0},{4,2},{6,4},{1,7},{3,1},{5,3},{7,5},{8,14},{10,8},{12,... | collective-permute-start | bytes 393224 | tf_op jit(solution)/shard_map/ppermute | solution.py:107
Sparse Core Ops, SparseCore 0:
  19.1 41.8 all-gather.1
  63.5 53.8 reduce-scatter.1
